TPU v7x, 256 devices: a whole 4x4x8 slice. The times are simulated.
256 devices in a mesh: win: 2 (over x_lo), seq: 128 (over x_hi, z, y, core).
Axes of the slice: x: 4 (x_hi: 2, x_lo: 2; x = x_hi * 2 + x_lo), y: 4, z: 8, core: 2. Of those that a mesh axis runs over, the one named last changes fastest.
Arguments:
- layer_input: bfloat16 [65536, 256], P(('win', 'seq')), parts along dimension 0, may hold values from -6 to 6
- w_in: bfloat16 [256, 768], replicated, may hold values from -0.375 to 0.375
- short_w: float32 [3, 768], replicated, may hold values from -3.5 to 3.5
- filters: float32 [2, 256, 32768], P(None, 'seq'), may hold values from -0.046875 to 0.046875
- filter_bias: float32 [2, 256], P(None, 'seq'), may hold values from -1 to 1
- w_out: bfloat16 [256, 256], replicated, may hold values from -0.375 to 0.375
Outputs:
- mixed: bfloat16 [65536, 256], P(('win', 'seq')), parts along dimension 0
There are 2 independent parts, one for each index of `win`. A program takes and returns all parts, laid end to end along the dimension named above; an argument that names none is the same for every part. Nothing has to cross between parts.
All inputs are finite; a program needn't handle non-finite values.
Results may differ from a plain program's by a relative error of at most 0.018.
Values may be sent and summed in bfloat16 or wider, within the bound.
No kernel may reach another device: no remote copies, remote signals or barrier semaphores. Data moves between devices by JAX's collectives and lax.ppermute only.
A program may use at most 64 MiB of HBM per device.

v0:
```python
import math

import jax
import jax.numpy as jnp
from jax import lax
from jax.sharding import PartitionSpec as P

PRECISE = lax.Precision.HIGHEST


def shifted(block, axis, distance):
    devices = range(lax.axis_size(axis))
    route = [(i - distance, i) for i in devices if i - distance in devices]
    return lax.ppermute(block, axis, route)


def table_pair(table):
    upper = table.astype(jnp.bfloat16)
    lower = (table - upper.astype(jnp.float32)).astype(jnp.bfloat16)
    return (upper, lower)


def split_product(form, table, data):
    upper, lower = table_pair(table)
    return jnp.einsum(form, upper, data, preferred_element_type=jnp.float32) + jnp.einsum(
        form, lower, data, preferred_element_type=jnp.float32
    )


def dft_tables(length):
    places = jnp.arange(length, dtype=jnp.int32)
    angles = (
        -2.0 * math.pi / length * (places[:, None] * places[None, :] % length).astype(jnp.float32)
    )
    return (jnp.cos(angles), jnp.sin(angles))


def direct_dft(real_part, imag_part):
    length = real_part.shape[-1]
    cosine, sine_tab = dft_tables(length)
    out_real = jnp.einsum("...n,kn->...k", real_part, cosine, precision=PRECISE) - jnp.einsum(
        "...n,kn->...k", imag_part, sine_tab, precision=PRECISE
    )
    out_imag = jnp.einsum("...n,kn->...k", real_part, sine_tab, precision=PRECISE) + jnp.einsum(
        "...n,kn->...k", imag_part, cosine, precision=PRECISE
    )
    return (out_real, out_imag)


def transform(real_part, imag_part):
    length = real_part.shape[-1]
    if length <= 256:
        return direct_dft(real_part, imag_part)
    factor = math.gcd(length, min(128, length // 128))
    remain = length // factor
    leading = real_part.shape[:-1]
    real_grid = real_part.reshape(leading + (factor, remain))
    cosine, sine_tab = dft_tables(factor)
    if imag_part is None:
        section_real = split_product("kn,...ns->...ks", cosine, real_grid)
        section_imag = split_product("kn,...ns->...ks", sine_tab, real_grid)
    else:
        imag_grid = imag_part.reshape(leading + (factor, remain))
        section_real = jnp.einsum(
            "kn,...ns->...ks", cosine, real_grid, precision=PRECISE
        ) - jnp.einsum("kn,...ns->...ks", sine_tab, imag_grid, precision=PRECISE)
        section_imag = jnp.einsum(
            "kn,...ns->...ks", sine_tab, real_grid, precision=PRECISE
        ) + jnp.einsum("kn,...ns->...ks", cosine, imag_grid, precision=PRECISE)
    places = jnp.arange(factor, dtype=jnp.int32)
    columns = jnp.arange(remain, dtype=jnp.int32)
    twist_angle = (
        -2.0 * math.pi / length * (places[:, None] * columns[None, :] % length).astype(jnp.float32)
    )
    twist_cos = jnp.cos(twist_angle)
    twist_sin = jnp.sin(twist_angle)
    turned_real = section_real * twist_cos - section_imag * twist_sin
    turned_imag = section_real * twist_sin + section_imag * twist_cos
    inner_real, inner_imag = transform(turned_real, turned_imag)
    out_real = jnp.swapaxes(inner_real, -1, -2).reshape(leading + (length,))
    out_imag = jnp.swapaxes(inner_imag, -1, -2).reshape(leading + (length,))
    return (out_real, out_imag)


def long_convolve(signal_in, filter_rows, bias_row):
    channels, length = signal_in.shape
    signal_low = jnp.concatenate([signal_in, jnp.zeros((channels, length), jnp.bfloat16)], 1)
    padding = jnp.zeros((channels, length), jnp.float32)
    blank = jnp.zeros((channels, 2 * length), jnp.float32)
    signal_real, signal_imag = transform(signal_low, None)
    kernel_real, kernel_imag = transform(jnp.concatenate([filter_rows, padding], 1), blank)
    prod_real = signal_real * kernel_real - signal_imag * kernel_imag
    prod_imag = signal_real * kernel_imag + signal_imag * kernel_real
    back_real, back_imag = transform(prod_real, -prod_imag)
    convolved = back_real[:, :length] * (1.0 / (2 * length))
    return (convolved + bias_row[:, None] * signal_in.astype(jnp.float32)).astype(jnp.bfloat16)


def gated(gate_rows, conv_rows):
    return (gate_rows.astype(jnp.float32) * conv_rows.astype(jnp.float32)).astype(jnp.bfloat16)


def local(layer_input, w_in, short_w, filters, filter_bias, w_out):
    width = w_out.shape[0]
    groups = lax.axis_size("seq")
    per = width // groups
    projected = lax.dot_general(
        w_in, layer_input, (((0,), (1,)), ((), ())), preferred_element_type=jnp.float32
    ).astype(jnp.bfloat16)
    positions = projected.shape[1]
    grouped = jnp.swapaxes(projected.reshape(3, groups, per, positions), 0, 1)
    spread = lax.all_to_all(
        grouped.reshape(groups, 3 * per, positions), "seq", split_axis=0, concat_axis=2, tiled=True
    ).reshape(3 * per, groups * positions)
    me = lax.axis_index("seq")
    taps = lax.dynamic_slice_in_dim(short_w.reshape(3, 3, groups, per), me, 1, axis=2)
    taps = taps.reshape(3, 3 * per)
    extended = jnp.pad(spread.astype(jnp.float32), ((0, 0), (2, 0)))
    length = spread.shape[1]
    short = (
        taps[0][:, None] * extended[:, 2:]
        + taps[1][:, None] * extended[:, 1 : length + 1]
        + taps[2][:, None] * extended[:, :length]
    ).astype(jnp.bfloat16)
    gate_list = (short[:per], short[per : 2 * per])
    state = short[2 * per :]
    for order in range(2):
        convolved = long_convolve(state, filters[order], filter_bias[order])
        state = gated(gate_list[order], convolved)
    returned = lax.all_to_all(state, "seq", split_axis=1, concat_axis=0, tiled=True)
    output = lax.dot_general(
        returned, w_out, (((0,), (0,)), ((), ())), preferred_element_type=jnp.float32
    )
    return output.astype(jnp.bfloat16)


def solution(mesh):
    return jax.shard_map(
        local,
        mesh=mesh,
        in_specs=(P(("win", "seq"), None), P(), P(), P(None, "seq", None), P(None, "seq"), P()),
        out_specs=P(("win", "seq"), None),
        check_vma=False,
    )
```

profile of v0, /device:TPU:1, one launch (start us, length us, event | category | flops | bytes accessed | tf_op | source)
XLA Modules:
  0.0 158.0 jit_solution(484680796387547686)
XLA Ops:
  0.0 1.0 copy-done
  1.0 1.2 convolution_convert_fusion
  2.4 1.0 copy.124
  3.4 17.0 %all-to-all-start = ((bf16[128,6,256]{2,1,0:T(8,128)(2,1)}), bf16[128,6,256]{2,1,0:T(8,128)(2,1)}, u32[]{:S(2)}, u32[]{:S(2)}) async-start(bf16[128,6,256]{2,1,0:T(8,128)(2,1)} %copy.124), calls=%async_computation | async-start | bytes 1048576 | tf_op jit(solution)/shard_map/all_to_all | solution.py:112
  20.5 1.0 fusion.98
  25.9 1.2 fusion.20
  27.1 1.2 fusion.25
  28.3 1.2 fusion.24
  29.4 12.5 %all-to-all-done = bf16[128,6,256]{2,1,0:T(8,128)(2,1)} async-done(((bf16[128,6,256]{2,1,0:T(8,128)(2,1)}), bf16[128,6,256]{2,1,0:T(8,128)(2,1)}, u32[]{:S(2)}, u32[]{:S(2)}) %all-to-all-start) | async-done | bytes 393248 | tf_op jit(solution)/shard_map/all_to_all | solution.py:112
  42.0 1.1 bitcast_convert_fusion
  46.1 2.9 %multiply_add_fusion.3 = (f32[2,128,512]{1,2,0:T(8,128)}, f32[2,128,512]{1,2,0:T(8,128)}, f32[2,128,512]{1,2,0:T(8,128)}, f32[2,128,512]{1,2,0:T(8,128)}, f32[2,128,512]{1,2,0:T(8,128)}, /*index=5*/f32[2,128,512]{1,2,0:T(8,128)}) fusion(f32[2,128,512]{1,2,0:T(8,128)S(1)} %fusion.20, f32[128,512]{0,1:T(8,128)S(1)} %get-tuple-element.48, ...), kind=kOutput, calls=%fused_computation.86 | convolution fusion | flops 204046336 | bytes 7340032 | tf_op jit(solution)/shard_map/kn,...ns->...ks/dot_general | solution.py:67
  49.0 1.3 copy.137
  50.3 2.1 %fusion.217 = f32[2,128,128,4]{2,3,1,0:T(4,128)} fusion(f32[2,128,4,128]{3,2,1,0:T(4,128)S(1)} %copy.137), kind=kOutput, calls=%fused_computation.263 | convolution fusion | flops 6291680 | bytes 1048576 | tf_op jit(solution)/shard_map/kn,...ns->...ks/dot_general | solution.py:64
  52.3 1.8 %fusion.234 = f32[2,128,128,4]{2,3,1,0:T(4,128)} fusion(f32[2,128,4,128]{3,2,1,0:T(4,128)S(1)} %copy.137), kind=kOutput, calls=%fused_computation.280 | convolution fusion | flops 6291680 | bytes 1048576 | tf_op jit(solution)/shard_map/kn,...ns->...ks/dot_general | solution.py:67
  54.4 1.0 fusion.220
  55.5 1.0 fusion.237
  56.8 1.0 fusion.208
  57.8 1.8 %fusion.225 = f32[2,128,128,4]{2,3,1,0:T(4,128)} fusion(f32[2,128,4,128]{3,2,1,0:T(4,128)S(1)} %copy.172), kind=kOutput, calls=%fused_computation.271 | convolution fusion | flops 6291680 | bytes 1048576 | tf_op jit(solution)/shard_map/kn,...ns->...ks/dot_general | solution.py:67
  59.9 2.9 %fusion.9 = f32[2,128,4,128]{3,2,1,0:T(4,128)} fusion(f32[2,128,128,4]{2,3,1,0:T(4,128)} %fusion.217, f32[2,128,4,128]{3,2,1,0:T(4,128)S(1)} %copy.138), kind=kOutput, calls=%fused_computation.20 | convolution fusion | flops 6422752 | bytes 1572864 | tf_op jit(solution)/shard_map/kn,...ns->...ks/dot_general | solution.py:66
  62.9 1.8 %fusion.8 = f32[2,128,4,128]{3,2,1,0:T(4,128)} fusion(f32[2,128,128,4]{2,3,1,0:T(4,128)S(1)} %copy-done.8, f32[2,128,4,128]{3,2,1,0:T(4,128)S(1)} %copy.138), kind=kOutput, calls=%fused_computation.18 | convolution fusion | flops 6422752 | bytes 1572864 | tf_op jit(solution)/shard_map/kn,...ns->...ks/dot_general | solution.py:69
  65.0 1.1 fusion.11
  66.0 1.9 %fusion.10 = f32[2,128,4,128]{3,2,1,0:T(4,128)} fusion(f32[2,128,128,4]{2,3,1,0:T(4,128)S(1)} %fusion.237, f32[2,128,4,128]{3,2,1,0:T(4,128)S(1)} %copy.130), kind=kOutput, calls=%fused_computation.22 | convolution fusion | flops 6422752 | bytes 1572864 | tf_op jit(solution)/shard_map/kn,...ns->...ks/dot_general | solution.py:69
  68.2 1.5 fusion.3
  69.7 1.9 %multiply_add_fusion.2 = (f32[2,128,4,128]{3,2,1,0:T(4,128)S(1)}, f32[2,128,4,128]{3,2,1,0:T(4,128)S(1)}, f32[2,128,4,128]{3,2,1,0:T(4,128)S(1)}, f32[2,128,4,12...) fusion(f32[2,128,4,128]{3,2,1,0:T(4,128)S(1)} %fusion.3, ...), kind=kOutput, calls=%fused_computation.84 | convolution fusion | flops 8782048 | bytes 6819840 | tf_op jit(solution)/shard_map/kn,...ns->...ks/dot_general | solution.py:69
  76.9 0.9 convolution_add_fusion.15
  77.8 0.9 convolution_subtract_fusion.13
  78.7 0.9 convolution_add_fusion.16
  79.6 1.0 negate_bitcast_fusion.1
  80.7 1.1 copy.147
  81.8 1.1 sub.185
  82.9 2.1 %fusion.137 = f32[2,512,128]{2,1,0:T(8,128)} fusion(f32[2,128,512]{2,1,0:T(8,128)S(1)} %sub.185), kind=kOutput, calls=%fused_computation.217 | convolution fusion | flops 201555968 | bytes 1048576 | tf_op jit(solution)/shard_map/kn,...ns->...ks/dot_general | solution.py:64
  85.0 1.9 %fusion.127 = f32[2,512,128]{2,1,0:T(8,128)} fusion(f32[2,128,512]{2,1,0:T(8,128)S(1)} %sub.185), kind=kOutput, calls=%fused_computation.207 | convolution fusion | flops 201555968 | bytes 1048576 | tf_op jit(solution)/shard_map/kn,...ns->...ks/dot_general | solution.py:67
  86.9 1.1 copy.149
  88.1 1.2 neg.22
  89.3 1.1 fusion.23
  90.4 2.1 %multiply_add_fusion.7 = (f32[2,128,512]{1,2,0:T(8,128)}, f32[2,128,512]{1,2,0:T(8,128)}) fusion(f32[2,128,512]{1,2,0:T(8,128)S(1)} %fusion.23, f32[128,512]{0,1:T(8,128)S(1)} %get-tuple-element.48, f32[128,512]{0,1:T(8,128)S(1)} %get-tuple-element.49, f32[2,512,128]{2,1,0:T(8,128)S(1)} %copy-done.12, f32[2,128,512]{2,1,0:T(8,128)S(1)} %neg.22), kind=kOutput, calls=%fused_computation.94 | convolution fusion | flops 202473472 | bytes 3145728 | tf_op jit(solution)/shard_map/kn,...ns->...ks/dot_general | solution.py:69
  92.6 1.3 copy.153
  93.8 1.8 %fusion.214 = f32[2,128,128,4]{2,3,1,0:T(4,128)} fusion(f32[2,128,4,128]{3,2,1,0:T(4,128)S(1)} %copy.153), kind=kOutput, calls=%fused_computation.260 | convolution fusion | flops 6291680 | bytes 1048576 | tf_op jit(solution)/shard_map/kn,...ns->...ks/dot_general | solution.py:64
  95.7 1.0 fusion.231
  96.7 1.3 copy.154
  98.0 2.1 %fusion.7 = f32[2,128,4,128]{3,2,1,0:T(4,128)S(1)} fusion(f32[2,128,128,4]{2,3,1,0:T(4,128)} %fusion.214, f32[2,128,4,128]{3,2,1,0:T(4,128)S(1)} %copy.154), kind=kOutput, calls=%fused_computation.16 | convolution fusion | flops 6422752 | bytes 1572864 | tf_op jit(solution)/shard_map/kn,...ns->...ks/dot_general | solution.py:66
  100.1 1.2 multiply_add_fusion.6
  102.3 0.9 fusion.21
  106.7 1.5 multiply_add_fusion.5
  108.2 1.3 copy.164
  109.5 1.8 %fusion.211 = f32[2,128,128,4]{2,3,1,0:T(4,128)} fusion(f32[2,128,4,128]{3,2,1,0:T(4,128)S(1)} %copy.164), kind=kOutput, calls=%fused_computation.257 | convolution fusion | flops 6291680 | bytes 1048576 | tf_op jit(solution)/shard_map/kn,...ns->...ks/dot_general | solution.py:64
  111.3 1.8 %fusion.228 = f32[2,128,128,4]{2,3,1,0:T(4,128)} fusion(f32[2,128,4,128]{3,2,1,0:T(4,128)S(1)} %copy.164), kind=kOutput, calls=%fused_computation.274 | convolution fusion | flops 6291680 | bytes 1048576 | tf_op jit(solution)/shard_map/kn,...ns->...ks/dot_general | solution.py:67
  113.2 1.3 copy.165
  114.4 2.1 %fusion.5 = f32[2,128,4,128]{3,2,1,0:T(4,128)S(1)} fusion(f32[2,128,128,4]{2,3,1,0:T(4,128)} %fusion.211, f32[2,128,4,128]{3,2,1,0:T(4,128)S(1)} %copy.165), kind=kOutput, calls=%fused_computation.12 | convolution fusion | flops 6422752 | bytes 1572864 | tf_op jit(solution)/shard_map/kn,...ns->...ks/dot_general | solution.py:66
  116.6 1.2 multiply_add_fusion.4
  119.6 0.9 convolution_add_fusion.11
  120.5 0.9 convolution_subtract_fusion.8
  121.4 0.9 convolution_add_fusion.12
  122.3 1.0 negate_bitcast_fusion
  124.2 1.1 fusion.133
  125.4 1.1 fusion.123
  126.9 1.1 fusion.18
  128.0 1.9 %multiply_add_fusion.1 = (f32[2,128,512]{1,2,0:T(8,128)}, f32[2,128,512]{1,2,0:T(8,128)S(1)}) fusion(f32[2,128,512]{1,2,0:T(8,128)S(1)} %fusion.18, f32[128,512]{0,1:T(8,128)S(1)} %get-tuple-element.48, f32[128,512]{0,1:T(8,128)S(1)} %get-tuple-element.49, f32[2,512,128]{2,1,0:T(8,128)S(1)} %fusion.123, f32[2,128,512]{2,1,0:T(8,128)S(1)} %neg.25), kind=kOutput, calls=%fused_computation.82 | convolution fusion | flops 202473472 | bytes 3145728 | tf_op jit(solution)/shard_map/kn,...ns->...ks/dot_general | solution.py:69
  130.2 1.0 fusion.205
  131.2 1.0 fusion.222
  132.5 1.1 fusion.1
  133.6 1.2 multiply_add_fusion
  135.7 0.9 fusion.16
  138.0 18.9 %all_to_all.28 = bf16[2,128,256]{2,0,1:T(2,128)(2,1)S(1)} all-to-all(bf16[2,128,256]{2,0,1:T(2,128)(2,1)S(1)} %bitcast.392), channel_id=1, replica_groups=mesh['win'=2,'seq'=128] {'seq'}, dimensions={1} | all-to-all | bytes 262144 | tf_op jit(solution)/shard_map/all_to_all | solution.py:130
  (105 shorter events, 24.8 us)
Async XLA Ops:
  0.0 1.0 copy-start
  3.4 38.5 %all-to-all-start = ((bf16[128,6,256]{2,1,0:T(8,128)(2,1)}), bf16[128,6,256]{2,1,0:T(8,128)(2,1)}, u32[]{:S(2)}, u32[]{:S(2)}) async-start(bf16[128,6,256]{2,1,0:T(8,128)(2,1)} %copy.124), calls=%async_computation | async-start | bytes 1048576 | tf_op jit(solution)/shard_map/all_to_all | solution.py:112
  20.5 2.8 %copy-start.21 = (f32[3,768]{1,0:T(4,128)S(1)}, f32[3,768]{1,0:T(4,128)}, u32[]{:S(2)}) copy-start(f32[3,768]{1,0:T(4,128)} %param.8) | copy-start | bytes 27652
  20.5 4.1 %copy-start.19 = (f32[2,2,32768]{2,1,0:T(2,128)S(1)}, f32[2,2,32768]{2,1,0:T(2,128)}, u32[]{:S(2)}) copy-start(f32[2,2,32768]{2,1,0:T(2,128)} %param.9) | copy-start | bytes 1572868
  24.6 0.7 copy-start.25
  42.0 1.1 copy-start.22
  43.7 1.3 copy-start.6
  50.2 3.9 %copy-start.5 = (f32[2,128,512]{1,2,0:T(8,128)S(1)}, f32[2,128,512]{1,2,0:T(8,128)}, u32[]{:S(2)}) copy-start(f32[2,128,512]{1,2,0:T(8,128)} %get-tuple-element.36) | copy-start | bytes 1572868
  54.4 2.1 %copy-start.4 = (f32[2,128,512]{1,2,0:T(8,128)S(1)}, f32[2,128,512]{1,2,0:T(8,128)}, u32[]{:S(2)}) copy-start(f32[2,128,512]{1,2,0:T(8,128)} %get-tuple-element.15) | copy-start | bytes 1572868
  56.8 2.9 %copy-start.3 = (f32[2,128,512]{1,2,0:T(8,128)S(1)}, f32[2,128,512]{1,2,0:T(8,128)}, u32[]{:S(2)}) copy-start(f32[2,128,512]{1,2,0:T(8,128)} %get-tuple-element.39) | copy-start | bytes 1572868
  59.9 3.0 %copy-start.8 = (f32[2,128,128,4]{2,3,1,0:T(4,128)S(1)}, f32[2,128,128,4]{2,3,1,0:T(4,128)}, u32[]{:S(2)}) copy-start(f32[2,128,128,4]{2,3,1,0:T(4,128)} %fusion.234) | copy-start | bytes 1572868
  62.9 1.8 %copy-start.2 = (f32[2,128,512]{1,2,0:T(8,128)S(1)}, f32[2,128,512]{1,2,0:T(8,128)}, u32[]{:S(2)}) copy-start(f32[2,128,512]{1,2,0:T(8,128)} %get-tuple-element.37) | copy-start | bytes 1572868
  66.0 1.9 %copy-start.1 = (f32[2,128,512]{1,2,0:T(8,128)S(1)}, f32[2,128,512]{1,2,0:T(8,128)}, u32[]{:S(2)}) copy-start(f32[2,128,512]{1,2,0:T(8,128)} %get-tuple-element.14) | copy-start | bytes 1572868
  67.9 1.8 %copy-start.16 = (f32[2,128,128,4]{2,3,1,0:T(4,128)S(1)}, f32[2,128,128,4]{2,3,1,0:T(4,128)}, u32[]{:S(2)}) copy-start(f32[2,128,128,4]{2,3,1,0:T(4,128)} %fusion.225) | copy-start | bytes 1572868
  68.1 1.5 copy-start.13
  68.1 1.5 copy-start.14
  68.2 1.5 copy-start.15
  88.1 1.2 copy-start.10
  89.3 1.1 copy-start.12
  103.2 1.0 copy-start.7
  103.2 1.0 copy-start.24
  104.5 0.7 copy-start.17
  114.4 2.2 %copy-start.9 = (f32[2,128,128,4]{2,3,1,0:T(4,128)S(1)}, f32[2,128,128,4]{2,3,1,0:T(4,128)}, u32[]{:S(2)}) copy-start(f32[2,128,128,4]{2,3,1,0:T(4,128)} %fusion.228) | copy-start | bytes 1572868
  130.2 2.1 %copy-start.11 = (f32[2,128,512]{1,2,0:T(8,128)S(1)}, f32[2,128,512]{1,2,0:T(8,128)}, u32[]{:S(2)}) copy-start(f32[2,128,512]{1,2,0:T(8,128)} %get-tuple-element.12) | copy-start | bytes 1572868
  136.6 1.0 copy-start.18
  136.6 1.0 copy-start.23
  137.2 19.7 %copy-start.20 = (bf16[256,256]{1,0:T(8,128)(2,1)S(1)}, bf16[256,256]{1,0:T(8,128)(2,1)}, u32[]{:S(2)}) copy-start(bf16[256,256]{1,0:T(8,128)(2,1)} %param.11) | copy-start | bytes 393220
where the time goes:
time: 161 us; the launch traced here: 158 us
  matrix products  83.3 us (52%)
  local copies, waits for them, and re-layouts  21.6 us (13%)
  blocking collectives  18.9 us (12%)
  starting transfers between devices  17 us (11%)
  waiting for transfers between devices  12.5 us (8%)
  other arithmetic  3.51 us (2%)
    all_to_all x1, blocking collectives, local(): lax.all_to_all(state, 'seq', split_axis=1, concat_axis=0, tiled=True)  18.9 us
    all_to_all x1, starting transfers between devices, local(): lax.all_to_all(grouped.reshape(groups, 3 * per, positions), 'seq', split_...  17 us
    dot_general x10, matrix products, transform(): jnp.einsum('kn,...ns->...ks', sine_tab, real_grid, precision=PRECISE)  15.8 us
    dot_general x10, matrix products, transform(): jnp.einsum('kn,...ns->...ks', cosine, real_grid, precision=PRECISE)  14.4 us
    dot_general x9, matrix products, transform(): jnp.einsum('kn,...ns->...ks', cosine, imag_grid, precision=PRECISE)  14.2 us
    dot_general x9, matrix products, transform(): jnp.einsum('kn,...ns->...ks', sine_tab, imag_grid, precision=PRECISE)  13.8 us
    all_to_all x1, waiting for transfers between devices, local(): lax.all_to_all(grouped.reshape(groups, 3 * per, positions), 'seq', split_...  12.5 us
    dot_general x6, matrix products, direct_dft(): jnp.einsum('...n,kn->...k', imag_part, sine_tab, precision=PRECISE)  5.65 us
  transfers between devices with their start and end apart: 1, of which 1 were waited for; matrix products, arithmetic and copies ran while one was open for 5% of the time, Pallas kernels for 0%

commit v1 on v0

v1 whole, which is shorter than its diff:
```python
import math

import jax
import jax.numpy as jnp
from jax import lax
from jax.experimental import pallas as pl
from jax.experimental.pallas import tpu as pltpu
from jax.sharding import PartitionSpec as P

SIDE = 256


def halves(values):
    upper = values.astype(jnp.bfloat16)
    return upper, (values - upper.astype(jnp.float32)).astype(jnp.bfloat16)


def product(left, right):
    left_hi, left_lo = halves(left)
    right_hi, right_lo = halves(right)
    total = jnp.dot(left_hi, right_hi, preferred_element_type=jnp.float32)
    total = total + jnp.dot(left_lo, right_hi, preferred_element_type=jnp.float32)
    return total + jnp.dot(left_hi, right_lo, preferred_element_type=jnp.float32)


def make_tables():
    rows = lax.broadcasted_iota(jnp.int32, (SIDE, SIDE), 0)
    cols = lax.broadcasted_iota(jnp.int32, (SIDE, SIDE), 1)
    rows, cols = lax.optimization_barrier((rows, cols))
    step = -2.0 * math.pi / SIDE
    small = ((rows * cols) % SIDE).astype(jnp.float32) * step
    big = (rows * cols).astype(jnp.float32) * (step / SIDE)
    f_re, f_im = jnp.cos(small), jnp.sin(small)
    half = SIDE // 2
    left_fwd = jnp.concatenate([f_re[:, :half], f_im[:, :half]], 0)
    right_fwd = jnp.concatenate(
        [jnp.concatenate([f_re, f_im], 1), jnp.concatenate([-f_im, f_re], 1)], 0
    )
    right_inv = jnp.concatenate(
        [jnp.concatenate([f_re, -f_im], 1), jnp.concatenate([f_im, f_re], 1)], 0
    )
    left_inv = jnp.concatenate([f_re[:half], f_im[:half]], 1)
    return left_fwd, right_fwd, right_inv, left_inv, jnp.cos(big), jnp.sin(big)


def spectrum(rows_in, left_fwd, right_fwd, tw_re, tw_im):
    stacked = product(left_fwd, rows_in)
    b_re, b_im = stacked[:SIDE], stacked[SIDE:]
    t_re = b_re * tw_re - b_im * tw_im
    t_im = b_re * tw_im + b_im * tw_re
    return product(jnp.concatenate([t_re, t_im], 1), right_fwd)


def convolve(sig, filt, bias, tabs):
    left_fwd, right_fwd, right_inv, left_inv, tw_re, tw_im = tabs
    signal = sig.astype(jnp.float32)
    s_spec = spectrum(signal, left_fwd, right_fwd, tw_re, tw_im)
    f_spec = spectrum(filt, left_fwd, right_fwd, tw_re, tw_im)
    s_re, s_im = s_spec[:, :SIDE], s_spec[:, SIDE:]
    f_re, f_im = f_spec[:, :SIDE], f_spec[:, SIDE:]
    p_re = s_re * f_re - s_im * f_im
    p_im = s_re * f_im + s_im * f_re
    d = product(jnp.concatenate([p_re, p_im], 1), right_inv)
    d_re, d_im = d[:, :SIDE], d[:, SIDE:]
    e_re = d_re * tw_re + d_im * tw_im
    e_im = d_im * tw_re - d_re * tw_im
    back = product(left_inv, jnp.concatenate([e_re, e_im], 0))
    scale = 1.0 / (SIDE * SIDE)
    return (back * scale + bias * signal).astype(jnp.bfloat16)


def chain_kernel(short_ref, filt_ref, bias_ref, lf_ref, rf_ref, ri_ref, li_ref, twr_ref, twi_ref, out_ref):
    channel = pl.program_id(0)
    tabs = (lf_ref[...], rf_ref[...], ri_ref[...], li_ref[...], twr_ref[...], twi_ref[...])
    state = short_ref[2, 0]
    for order in range(2):
        conv = convolve(state, filt_ref[order, 0], bias_ref[order, channel], tabs)
        state = (short_ref[order, 0].astype(jnp.float32) * conv.astype(jnp.float32)).astype(jnp.bfloat16)
    out_ref[0] = state


def chain(short, filters, bias):
    per = short.shape[1]
    half = SIDE // 2
    tabs = make_tables()
    full = lambda shape: pl.BlockSpec(shape, lambda c: (0,) * len(shape))
    return pl.pallas_call(
        chain_kernel,
        grid=(per,),
        in_specs=[
            pl.BlockSpec((3, 1, half, SIDE), lambda c: (0, c, 0, 0)),
            pl.BlockSpec((2, 1, half, SIDE), lambda c: (0, c, 0, 0)),
            pl.BlockSpec(memory_space=pltpu.SMEM),
            full((2 * SIDE, half)),
            full((2 * SIDE, 2 * SIDE)),
            full((2 * SIDE, 2 * SIDE)),
            full((half, 2 * SIDE)),
            full((SIDE, SIDE)),
            full((SIDE, SIDE)),
        ],
        out_specs=pl.BlockSpec((1, half, SIDE), lambda c: (c, 0, 0)),
        out_shape=jax.ShapeDtypeStruct((per, half, SIDE), jnp.bfloat16),
        compiler_params=pltpu.CompilerParams(vmem_limit_bytes=48 * 1024 * 1024),
    )(short, filters, bias, *tabs)


def local(layer_input, w_in, short_w, filters, filter_bias, w_out):
    width = w_out.shape[0]
    groups = lax.axis_size("seq")
    per = width // groups
    projected = lax.dot_general(
        w_in, layer_input, (((0,), (1,)), ((), ())), preferred_element_type=jnp.float32
    ).astype(jnp.bfloat16)
    positions = projected.shape[1]
    grouped = jnp.swapaxes(projected.reshape(3, groups, per, positions), 0, 1)
    spread = lax.all_to_all(
        grouped.reshape(groups, 3 * per, positions), "seq", split_axis=0, concat_axis=2, tiled=True
    ).reshape(3 * per, groups * positions)
    me = lax.axis_index("seq")
    taps = lax.dynamic_slice_in_dim(short_w.reshape(3, 3, groups, per), me, 1, axis=2)
    taps = taps.reshape(3, 3 * per)
    extended = jnp.pad(spread.astype(jnp.float32), ((0, 0), (2, 0)))
    length = spread.shape[1]
    short = (
        taps[0][:, None] * extended[:, 2:]
        + taps[1][:, None] * extended[:, 1 : length + 1]
        + taps[2][:, None] * extended[:, :length]
    ).astype(jnp.bfloat16)
    half = SIDE // 2
    state = chain(
        short.reshape(3, per, half, SIDE),
        filters.reshape(2, per, half, SIDE),
        filter_bias,
    ).reshape(per, length)
    returned = lax.all_to_all(state, "seq", split_axis=1, concat_axis=0, tiled=True)
    output = lax.dot_general(
        returned, w_out, (((0,), (0,)), ((), ())), preferred_element_type=jnp.float32
    )
    return output.astype(jnp.bfloat16)


def solution(mesh):
    return jax.shard_map(
        local,
        mesh=mesh,
        in_specs=(P(("win", "seq"), None), P(), P(), P(None, "seq", None), P(None, "seq"), P()),
        out_specs=P(("win", "seq"), None),
        check_vma=False,
    )
```

time: 161 us -> 77.6 us (0.48); the launches traced: 158 us -> 77.3 us
  matrix products: 83.3 us -> 2.99 us
  local copies, waits for them, and re-layouts: 21.6 us -> 5.34 us
  Pallas kernels: 0 us -> 12.3 us
  other arithmetic: 3.51 us -> 6.82 us
    dot_general x66 -> x0, matrix products: 81.2 us -> none  [the longest x10 15.8 us: transform(): jnp.einsum('kn,...ns->...ks', sine_tab, real_grid, precision=PRECISE)]
    pallas_call x0 -> x1, Pallas kernels: none -> 12.3 us  [chain(): pl.pallas_call(chain_kernel, grid=(per,), in_specs=[pl.BlockSpec((3, 1, h...]
    reshape x12 -> x1, local copies, waits for them, and re-layouts: 7.97 us -> 0.45 us  [local(): filters.reshape(2, per, half, SIDE)]
    sub x6 -> x0, local copies, waits for them, and re-layouts: 3.95 us -> none  [the longest x4 3.09 us: long_convolve(): prod_real = signal_real * kernel_real - signal_imag * kernel_imag]
    neg x4 -> x0, local copies, waits for them, and re-layouts: 2.74 us -> none  [long_convolve(): back_real, back_imag = transform(prod_real, -prod_imag)]
    cos x0 -> x1, other arithmetic: none -> 2.55 us  [make_tables(): jnp.cos(big)]
  transfers between devices with their start and end apart: 1 -> 1, of which waited for: 1 -> 1; matrix products, arithmetic and copies ran while one was open for 5% -> 8% of each run, Pallas kernels for 0% -> 0%
where the time goes in v1:
time: 77.6 us; the launch traced here: 77.3 us
  blocking collectives  18.9 us (24%)
  starting transfers between devices  16.8 us (22%)
  waiting for transfers between devices  13.9 us (18%)
  Pallas kernels  12.3 us (16%)
  other arithmetic  6.82 us (9%)
  local copies, waits for them, and re-layouts  5.34 us (7%)
  matrix products  2.99 us (4%)
    all_to_all x1, blocking collectives, local(): lax.all_to_all(state, 'seq', split_axis=1, concat_axis=0, tiled=True)  18.9 us
    all_to_all x1, starting transfers between devices, local(): lax.all_to_all(grouped.reshape(groups, 3 * per, positions), 'seq', split_...  16.8 us
    all_to_all x1, waiting for transfers between devices, local(): lax.all_to_all(grouped.reshape(groups, 3 * per, positions), 'seq', split_...  13.9 us
    pallas_call x1, Pallas kernels, chain(): pl.pallas_call(chain_kernel, grid=(per,), in_specs=[pl.BlockSpec((3, 1, h...  12.3 us
    unnamed x23, local copies, waits for them, and re-layouts  2.57 us
    cos x1, other arithmetic, make_tables(): jnp.cos(big)  2.55 us
    dot_general x1, matrix products, local(): lax.dot_general(returned, w_out, (((0,), (0,)), ((), ())), preferred_elem...  1.79 us
    sin x1, other arithmetic, make_tables(): jnp.sin(big)  1.59 us
  transfers between devices with their start and end apart: 1, of which 1 were waited for; matrix products, arithmetic and copies ran while one was open for 8% of the time, Pallas kernels for 0%

profile of v1, /device:TPU:1, one launch (start us, length us, event | category | flops | bytes accessed | tf_op | source)
XLA Modules:
  0.0 77.3 jit_solution(6548681128698394147)
XLA Ops:
  0.0 0.0 copy-start
  0.0 1.0 %copy-done = bf16[256,768]{1,0:T(8,128)(2,1)S(1)} copy-done((bf16[256,768]{1,0:T(8,128)(2,1)S(1)}, bf16[256,768]{1,0:T(8,128)(2,1)}, u32[]{:S(2)}) %copy-start) | copy-done | bytes 393240
  1.0 1.2 %convolution_convert_fusion = bf16[768,256]{1,0:T(8,128)(2,1)S(1)} fusion(bf16[256,768]{1,0:T(8,128)(2,1)S(1)} %copy-done, bf16[256,256]{1,0:T(8,128)(2,1)} %param.6), kind=kOutput, calls=%fused_computation.4 | convolution fusion | flops 100859904 | bytes 917504 | tf_op jit(solution)/shard_map/dot_general | solution.py:111
  2.2 0.2 reshape.37
  2.4 1.0 %copy.11 = bf16[128,6,256]{2,1,0:T(8,128)(2,1)} copy(bf16[128,6,256]{2,0,1:T(8,128)(2,1)S(1)} %bitcast.20) | data formatting | bytes 786432 | tf_op jit(solution)/shard_map/reshape | solution.py:117
  3.4 16.8 %all-to-all-start = ((bf16[128,6,256]{2,1,0:T(8,128)(2,1)}), bf16[128,6,256]{2,1,0:T(8,128)(2,1)}, u32[]{:S(2)}, u32[]{:S(2)}) async-start(bf16[128,6,256]{2,1,0:T(8,128)(2,1)} %copy.11), calls=%async_computation | async-start | bytes 1048576 | tf_op jit(solution)/shard_map/all_to_all | solution.py:116
  20.4 1.6 %fusion.5 = (f32[256,256]{1,0:T(8,128)}, s32[256,256]{1,0:T(8,128)S(1)}) fusion(s32[256,256]{1,0:T(8,128)S(1)} %iota.10, s32[256,256]{1,0:T(8,128)S(1)} %iota.11), kind=kLoop, calls=%fused_computation.19 | loop fusion | flops 196608 | bytes 1048576 | tf_op jit(solution)/shard_map/sin | solution.py:43
  21.9 0.0 copy-start.10
  21.9 2.5 %fusion.6 = (f32[256,256]{1,0:T(8,128)S(1)}, f32[256,256]{1,0:T(8,128)S(1)}, f32[256,256]{1,0:T(8,128)}, f32[256,256]{1,0:T(8,128)S(1)}) fusion(s32[256,256]{1,0:T(8,128)S(1)} %get-tuple-element.13), kind=kLoop, calls=%fused_computation.20 | loop fusion | flops 1048576 | bytes 1310720 | tf_op jit(solution)/shard_map/cos | solution.py:43
  24.5 0.0 copy-start.6
  24.5 0.0 copy-start.4
  24.5 0.0 copy-start.9
  24.5 0.7 copy-done.6
  25.2 0.1 copy-done.4
  25.3 0.0 copy-done.10
  25.3 0.5 reshape.36
  25.9 0.1 mul.46
  26.0 0.1 mul.49
  26.1 0.1 mul.52
  26.2 0.0 copy-done.9
  26.2 0.5 reshape.40.filt_ref
  26.6 0.0 copy-start.5
  26.6 0.0 copy-start.7
  26.6 0.0 copy-start.8
  26.7 0.7 pad_maximum_fusion.5.li_ref
  27.4 0.2 copy-done.5
  27.6 0.2 copy-done.7
  27.7 0.1 copy-done.8
  27.8 0.2 fusion.1
  28.0 13.9 %all-to-all-done = bf16[128,6,256]{2,1,0:T(8,128)(2,1)} async-done(((bf16[128,6,256]{2,1,0:T(8,128)(2,1)}), bf16[128,6,256]{2,1,0:T(8,128)(2,1)}, u32[]{:S(2)}, u32[]{:S(2)}) %all-to-all-start) | async-done | bytes 393248 | tf_op jit(solution)/shard_map/all_to_all | solution.py:116
  42.0 1.1 %bitcast_convert_fusion = f32[128,1,6,256]{3,2,0,1:T(8,128)S(1)} fusion(bf16[128,6,256]{2,1,0:T(8,128)(2,1)} %all-to-all-done), kind=kLoop, calls=%fused_computation.9 | loop fusion | flops 196608 | bytes 1179648 | tf_op jit(solution)/shard_map/convert_element_type | solution.py:122
  43.1 0.0 copy-start.1
  43.1 0.0 copy-start.2
  43.1 0.0 copy-start.3
  43.1 0.6 add_convert_fusion
  43.8 0.1 copy.13
  43.8 0.2 copy-done.1
  44.0 0.1 copy-done.2
  44.1 0.0 copy-done.3
  44.1 12.3 %shard_map.64 = bf16[2,128,256]{2,1,0:T(8,128)(2,1)S(1)} custom-call(bf16[3,2,128,256]{3,2,1,0:T(8,128)(2,1)S(1)} %bitcast.17, f32[2,2,128,256]{3,2,1,0:T(8,128)S(1)} %reshape.40.filt_ref, f32[2,2]{1,0:T(2,128)S(1)} %copy-done.3, f32[512,128]{1,0:T(8,128)S(1)} %pad_maximum_fusion.4.lf_ref, f32[512,512]{1,0:T(8,128)S(1)} %get-tuple-element.15.rf_ref, ...), custom_call_target="tpu_custom_call" | custom-call | tf_op jit(solution)/shard_map/pallas_call | solution.py:87
  56.4 0.1 copy.12
  56.6 18.9 %all_to_all.25 = bf16[2,128,256]{2,0,1:T(2,128)(2,1)S(1)} all-to-all(bf16[2,128,256]{2,0,1:T(2,128)(2,1)S(1)} %copy.12), channel_id=1, replica_groups=mesh['win'=2,'seq'=128] {'seq'}, dimensions={1} | all-to-all | bytes 262144 | tf_op jit(solution)/shard_map/all_to_all | solution.py:135
  75.4 0.1 all_to_all.22
  75.5 1.8 %convolution_convert_fusion.1 = bf16[256,256]{1,0:T(8,128)(2,1)} fusion(bf16[256,256]{1,0:T(8,128)(2,1)S(1)} %all_to_all.22, bf16[256,256]{1,0:T(8,128)(2,1)} %param.11), kind=kOutput, calls=%fused_computation.5 | convolution fusion | flops 33619968 | bytes 393216 | tf_op jit(solution)/shard_map/dot_general | solution.py:136
  (9 shorter events, 0.2 us)
Async XLA Ops:
  0.0 1.0 %copy-start = (bf16[256,768]{1,0:T(8,128)(2,1)S(1)}, bf16[256,768]{1,0:T(8,128)(2,1)}, u32[]{:S(2)}) copy-start(bf16[256,768]{1,0:T(8,128)(2,1)} %param.7) | copy-start | bytes 1179652
  3.4 38.5 %all-to-all-start = ((bf16[128,6,256]{2,1,0:T(8,128)(2,1)}), bf16[128,6,256]{2,1,0:T(8,128)(2,1)}, u32[]{:S(2)}, u32[]{:S(2)}) async-start(bf16[128,6,256]{2,1,0:T(8,128)(2,1)} %copy.11), calls=%async_computation | async-start | bytes 1048576 | tf_op jit(solution)/shard_map/all_to_all | solution.py:116
  21.9 3.4 %copy-start.10 = (f32[3,768]{1,0:T(4,128)S(1)}, f32[3,768]{1,0:T(4,128)}, u32[]{:S(2)}) copy-start(f32[3,768]{1,0:T(4,128)} %param.8) | copy-start | bytes 27652
  24.5 0.7 copy-start.6
  24.5 0.8 %copy-start.4 = (f32[256,256]{1,0:T(8,128)}, f32[256,256]{1,0:T(8,128)S(1)}, u32[]{:S(2)}) copy-start(f32[256,256]{1,0:T(8,128)S(1)} %get-tuple-element.17) | copy-start | bytes 786436
  24.5 1.7 %copy-start.9 = (f32[2,2,32768]{2,1,0:T(2,128)S(1)}, f32[2,2,32768]{2,1,0:T(2,128)}, u32[]{:S(2)}) copy-start(f32[2,2,32768]{2,1,0:T(2,128)} %param.9) | copy-start | bytes 1572868
  26.6 1.0 %copy-start.5 = (f32[256,256]{1,0:T(8,128)S(1)}, f32[256,256]{1,0:T(8,128)}, u32[]{:S(2)}) copy-start(f32[256,256]{1,0:T(8,128)} %copy-done.4) | copy-start | bytes 786436
  26.6 1.1 %copy-start.7 = (f32[256,256]{1,0:T(8,128)S(1)}, f32[256,256]{1,0:T(8,128)}, u32[]{:S(2)}) copy-start(f32[256,256]{1,0:T(8,128)} %copy-done.6) | copy-start | bytes 786436
  26.6 1.2 %copy-start.8 = (f32[256,256]{1,0:T(8,128)S(1)}, f32[256,256]{1,0:T(8,128)}, u32[]{:S(2)}) copy-start(f32[256,256]{1,0:T(8,128)} %get-tuple-element.18) | copy-start | bytes 786436
  43.1 1.0 %copy-start.1 = (f32[128,512]{1,0:T(8,128)S(1)}, f32[128,512]{1,0:T(8,128)}, u32[]{:S(2)}) copy-start(f32[128,512]{1,0:T(8,128)} %pad_maximum_fusion.5.li_ref) | copy-start | bytes 786436
  43.1 1.0 %copy-start.2 = (f32[256,256]{1,0:T(8,128)S(1)}, f32[256,256]{1,0:T(8,128)}, u32[]{:S(2)}) copy-start(f32[256,256]{1,0:T(8,128)} %get-tuple-element.12.twi_ref) | copy-start | bytes 786436
  43.1 1.0 %copy-start.3 = (f32[2,2]{1,0:T(2,128)S(1)}, f32[2,2]{1,0:T(2,128)}, u32[]{:S(2)}) copy-start(f32[2,2]{1,0:T(2,128)} %bias_ref.1) | copy-start | bytes 52

commit v2 on v1

--- a/solution.py
+++ b/solution.py
@@ -23,6 +23,12 @@
     return total + jnp.dot(left_hi, right_lo, preferred_element_type=jnp.float32)
 
 
+def single(left, right):
+    return jnp.dot(
+        left.astype(jnp.bfloat16), right.astype(jnp.bfloat16), preferred_element_type=jnp.float32
+    )
+
+
 def make_tables():
     rows = lax.broadcasted_iota(jnp.int32, (SIDE, SIDE), 0)
     cols = lax.broadcasted_iota(jnp.int32, (SIDE, SIDE), 1)
@@ -43,53 +49,80 @@
     return left_fwd, right_fwd, right_inv, left_inv, jnp.cos(big), jnp.sin(big)
 
 
-def spectrum(rows_in, left_fwd, right_fwd, tw_re, tw_im):
-    stacked = product(left_fwd, rows_in)
+def spectrum(rows_in, left_fwd, right_fwd, tw_re, tw_im, mul):
+    stacked = mul(left_fwd, rows_in)
     b_re, b_im = stacked[:SIDE], stacked[SIDE:]
     t_re = b_re * tw_re - b_im * tw_im
     t_im = b_re * tw_im + b_im * tw_re
-    return product(jnp.concatenate([t_re, t_im], 1), right_fwd)
+    return mul(jnp.concatenate([t_re, t_im], 1), right_fwd)
 
 
-def convolve(sig, filt, bias, tabs):
+def filter_kernel(filt_ref, lf_ref, rf_ref, twr_ref, twi_ref, out_ref):
+    out_ref[0, 0] = spectrum(
+        filt_ref[0, 0], lf_ref[...], rf_ref[...], twr_ref[...], twi_ref[...], product
+    )
+
+
+def filter_spectra(filters, tabs):
+    left_fwd, right_fwd, _, _, tw_re, tw_im = tabs
+    orders, per = filters.shape[:2]
+    half = SIDE // 2
+    full = lambda shape: pl.BlockSpec(shape, lambda o, c: (0,) * len(shape))
+    return pl.pallas_call(
+        filter_kernel,
+        grid=(orders, per),
+        in_specs=[
+            pl.BlockSpec((1, 1, half, SIDE), lambda o, c: (o, c, 0, 0)),
+            full((2 * SIDE, half)),
+            full((2 * SIDE, 2 * SIDE)),
+            full((SIDE, SIDE)),
+            full((SIDE, SIDE)),
+        ],
+        out_specs=pl.BlockSpec((1, 1, SIDE, 2 * SIDE), lambda o, c: (o, c, 0, 0)),
+        out_shape=jax.ShapeDtypeStruct((orders, per, SIDE, 2 * SIDE), jnp.float32),
+        compiler_params=pltpu.CompilerParams(vmem_limit_bytes=48 * 1024 * 1024),
+    )(filters, left_fwd, right_fwd, tw_re, tw_im)
+
+
+def convolve(sig, f_spec, bias, tabs):
     left_fwd, right_fwd, right_inv, left_inv, tw_re, tw_im = tabs
     signal = sig.astype(jnp.float32)
-    s_spec = spectrum(signal, left_fwd, right_fwd, tw_re, tw_im)
-    f_spec = spectrum(filt, left_fwd, right_fwd, tw_re, tw_im)
+    s_spec = spectrum(sig, left_fwd, right_fwd, tw_re, tw_im, single)
     s_re, s_im = s_spec[:, :SIDE], s_spec[:, SIDE:]
     f_re, f_im = f_spec[:, :SIDE], f_spec[:, SIDE:]
     p_re = s_re * f_re - s_im * f_im
     p_im = s_re * f_im + s_im * f_re
-    d = product(jnp.concatenate([p_re, p_im], 1), right_inv)
+    d = single(jnp.concatenate([p_re, p_im], 1), right_inv)
     d_re, d_im = d[:, :SIDE], d[:, SIDE:]
     e_re = d_re * tw_re + d_im * tw_im
     e_im = d_im * tw_re - d_re * tw_im
-    back = product(left_inv, jnp.concatenate([e_re, e_im], 0))
+    back = single(left_inv, jnp.concatenate([e_re, e_im], 0))
     scale = 1.0 / (SIDE * SIDE)
     return (back * scale + bias * signal).astype(jnp.bfloat16)
 
 
-def chain_kernel(short_ref, filt_ref, bias_ref, lf_ref, rf_ref, ri_ref, li_ref, twr_ref, twi_ref, out_ref):
+def chain_kernel(short_ref, spec_ref, bias_ref, lf_ref, rf_ref, ri_ref, li_ref, twr_ref, twi_ref, out_ref):
     channel = pl.program_id(0)
     tabs = (lf_ref[...], rf_ref[...], ri_ref[...], li_ref[...], twr_ref[...], twi_ref[...])
     state = short_ref[2, 0]
     for order in range(2):
-        conv = convolve(state, filt_ref[order, 0], bias_ref[order, channel], tabs)
+        conv = convolve(state, spec_ref[order, 0], bias_ref[order, channel], tabs)
         state = (short_ref[order, 0].astype(jnp.float32) * conv.astype(jnp.float32)).astype(jnp.bfloat16)
     out_ref[0] = state
 
 
-def chain(short, filters, bias):
+def chain(short, spectra, bias, tabs):
     per = short.shape[1]
     half = SIDE // 2
-    tabs = make_tables()
+    left_fwd, right_fwd, right_inv, left_inv, tw_re, tw_im = tabs
+    low = lambda t: t.astype(jnp.bfloat16)
     full = lambda shape: pl.BlockSpec(shape, lambda c: (0,) * len(shape))
     return pl.pallas_call(
         chain_kernel,
         grid=(per,),
         in_specs=[
             pl.BlockSpec((3, 1, half, SIDE), lambda c: (0, c, 0, 0)),
-            pl.BlockSpec((2, 1, half, SIDE), lambda c: (0, c, 0, 0)),
+            pl.BlockSpec((2, 1, SIDE, 2 * SIDE), lambda c: (0, c, 0, 0)),
             pl.BlockSpec(memory_space=pltpu.SMEM),
             full((2 * SIDE, half)),
             full((2 * SIDE, 2 * SIDE)),
@@ -101,7 +134,7 @@
         out_specs=pl.BlockSpec((1, half, SIDE), lambda c: (c, 0, 0)),
         out_shape=jax.ShapeDtypeStruct((per, half, SIDE), jnp.bfloat16),
         compiler_params=pltpu.CompilerParams(vmem_limit_bytes=48 * 1024 * 1024),
-    )(short, filters, bias, *tabs)
+    )(short, spectra, bias, low(left_fwd), low(right_fwd), low(right_inv), low(left_inv), tw_re, tw_im)
 
 
 def local(layer_input, w_in, short_w, filters, filter_bias, w_out):
@@ -113,6 +146,8 @@
     ).astype(jnp.bfloat16)
     positions = projected.shape[1]
     grouped = jnp.swapaxes(projected.reshape(3, groups, per, positions), 0, 1)
+    tabs = make_tables()
+    spectra = filter_spectra(filters.reshape(2, per, SIDE // 2, SIDE), tabs)
     spread = lax.all_to_all(
         grouped.reshape(groups, 3 * per, positions), "seq", split_axis=0, concat_axis=2, tiled=True
     ).reshape(3 * per, groups * positions)
@@ -129,8 +164,9 @@
     half = SIDE // 2
     state = chain(
         short.reshape(3, per, half, SIDE),
-        filters.reshape(2, per, half, SIDE),
+        spectra,
         filter_bias,
+        tabs,
     ).reshape(per, length)
     returned = lax.all_to_all(state, "seq", split_axis=1, concat_axis=0, tiled=True)
     output = lax.dot_general(

time: 77.6 us -> 69.5 us (0.90)
  waiting for transfers between devices: 13.9 us -> 8.97 us
  Pallas kernels: 12.3 us -> 9.41 us
  local copies, waits for them, and re-layouts: 5.34 us -> 3.91 us
  other arithmetic: 6.82 us -> 7.75 us
    pallas_call x1, Pallas kernels: 12.3 us -> 4.33 us  [chain(): pl.pallas_call(chain_kernel, grid=(per,), in_specs=[pl.BlockSpec((3, 1, h...]
    pallas_call x0 -> x1, Pallas kernels: none -> 5.08 us  [filter_spectra(): pl.pallas_call(filter_kernel, grid=(orders, per), in_specs=[pl.BlockSpec(...]
    all_to_all x1, waiting for transfers between devices: 13.9 us -> 8.97 us  [local(): lax.all_to_all(grouped.reshape(groups, 3 * per, positions), 'seq', split_...]
    cos x1 -> x0, other arithmetic: 2.55 us -> none  [make_tables(): jnp.cos(big)]
    another operation x0 -> x2, other arithmetic: none -> 1.67 us
    unnamed x23 -> x37, local copies, waits for them, and re-layouts: 2.57 us -> 1.14 us
  transfers between devices with their start and end apart: 1 -> 1, of which waited for: 1 -> 1; matrix products, arithmetic and copies ran while one was open for 8% -> 11% of each run, Pallas kernels for 0% -> 7%
where the time goes in v2:
time: 69.5 us; the launch traced here: 69.2 us
  blocking collectives  18.8 us (27%)
  starting transfers between devices  17 us (24%)
  Pallas kernels  9.41 us (14%)
  waiting for transfers between devices  8.97 us (13%)
  other arithmetic  7.75 us (11%)
  local copies, waits for them, and re-layouts  3.91 us (6%)
  matrix products  3 us (4%)
    all_to_all x1, blocking collectives, local(): lax.all_to_all(state, 'seq', split_axis=1, concat_axis=0, tiled=True)  18.8 us
    all_to_all x1, starting transfers between devices, local(): lax.all_to_all(grouped.reshape(groups, 3 * per, positions), 'seq', split_...  17 us
    all_to_all x1, waiting for transfers between devices, local(): lax.all_to_all(grouped.reshape(groups, 3 * per, positions), 'seq', split_...  8.97 us
    pallas_call x1, Pallas kernels, filter_spectra(): pl.pallas_call(filter_kernel, grid=(orders, per), in_specs=[pl.BlockSpec(...  5.08 us
    pallas_call x1, Pallas kernels, chain(): pl.pallas_call(chain_kernel, grid=(per,), in_specs=[pl.BlockSpec((3, 1, h...  4.33 us
    sin x1, other arithmetic, make_tables(): jnp.sin(big)  1.9 us
    dot_general x1, matrix products, local(): lax.dot_general(returned, w_out, (((0,), (0,)), ((), ())), preferred_elem...  1.79 us
    another operation x2, other arithmetic  1.67 us
  transfers between devices with their start and end apart: 1, of which 1 were waited for; matrix products, arithmetic and copies ran while one was open for 11% of the time, Pallas kernels for 7%

profile of v2, /device:TPU:1, one launch (start us, length us, event | category | flops | bytes accessed | tf_op | source)
XLA Modules:
  0.0 69.2 jit_solution(9582574292384296657)
XLA Ops:
  0.0 0.0 copy-start
  0.0 1.0 %copy-done = bf16[256,768]{1,0:T(8,128)(2,1)S(1)} copy-done((bf16[256,768]{1,0:T(8,128)(2,1)S(1)}, bf16[256,768]{1,0:T(8,128)(2,1)}, u32[]{:S(2)}) %copy-start) | copy-done | bytes 393240
  1.0 1.2 %convolution_convert_fusion = bf16[768,256]{1,0:T(8,128)(2,1)S(1)} fusion(bf16[256,768]{1,0:T(8,128)(2,1)S(1)} %copy-done, bf16[256,256]{1,0:T(8,128)(2,1)} %param.6), kind=kOutput, calls=%fused_computation | convolution fusion | flops 100859904 | bytes 917504 | tf_op jit(solution)/shard_map/dot_general | solution.py:144
  2.2 0.2 reshape.37
  2.4 1.0 %copy.11 = bf16[128,6,256]{2,1,0:T(8,128)(2,1)} copy(bf16[128,6,256]{2,0,1:T(8,128)(2,1)S(1)} %bitcast.20) | data formatting | bytes 786432 | tf_op jit(solution)/shard_map/reshape | solution.py:152
  3.4 0.0 copy-start.16
  3.4 17.0 %all-to-all-start = ((bf16[128,6,256]{2,1,0:T(8,128)(2,1)}), bf16[128,6,256]{2,1,0:T(8,128)(2,1)}, u32[]{:S(2)}, u32[]{:S(2)}) async-start(bf16[128,6,256]{2,1,0:T(8,128)(2,1)} %copy.11), calls=%async_computation | async-start | bytes 1048576 | tf_op jit(solution)/shard_map/all_to_all | solution.py:151
  20.5 0.0 copy-start.17
  20.5 1.6 %negate_convert_fusion = (bf16[256,256]{1,0:T(8,128)(2,1)}, f32[256,256]{1,0:T(8,128)S(1)}, s32[256,256]{1,0:T(8,128)S(1)}) fusion(s32[256,256]{1,0:T(8,128)S(1)} %iota.10, s32[256,256]{1,0:T(8,128)S(1)} %iota.11), kind=kLoop, calls=%fused_computation.22 | loop fusion | flops 1048576 | bytes 1179648 | tf_op jit(solution)/shard_map/convert.12
  22.1 0.0 copy-start.5
  22.1 1.9 %fusion.3 = (f32[256,256]{1,0:T(8,128)S(1)}, f32[256,256]{1,0:T(8,128)S(1)}, bf16[256,256]{1,0:T(8,128)(2,1)S(1)}, f32[256,256]{1,0:T(8,128)S(1)}) fusion(s32[256,256]{1,0:T(8,128)S(1)} %get-tuple-element.14), kind=kLoop, calls=%fused_computation.14 | loop fusion | flops 1048576 | bytes 1179648 | tf_op jit(solution)/shard_map/sin | solution.py:49
  24.1 0.0 copy-start.7
  24.1 0.0 copy-start.13
  24.1 0.0 copy-start.9
  24.1 0.0 copy-done.16
  24.1 0.0 copy-start.11
  24.1 0.5 reshape.40.filt_ref
  24.6 0.0 copy-done.17
  24.6 0.5 reshape.36
  25.2 0.1 mul.46
  25.3 0.1 mul.49
  25.4 0.1 mul.52
  25.5 0.0 copy-done.5
  25.6 0.1 maximum_maximum_fusion.rf_ref
  25.7 0.0 copy-done.7
  25.7 0.0 copy-done.13
  25.7 0.0 copy-done.9
  25.7 0.0 copy-done.11
  25.7 0.0 copy-start.10
  25.7 0.0 copy-start.12
  25.7 0.0 copy-start.6
  25.7 0.0 copy-start.8
  25.7 0.0 copy-start.14
  25.8 0.0 copy-start.15
  25.8 5.1 %shard_map.64.spec_ref = f32[2,2,256,512]{3,2,1,0:T(8,128)S(1)} custom-call(f32[2,2,128,256]{3,2,1,0:T(8,128)S(1)} %reshape.40.filt_ref, f32[512,128]{1,0:T(8,128)S(1)} %pad_maximum_fusion.lf_ref, f32[512,512]{1,0:T(8,128)S(1)} %maximum_maximum_fusion.rf_ref, f32[256,256]{1,0:T(8,128)S(1)} %get-tuple-element.20.twr_ref, f32[256,256]{1,0:T(8,128)S(1)} %get-tuple-element.19.twi_ref), custom_call_target="tpu_custom_call" | custom-call | tf_op jit(solution)/shard_map/pallas_call | solution.py:71
  30.9 0.0 copy-done.10
  30.9 0.0 copy-done.12
  30.9 0.7 fusion.7.lf_ref
  31.5 0.7 pad_maximum_fusion.1.li_ref
  32.2 0.0 copy-done.6
  32.2 0.0 copy-done.8
  32.2 0.0 copy-done.14
  32.2 0.0 copy-done.15
  32.2 0.9 %maximum_maximum_fusion.1 = (bf16[512,512]{1,0:T(8,128)(2,1)S(1)}, bf16[512,512]{1,0:T(8,128)(2,1)}) fusion(bf16[256,256]{1,0:T(8,128)(2,1)S(1)} %copy-done.14, bf16[256,256]{1,0:T(8,128)(2,1)S(1)} %get-tuple-element.17, bf16[256,256]{1,0:T(8,128)(2,1)S(1)} %copy-done.15, f32[256,256]{1,0:T(8,128)S(1)} %copy-done.8, f32[256,256]{1,0:T(8,128)S(1)} %get-tuple-element.18, ...), kind=kLoop, calls=%fused_computation.4 | loop fusion | flops 4194304 | bytes 2228224 | tf_op jit(solution)/shard_map/concatenate | solution.py:45
  33.1 0.0 copy-start.4
  33.1 9.0 %all-to-all-done = bf16[128,6,256]{2,1,0:T(8,128)(2,1)} async-done(((bf16[128,6,256]{2,1,0:T(8,128)(2,1)}), bf16[128,6,256]{2,1,0:T(8,128)(2,1)}, u32[]{:S(2)}, u32[]{:S(2)}) %all-to-all-start) | async-done | bytes 393248 | tf_op jit(solution)/shard_map/all_to_all | solution.py:151
  42.1 0.0 copy-start.1
  42.1 0.0 copy-start.2
  42.1 0.0 copy-start.3
  42.1 1.2 %bitcast_convert_fusion = f32[128,1,6,256]{3,2,0,1:T(8,128)S(1)} fusion(bf16[128,6,256]{2,1,0:T(8,128)(2,1)} %all-to-all-done), kind=kLoop, calls=%fused_computation.5 | loop fusion | flops 196608 | bytes 1179648 | tf_op jit(solution)/shard_map/convert_element_type | solution.py:157
  43.3 0.6 add_convert_fusion
  43.9 0.1 copy.13
  44.0 0.0 copy-done.4
  44.0 0.0 copy-done.1
  44.0 0.0 copy-done.2
  44.0 0.0 copy-done.3
  44.1 4.3 %shard_map.65 = bf16[2,128,256]{2,1,0:T(8,128)(2,1)S(1)} custom-call(bf16[3,2,128,256]{3,2,1,0:T(8,128)(2,1)S(1)} %bitcast.17, f32[2,2,256,512]{3,2,1,0:T(8,128)S(1)} %shard_map.64.spec_ref, f32[2,2]{1,0:T(2,128)S(1)} %copy-done.4, bf16[512,128]{1,0:T(8,128)(2,1)S(1)} %copy-done.2, bf16[512,512]{1,0:T(8,128)(2,1)S(1)} %copy-done.1, ...), custom_call_target="tpu_custom_call" | custom-call | tf_op jit(solution)/shard_map/pallas_call | solution.py:120
  48.4 0.1 copy.12
  48.5 18.8 %all_to_all.25 = bf16[2,128,256]{2,0,1:T(2,128)(2,1)S(1)} all-to-all(bf16[2,128,256]{2,0,1:T(2,128)(2,1)S(1)} %copy.12), channel_id=1, replica_groups=mesh['win'=2,'seq'=128] {'seq'}, dimensions={1} | all-to-all | bytes 262144 | tf_op jit(solution)/shard_map/all_to_all | solution.py:171
  67.4 0.1 all_to_all.22
  67.4 1.8 %convolution_convert_fusion.1 = bf16[256,256]{1,0:T(8,128)(2,1)} fusion(bf16[256,256]{1,0:T(8,128)(2,1)S(1)} %all_to_all.22, bf16[256,256]{1,0:T(8,128)(2,1)} %param.11), kind=kOutput, calls=%fused_computation.1 | convolution fusion | flops 33619968 | bytes 393216 | tf_op jit(solution)/shard_map/dot_general | solution.py:172
  (10 shorter events, 0.2 us)
Async XLA Ops:
  0.0 1.0 %copy-start = (bf16[256,768]{1,0:T(8,128)(2,1)S(1)}, bf16[256,768]{1,0:T(8,128)(2,1)}, u32[]{:S(2)}) copy-start(bf16[256,768]{1,0:T(8,128)(2,1)} %param.7) | copy-start | bytes 1179652
  3.4 20.7 %copy-start.16 = (f32[2,2,32768]{2,1,0:T(2,128)S(1)}, f32[2,2,32768]{2,1,0:T(2,128)}, u32[]{:S(2)}) copy-start(f32[2,2,32768]{2,1,0:T(2,128)} %param.9) | copy-start | bytes 1572868
  3.4 38.7 %all-to-all-start = ((bf16[128,6,256]{2,1,0:T(8,128)(2,1)}), bf16[128,6,256]{2,1,0:T(8,128)(2,1)}, u32[]{:S(2)}, u32[]{:S(2)}) async-start(bf16[128,6,256]{2,1,0:T(8,128)(2,1)} %copy.11), calls=%async_computation | async-start | bytes 1048576 | tf_op jit(solution)/shard_map/all_to_all | solution.py:151
  20.5 4.1 %copy-start.17 = (f32[3,768]{1,0:T(4,128)S(1)}, f32[3,768]{1,0:T(4,128)}, u32[]{:S(2)}) copy-start(f32[3,768]{1,0:T(4,128)} %param.8) | copy-start | bytes 27652
  22.1 3.4 %copy-start.5 = (f32[256,256]{1,0:T(8,128)}, f32[256,256]{1,0:T(8,128)S(1)}, u32[]{:S(2)}) copy-start(f32[256,256]{1,0:T(8,128)S(1)} %get-tuple-element.13) | copy-start | bytes 786436
  24.1 1.6 %copy-start.7 = (f32[256,256]{1,0:T(8,128)}, f32[256,256]{1,0:T(8,128)S(1)}, u32[]{:S(2)}) copy-start(f32[256,256]{1,0:T(8,128)S(1)} %get-tuple-element.22) | copy-start | bytes 786436
  24.1 1.6 %copy-start.13 = (bf16[256,256]{1,0:T(8,128)(2,1)}, bf16[256,256]{1,0:T(8,128)(2,1)S(1)}, u32[]{:S(2)}) copy-start(bf16[256,256]{1,0:T(8,128)(2,1)S(1)} %get-tuple-element.21) | copy-start | bytes 393220
  24.1 1.6 %copy-start.9 = (f32[256,128]{1,0:T(8,128)}, f32[256,128]{1,0:T(8,128)S(1)}, u32[]{:S(2)}) copy-start(f32[256,128]{1,0:T(8,128)S(1)} %slice.42) | copy-start | bytes 393220
  24.1 1.6 %copy-start.11 = (f32[256,128]{1,0:T(8,128)}, f32[256,128]{1,0:T(8,128)S(1)}, u32[]{:S(2)}) copy-start(f32[256,128]{1,0:T(8,128)S(1)} %slice.43) | copy-start | bytes 393220
  25.7 5.2 %copy-start.10 = (f32[256,128]{1,0:T(8,128)S(1)}, f32[256,128]{1,0:T(8,128)}, u32[]{:S(2)}) copy-start(f32[256,128]{1,0:T(8,128)} %copy-done.9) | copy-start | bytes 393220
  25.7 5.2 %copy-start.12 = (f32[256,128]{1,0:T(8,128)S(1)}, f32[256,128]{1,0:T(8,128)}, u32[]{:S(2)}) copy-start(f32[256,128]{1,0:T(8,128)} %copy-done.11) | copy-start | bytes 393220
  25.7 6.5 %copy-start.6 = (f32[256,256]{1,0:T(8,128)S(1)}, f32[256,256]{1,0:T(8,128)}, u32[]{:S(2)}) copy-start(f32[256,256]{1,0:T(8,128)} %copy-done.5) | copy-start | bytes 786436
  25.7 6.5 %copy-start.8 = (f32[256,256]{1,0:T(8,128)S(1)}, f32[256,256]{1,0:T(8,128)}, u32[]{:S(2)}) copy-start(f32[256,256]{1,0:T(8,128)} %copy-done.7) | copy-start | bytes 786436
  25.7 6.5 %copy-start.14 = (bf16[256,256]{1,0:T(8,128)(2,1)S(1)}, bf16[256,256]{1,0:T(8,128)(2,1)}, u32[]{:S(2)}) copy-start(bf16[256,256]{1,0:T(8,128)(2,1)} %copy-done.13) | copy-start | bytes 393220
  25.8 6.5 %copy-start.15 = (bf16[256,256]{1,0:T(8,128)(2,1)S(1)}, bf16[256,256]{1,0:T(8,128)(2,1)}, u32[]{:S(2)}) copy-start(bf16[256,256]{1,0:T(8,128)(2,1)} %get-tuple-element.12) | copy-start | bytes 393220
  33.1 10.9 %copy-start.4 = (f32[2,2]{1,0:T(2,128)S(1)}, f32[2,2]{1,0:T(2,128)}, u32[]{:S(2)}) copy-start(f32[2,2]{1,0:T(2,128)} %bias_ref.1) | copy-start | bytes 52
  42.1 1.9 %copy-start.1 = (bf16[512,512]{1,0:T(8,128)(2,1)S(1)}, bf16[512,512]{1,0:T(8,128)(2,1)}, u32[]{:S(2)}) copy-start(bf16[512,512]{1,0:T(8,128)(2,1)} %get-tuple-element.24.rf_ref) | copy-start | bytes 1572868
  42.1 1.9 %copy-start.2 = (bf16[512,128]{1,0:T(8,128)(2,1)S(1)}, bf16[512,128]{1,0:T(8,128)(2,1)}, u32[]{:S(2)}) copy-start(bf16[512,128]{1,0:T(8,128)(2,1)} %fusion.7.lf_ref) | copy-start | bytes 393220
  42.1 1.9 %copy-start.3 = (bf16[128,512]{1,0:T(8,128)(2,1)S(1)}, bf16[128,512]{1,0:T(8,128)(2,1)}, u32[]{:S(2)}) copy-start(bf16[128,512]{1,0:T(8,128)(2,1)} %pad_maximum_fusion.1.li_ref) | copy-start | bytes 393220

commit v3 on v2

--- a/solution.py
+++ b/solution.py
@@ -101,20 +101,52 @@
     return (back * scale + bias * signal).astype(jnp.bfloat16)
 
 
-def chain_kernel(short_ref, spec_ref, bias_ref, lf_ref, rf_ref, ri_ref, li_ref, twr_ref, twi_ref, out_ref):
+def shift_tables():
+    big_r = lax.broadcasted_iota(jnp.int32, (2 * SIDE, 2 * SIDE), 0)
+    big_c = lax.broadcasted_iota(jnp.int32, (2 * SIDE, 2 * SIDE), 1)
+    small_r = lax.broadcasted_iota(jnp.int32, (SIDE // 2, SIDE // 2), 0)
+    small_c = lax.broadcasted_iota(jnp.int32, (SIDE // 2, SIDE // 2), 1)
+    big_r, big_c, small_r, small_c = lax.optimization_barrier((big_r, big_c, small_r, small_c))
+    upper = big_r < SIDE
+    source = jnp.where(upper, big_r, big_r - 2 * SIDE)
+    lag = jnp.where(big_c < SIDE, 1, 2)
+    target = jnp.where(big_c < SIDE, big_c, big_c - SIDE)
+    shifts = (source + lag == target).astype(jnp.bfloat16)
+    rows = (small_c + 1 == small_r).astype(jnp.bfloat16)
+    return shifts, rows
+
+
+def chain_kernel(
+    proj_ref, spec_ref, bias_ref, taps_ref, sh_ref, rw_ref,
+    lf_ref, rf_ref, ri_ref, li_ref, twr_ref, twi_ref, out_ref,
+):
     channel = pl.program_id(0)
     tabs = (lf_ref[...], rf_ref[...], ri_ref[...], li_ref[...], twr_ref[...], twi_ref[...])
-    state = short_ref[2, 0]
+    streams = []
+    for stream in range(3):
+        p = proj_ref[stream, 0]
+        q = jnp.dot(rw_ref[...], p, preferred_element_type=jnp.float32).astype(jnp.bfloat16)
+        moved = jnp.dot(
+            jnp.concatenate([p, q], 1), sh_ref[...], preferred_element_type=jnp.float32
+        )
+        short = (
+            taps_ref[stream, channel] * p.astype(jnp.float32)
+            + taps_ref[3 + stream, channel] * moved[:, :SIDE]
+            + taps_ref[6 + stream, channel] * moved[:, SIDE:]
+        )
+        streams.append(short.astype(jnp.bfloat16))
+    state = streams[2]
     for order in range(2):
         conv = convolve(state, spec_ref[order, 0], bias_ref[order, channel], tabs)
-        state = (short_ref[order, 0].astype(jnp.float32) * conv.astype(jnp.float32)).astype(jnp.bfloat16)
+        state = (streams[order].astype(jnp.float32) * conv.astype(jnp.float32)).astype(jnp.bfloat16)
     out_ref[0] = state
 
 
-def chain(short, spectra, bias, tabs):
-    per = short.shape[1]
+def chain(proj, spectra, bias, taps, tabs):
+    per = proj.shape[1]
     half = SIDE // 2
     left_fwd, right_fwd, right_inv, left_inv, tw_re, tw_im = tabs
+    shifts, rows = shift_tables()
     low = lambda t: t.astype(jnp.bfloat16)
     full = lambda shape: pl.BlockSpec(shape, lambda c: (0,) * len(shape))
     return pl.pallas_call(
@@ -124,6 +156,9 @@
             pl.BlockSpec((3, 1, half, SIDE), lambda c: (0, c, 0, 0)),
             pl.BlockSpec((2, 1, SIDE, 2 * SIDE), lambda c: (0, c, 0, 0)),
             pl.BlockSpec(memory_space=pltpu.SMEM),
+            pl.BlockSpec(memory_space=pltpu.SMEM),
+            full((2 * SIDE, 2 * SIDE)),
+            full((half, half)),
             full((2 * SIDE, half)),
             full((2 * SIDE, 2 * SIDE)),
             full((2 * SIDE, 2 * SIDE)),
@@ -134,7 +169,10 @@
         out_specs=pl.BlockSpec((1, half, SIDE), lambda c: (c, 0, 0)),
         out_shape=jax.ShapeDtypeStruct((per, half, SIDE), jnp.bfloat16),
         compiler_params=pltpu.CompilerParams(vmem_limit_bytes=48 * 1024 * 1024),
-    )(short, spectra, bias, low(left_fwd), low(right_fwd), low(right_inv), low(left_inv), tw_re, tw_im)
+    )(
+        proj, spectra, bias, taps, shifts, rows,
+        low(left_fwd), low(right_fwd), low(right_inv), low(left_inv), tw_re, tw_im,
+    )
 
 
 def local(layer_input, w_in, short_w, filters, filter_bias, w_out):
@@ -145,29 +183,22 @@
         w_in, layer_input, (((0,), (1,)), ((), ())), preferred_element_type=jnp.float32
     ).astype(jnp.bfloat16)
     positions = projected.shape[1]
-    grouped = jnp.swapaxes(projected.reshape(3, groups, per, positions), 0, 1)
     tabs = make_tables()
     spectra = filter_spectra(filters.reshape(2, per, SIDE // 2, SIDE), tabs)
+    grouped = jnp.swapaxes(projected.reshape(3, groups, per, positions), 0, 1)
     spread = lax.all_to_all(
-        grouped.reshape(groups, 3 * per, positions), "seq", split_axis=0, concat_axis=2, tiled=True
-    ).reshape(3 * per, groups * positions)
+        grouped.reshape(groups, 3 * per, positions), "seq", split_axis=0, concat_axis=0, tiled=True
+    )
+    spread = jnp.swapaxes(spread, 0, 1)
     me = lax.axis_index("seq")
-    taps = lax.dynamic_slice_in_dim(short_w.reshape(3, 3, groups, per), me, 1, axis=2)
-    taps = taps.reshape(3, 3 * per)
-    extended = jnp.pad(spread.astype(jnp.float32), ((0, 0), (2, 0)))
-    length = spread.shape[1]
-    short = (
-        taps[0][:, None] * extended[:, 2:]
-        + taps[1][:, None] * extended[:, 1 : length + 1]
-        + taps[2][:, None] * extended[:, :length]
-    ).astype(jnp.bfloat16)
-    half = SIDE // 2
+    taps = lax.dynamic_slice_in_dim(short_w.reshape(9, groups, per), me, 1, axis=1)
     state = chain(
-        short.reshape(3, per, half, SIDE),
+        spread.reshape(3, per, SIDE // 2, SIDE),
         spectra,
         filter_bias,
+        taps.reshape(9, per),
         tabs,
-    ).reshape(per, length)
+    ).reshape(per, groups * positions)
     returned = lax.all_to_all(state, "seq", split_axis=1, concat_axis=0, tiled=True)
     output = lax.dot_general(
         returned, w_out, (((0,), (0,)), ((), ())), preferred_element_type=jnp.float32

time: 69.5 us -> 87.1 us (1.25)
  local copies, waits for them, and re-layouts: 3.91 us -> 18.8 us
  waiting for transfers between devices: 8.97 us -> 0.01 us
  blocking collectives: 18.8 us -> 27.6 us
  other arithmetic: 7.75 us -> 9.11 us
  Pallas kernels: 9.41 us -> 10.7 us
    all_to_all x1, waiting for transfers between devices: 8.97 us -> 0.01 us  [local(): lax.all_to_all(grouped.reshape(groups, 3 * per, positions), 'seq', split_...]
    all_to_all x1, blocking collectives: 18.8 us -> 27.6 us  [local(): lax.all_to_all(state, 'seq', split_axis=1, concat_axis=0, tiled=True)]
    unnamed x37 -> x64, local copies, waits for them, and re-layouts: 1.14 us -> 9.62 us
    iota x0 -> x4, local copies, waits for them, and re-layouts: none -> 3.38 us  [the longest x1 1.1 us: shift_tables(): big_c = lax.broadcasted_iota(jnp.int32, (2 * SIDE, 2 * SIDE), 1)]
    pallas_call x1, Pallas kernels: 4.33 us -> 5.6 us  [chain(): pl.pallas_call(chain_kernel, grid=(per,), in_specs=[pl.BlockSpec((3, 1, h...]
    slice x2, local copies, waits for them, and re-layouts: 0.01 us -> 1.25 us  [make_tables(): left_inv = jnp.concatenate([f_re[:half], f_im[:half]], 1)]
    transpose x0 -> x1, local copies, waits for them, and re-layouts: none -> 1.12 us  [local(): spread = jnp.swapaxes(spread, 0, 1)]
  transfers between devices with their start and end apart: 1 -> 1, of which waited for: 1 -> 0; matrix products, arithmetic and copies ran while one was open for 11% -> 18% of each run, Pallas kernels for 7% -> 6%
where the time goes in v3:
time: 87.1 us; the launch traced here: 86.4 us
  blocking collectives  27.6 us (32%)
  local copies, waits for them, and re-layouts  18.8 us (22%)
  starting transfers between devices  16.8 us (19%)
  Pallas kernels  10.7 us (12%)
  other arithmetic  9.11 us (10%)
  matrix products  3 us (3%)
    all_to_all x1, blocking collectives, local(): lax.all_to_all(state, 'seq', split_axis=1, concat_axis=0, tiled=True)  27.6 us
    all_to_all x1, starting transfers between devices, local(): lax.all_to_all(grouped.reshape(groups, 3 * per, positions), 'seq', split_...  16.8 us
    unnamed x64, local copies, waits for them, and re-layouts  9.62 us
    pallas_call x1, Pallas kernels, chain(): pl.pallas_call(chain_kernel, grid=(per,), in_specs=[pl.BlockSpec((3, 1, h...  5.6 us
    pallas_call x1, Pallas kernels, filter_spectra(): pl.pallas_call(filter_kernel, grid=(orders, per), in_specs=[pl.BlockSpec(...  5.08 us
    sin x1, other arithmetic, make_tables(): jnp.sin(big)  2.62 us
    dot_general x1, matrix products, local(): lax.dot_general(returned, w_out, (((0,), (0,)), ((), ())), preferred_elem...  1.79 us
  transfers between devices with their start and end apart: 1, of which 0 were waited for; matrix products, arithmetic and copies ran while one was open for 18% of the time, Pallas kernels for 6%

profile of v3, /device:TPU:1, one launch (start us, length us, event | category | flops | bytes accessed | tf_op | source)
XLA Modules:
  0.0 86.4 jit_solution(2582899957162779649)
XLA Ops:
  0.0 0.0 copy-start
  0.0 1.0 %copy-done = bf16[256,768]{1,0:T(8,128)(2,1)S(1)} copy-done((bf16[256,768]{1,0:T(8,128)(2,1)S(1)}, bf16[256,768]{1,0:T(8,128)(2,1)}, u32[]{:S(2)}) %copy-start) | copy-done | bytes 393240
  1.0 1.2 %convolution_convert_fusion = bf16[768,256]{1,0:T(8,128)(2,1)S(1)} fusion(bf16[256,768]{1,0:T(8,128)(2,1)S(1)} %copy-done, bf16[256,256]{1,0:T(8,128)(2,1)} %param.6), kind=kOutput, calls=%fused_computation.3 | convolution fusion | flops 100859904 | bytes 917504 | tf_op jit(solution)/shard_map/dot_general | solution.py:182
  2.2 0.2 reshape.23
  2.4 1.0 %copy.20 = bf16[128,6,256]{2,1,0:T(8,128)(2,1)} copy(bf16[128,6,256]{2,0,1:T(8,128)(2,1)S(1)} %bitcast.12) | data formatting | bytes 786432 | tf_op jit(solution)/shard_map/reshape | solution.py:190
  3.4 16.8 %all-to-all-start = ((bf16[128,6,256]{2,1,0:T(8,128)(2,1)}), bf16[128,6,256]{2,1,0:T(8,128)(2,1)}, u32[]{:S(2)}, u32[]{:S(2)}) async-start(bf16[128,6,256]{2,1,0:T(8,128)(2,1)} %copy.20), calls=%async_computation | async-start | bytes 1048576 | tf_op jit(solution)/shard_map/all_to_all | solution.py:189
  20.4 1.6 %negate_convert_fusion = (bf16[256,256]{1,0:T(8,128)(2,1)}, f32[256,256]{1,0:T(8,128)S(1)}, s32[256,256]{1,0:T(8,128)S(1)}) fusion(s32[256,256]{1,0:T(8,128)S(1)} %iota.30, s32[256,256]{1,0:T(8,128)S(1)} %iota.31), kind=kLoop, calls=%fused_computation.26 | loop fusion | flops 1048576 | bytes 1179648 | tf_op jit(solution)/shard_map/convert.9
  22.0 0.0 copy-start.19
  22.0 0.0 copy-start.21
  22.1 0.0 copy-start.31
  22.1 2.6 %fusion.6 = (f32[256,256]{1,0:T(8,128)}, f32[256,256]{1,0:T(8,128)}, bf16[256,256]{1,0:T(8,128)(2,1)S(1)}, f32[256,256]{1,0:T(8,128)S(1)}) fusion(s32[256,256]{1,0:T(8,128)S(1)} %get-tuple-element.19), kind=kLoop, calls=%fused_computation.18 | loop fusion | flops 1048576 | bytes 1179648 | tf_op jit(solution)/shard_map/sin | solution.py:49
  24.7 0.7 pad_maximum_fusion.lf_ref
  25.4 0.7 fusion.11.lf_ref
  26.1 0.1 maximum_maximum_fusion.rf_ref
  26.2 0.0 copy-done.13
  26.2 0.0 copy-done.19
  26.2 0.0 copy-done.31
  26.2 0.5 reshape.27
  26.8 0.0 copy-done.26
  26.8 1.2 %reshape.26.filt_ref = f32[2,2,128,256]{3,2,1,0:T(8,128)} reshape(f32[2,2,32768]{2,1,0:T(2,128)S(1)} %copy-done.26) | data formatting | bytes 1048576 | tf_op jit(solution)/shard_map/reshape | solution.py:187
  28.1 0.0 copy-done.17
  28.1 0.0 copy-done.21
  28.1 0.6 slice.21
  28.7 0.0 copy-done.23
  28.7 0.6 slice.20
  29.3 1.0 %iota.32 = s32[512,512]{1,0:T(8,128)} iota(), iota_dimension=0 | iota | bytes 1048576 | tf_op jit(solution)/shard_map/iota | solution.py:105
  30.4 1.1 %iota.33 = s32[512,512]{1,0:T(8,128)} iota(), iota_dimension=1 | iota | bytes 1048576 | tf_op jit(solution)/shard_map/iota | solution.py:106
  31.5 0.6 iota.34
  32.1 0.6 iota.35
  32.7 0.1 copy.22
  32.8 0.1 copy.23.taps_ref
  32.9 0.9 %copy-done.1 = f32[256,256]{1,0:T(8,128)S(1)} copy-done((f32[256,256]{1,0:T(8,128)S(1)}, f32[256,256]{1,0:T(8,128)}, u32[]{:S(2)}) %copy-start.1) | copy-done | bytes 262168
  33.9 0.9 %copy-done.3 = f32[256,256]{1,0:T(8,128)S(1)} copy-done((f32[256,256]{1,0:T(8,128)S(1)}, f32[256,256]{1,0:T(8,128)}, u32[]{:S(2)}) %copy-start.3) | copy-done | bytes 262168
  34.8 1.0 %copy-done.5 = f32[2,2,128,256]{3,2,1,0:T(8,128)S(1)} copy-done((f32[2,2,128,256]{3,2,1,0:T(8,128)S(1)}, f32[2,2,128,256]{3,2,1,0:T(8,128)}, u32[]{:S(2)}) %copy-start.5) | copy-done | bytes 524312
  35.9 0.9 %copy-done.8 = f32[512,128]{1,0:T(8,128)S(1)} copy-done((f32[512,128]{1,0:T(8,128)S(1)}, f32[512,128]{1,0:T(8,128)}, u32[]{:S(2)}) %copy-start.8) | copy-done | bytes 262168
  36.8 0.0 copy-start.20
  36.8 0.0 copy-start.22
  36.8 0.0 copy-start.24
  36.9 0.0 copy-start.25
  36.9 5.1 %shard_map.64.spec_ref = f32[2,2,256,512]{3,2,1,0:T(8,128)S(1)} custom-call(f32[2,2,128,256]{3,2,1,0:T(8,128)S(1)} %copy-done.5, f32[512,128]{1,0:T(8,128)S(1)} %copy-done.8, f32[512,512]{1,0:T(8,128)S(1)} %maximum_maximum_fusion.rf_ref, f32[256,256]{1,0:T(8,128)S(1)} %copy-done.3, f32[256,256]{1,0:T(8,128)S(1)} %copy-done.1), custom_call_target="tpu_custom_call" | custom-call | tf_op jit(solution)/shard_map/pallas_call | solution.py:71
  42.0 0.0 copy-done.29
  42.0 0.0 copy-done.30
  42.0 0.0 copy-start.27
  42.0 0.7 pad_maximum_fusion.1.li_ref
  42.7 0.0 copy-done.14
  42.7 0.0 copy-done.24
  42.7 0.0 copy-done.25
  42.7 0.9 %maximum_maximum_fusion.1 = (bf16[512,512]{1,0:T(8,128)(2,1)S(1)}, bf16[512,512]{1,0:T(8,128)(2,1)}) fusion(bf16[256,256]{1,0:T(8,128)(2,1)S(1)} %copy-done.24, bf16[256,256]{1,0:T(8,128)(2,1)S(1)} %copy-done.22, bf16[256,256]{1,0:T(8,128)(2,1)S(1)} %copy-done.25, f32[256,256]{1,0:T(8,128)S(1)} %copy-done.18, f32[256,256]{1,0:T(8,128)S(1)} %copy-done.20, ...), kind=kLoop, calls=%fused_computation.9 | loop fusion | flops 4194304 | bytes 2228224 | tf_op jit(solution)/shard_map/concatenate | solution.py:45
  43.6 0.0 copy-done.28
  43.6 0.0 copy-start.12
  43.6 0.6 fusion.8.rw_ref
  44.3 1.2 %fusion.2.sh_ref = bf16[512,512]{1,0:T(8,128)(2,1)} fusion(s32[512,512]{1,0:T(8,128)S(1)} %copy-done.16, s32[512,512]{1,0:T(8,128)S(1)} %copy-done.15), kind=kLoop, calls=%fused_computation.8 | loop fusion | flops 2621440 | bytes 2621440 | tf_op jit(solution)/shard_map/convert_element_type | solution.py:114
  45.4 0.0 all-to-all-done
  45.4 1.1 %copy.21 = bf16[6,128,256]{2,1,0:T(8,128)(2,1)S(1)} copy(bf16[6,128,256]{2,0,1:T(8,128)(2,1)} %bitcast.2) | data formatting | bytes 786432 | tf_op jit(solution)/shard_map/transpose | solution.py:192
  46.6 1.0 %copy-done.6 = bf16[512,512]{1,0:T(8,128)(2,1)S(1)} copy-done((bf16[512,512]{1,0:T(8,128)(2,1)S(1)}, bf16[512,512]{1,0:T(8,128)(2,1)}, u32[]{:S(2)}) %copy-start.6) | copy-done | bytes 524312
  47.6 1.0 %copy-done.7 = bf16[512,512]{1,0:T(8,128)(2,1)S(1)} copy-done((bf16[512,512]{1,0:T(8,128)(2,1)S(1)}, bf16[512,512]{1,0:T(8,128)(2,1)}, u32[]{:S(2)}) %copy-start.7) | copy-done | bytes 524312
  48.6 0.9 %copy-done.9 = bf16[512,128]{1,0:T(8,128)(2,1)S(1)} copy-done((bf16[512,128]{1,0:T(8,128)(2,1)S(1)}, bf16[512,128]{1,0:T(8,128)(2,1)}, u32[]{:S(2)}) %copy-start.9) | copy-done | bytes 131096
  49.6 0.9 %copy-done.10 = bf16[128,512]{1,0:T(8,128)(2,1)S(1)} copy-done((bf16[128,512]{1,0:T(8,128)(2,1)S(1)}, bf16[128,512]{1,0:T(8,128)(2,1)}, u32[]{:S(2)}) %copy-start.10) | copy-done | bytes 131096
  50.5 0.8 copy-done.11
  51.2 5.6 %shard_map.65 = bf16[2,128,256]{2,1,0:T(8,128)(2,1)S(1)} custom-call(bf16[3,2,128,256]{3,2,1,0:T(8,128)(2,1)S(1)} %bitcast.11, f32[2,2,256,512]{3,2,1,0:T(8,128)S(1)} %shard_map.64.spec_ref, f32[2,2]{1,0:T(2,128)S(1)} %copy-done.12, f32[9,2]{1,0:T(8,128)S(1)} %copy.23.taps_ref, bf16[512,512]{1,0:T(8,128)(2,1)S(1)} %copy-done.7, ...), custom_call_target="tpu_custom_call" | custom-call | tf_op jit(solution)/shard_map/pallas_call | solution.py:152
  56.8 0.1 copy.24
  57.0 27.6 %all_to_all.21 = bf16[2,128,256]{2,0,1:T(2,128)(2,1)S(1)} all-to-all(bf16[2,128,256]{2,0,1:T(2,128)(2,1)S(1)} %copy.24), channel_id=1, replica_groups=mesh['win'=2,'seq'=128] {'seq'}, dimensions={1} | all-to-all | bytes 262144 | tf_op jit(solution)/shard_map/all_to_all | solution.py:202
  84.6 0.1 all_to_all.18
  84.7 1.8 %convolution_convert_fusion.1 = bf16[256,256]{1,0:T(8,128)(2,1)} fusion(bf16[256,256]{1,0:T(8,128)(2,1)S(1)} %all_to_all.18, bf16[256,256]{1,0:T(8,128)(2,1)} %param.11), kind=kOutput, calls=%fused_computation.4 | convolution fusion | flops 33619968 | bytes 393216 | tf_op jit(solution)/shard_map/dot_general | solution.py:203
  (38 shorter events, 0.2 us)
Async XLA Ops:
  0.0 1.0 %copy-start = (bf16[256,768]{1,0:T(8,128)(2,1)S(1)}, bf16[256,768]{1,0:T(8,128)(2,1)}, u32[]{:S(2)}) copy-start(bf16[256,768]{1,0:T(8,128)(2,1)} %param.7) | copy-start | bytes 1179652
  3.4 42.0 %all-to-all-start = ((bf16[128,6,256]{2,1,0:T(8,128)(2,1)}), bf16[128,6,256]{2,1,0:T(8,128)(2,1)}, u32[]{:S(2)}, u32[]{:S(2)}) async-start(bf16[128,6,256]{2,1,0:T(8,128)(2,1)} %copy.20), calls=%async_computation | async-start | bytes 1048576 | tf_op jit(solution)/shard_map/all_to_all | solution.py:189
  22.0 4.2 %copy-start.13 = (f32[256,256]{1,0:T(8,128)}, f32[256,256]{1,0:T(8,128)S(1)}, u32[]{:S(2)}) copy-start(f32[256,256]{1,0:T(8,128)S(1)} %get-tuple-element.18) | copy-start | bytes 786436
  22.0 4.2 %copy-start.19 = (f32[256,256]{1,0:T(8,128)}, f32[256,256]{1,0:T(8,128)S(1)}, u32[]{:S(2)}) copy-start(f32[256,256]{1,0:T(8,128)S(1)} %get-tuple-element.23) | copy-start | bytes 786436
  22.0 6.1 %copy-start.21 = (bf16[256,256]{1,0:T(8,128)(2,1)}, bf16[256,256]{1,0:T(8,128)(2,1)S(1)}, u32[]{:S(2)}) copy-start(bf16[256,256]{1,0:T(8,128)(2,1)S(1)} %get-tuple-element.22) | copy-start | bytes 393220
  22.1 4.2 %copy-start.31 = (f32[3,768]{1,0:T(4,128)S(1)}, f32[3,768]{1,0:T(4,128)}, u32[]{:S(2)}) copy-start(f32[3,768]{1,0:T(4,128)} %param.8) | copy-start | bytes 27652
  24.7 3.4 %copy-start.17 = (f32[256,256]{1,0:T(8,128)}, f32[256,256]{1,0:T(8,128)S(1)}, u32[]{:S(2)}) copy-start(f32[256,256]{1,0:T(8,128)S(1)} %get-tuple-element.27) | copy-start | bytes 786436
  24.7 4.0 %copy-start.23 = (bf16[256,256]{1,0:T(8,128)(2,1)}, bf16[256,256]{1,0:T(8,128)(2,1)S(1)}, u32[]{:S(2)}) copy-start(bf16[256,256]{1,0:T(8,128)(2,1)S(1)} %get-tuple-element.26) | copy-start | bytes 393220
  24.7 2.1 %copy-start.26 = (f32[2,2,32768]{2,1,0:T(2,128)S(1)}, f32[2,2,32768]{2,1,0:T(2,128)}, u32[]{:S(2)}) copy-start(f32[2,2,32768]{2,1,0:T(2,128)} %param.9) | copy-start | bytes 1572868
  32.9 0.9 %copy-start.1 = (f32[256,256]{1,0:T(8,128)S(1)}, f32[256,256]{1,0:T(8,128)}, u32[]{:S(2)}) copy-start(f32[256,256]{1,0:T(8,128)} %get-tuple-element.24.twi_ref) | copy-start | bytes 786436
  33.9 0.9 %copy-start.3 = (f32[256,256]{1,0:T(8,128)S(1)}, f32[256,256]{1,0:T(8,128)}, u32[]{:S(2)}) copy-start(f32[256,256]{1,0:T(8,128)} %get-tuple-element.25.twr_ref) | copy-start | bytes 786436
  34.8 1.0 %copy-start.5 = (f32[2,2,128,256]{3,2,1,0:T(8,128)S(1)}, f32[2,2,128,256]{3,2,1,0:T(8,128)}, u32[]{:S(2)}) copy-start(f32[2,2,128,256]{3,2,1,0:T(8,128)} %reshape.26.filt_ref) | copy-start | bytes 1572868
  35.9 0.9 %copy-start.8 = (f32[512,128]{1,0:T(8,128)S(1)}, f32[512,128]{1,0:T(8,128)}, u32[]{:S(2)}) copy-start(f32[512,128]{1,0:T(8,128)} %pad_maximum_fusion.lf_ref) | copy-start | bytes 786436
  36.8 5.1 %copy-start.29 = (bf16[128,256]{1,0:T(8,128)(2,1)S(1)}, bf16[128,256]{1,0:T(8,128)(2,1)}, u32[]{:S(2)}) copy-start(bf16[128,256]{1,0:T(8,128)(2,1)} %slice.21) | copy-start | bytes 196612
  36.8 5.2 %copy-start.30 = (bf16[128,256]{1,0:T(8,128)(2,1)S(1)}, bf16[128,256]{1,0:T(8,128)(2,1)}, u32[]{:S(2)}) copy-start(bf16[128,256]{1,0:T(8,128)(2,1)} %slice.20) | copy-start | bytes 196612
  36.8 5.9 %copy-start.14 = (f32[256,256]{1,0:T(8,128)S(1)}, f32[256,256]{1,0:T(8,128)}, u32[]{:S(2)}) copy-start(f32[256,256]{1,0:T(8,128)} %copy-done.13) | copy-start | bytes 786436
  36.8 5.9 %copy-start.18 = (f32[256,256]{1,0:T(8,128)S(1)}, f32[256,256]{1,0:T(8,128)}, u32[]{:S(2)}) copy-start(f32[256,256]{1,0:T(8,128)} %copy-done.17) | copy-start | bytes 786436
  36.8 5.9 %copy-start.20 = (f32[256,256]{1,0:T(8,128)S(1)}, f32[256,256]{1,0:T(8,128)}, u32[]{:S(2)}) copy-start(f32[256,256]{1,0:T(8,128)} %copy-done.19) | copy-start | bytes 786436
  36.8 5.9 %copy-start.22 = (bf16[256,256]{1,0:T(8,128)(2,1)S(1)}, bf16[256,256]{1,0:T(8,128)(2,1)}, u32[]{:S(2)}) copy-start(bf16[256,256]{1,0:T(8,128)(2,1)} %copy-done.21) | copy-start | bytes 393220
  36.8 5.8 %copy-start.24 = (bf16[256,256]{1,0:T(8,128)(2,1)S(1)}, bf16[256,256]{1,0:T(8,128)(2,1)}, u32[]{:S(2)}) copy-start(bf16[256,256]{1,0:T(8,128)(2,1)} %copy-done.23) | copy-start | bytes 393220
  36.9 5.8 %copy-start.25 = (bf16[256,256]{1,0:T(8,128)(2,1)S(1)}, bf16[256,256]{1,0:T(8,128)(2,1)}, u32[]{:S(2)}) copy-start(bf16[256,256]{1,0:T(8,128)(2,1)} %get-tuple-element.17) | copy-start | bytes 393220
  42.0 1.6 %copy-start.27 = (s32[128,128]{1,0:T(8,128)S(1)}, s32[128,128]{1,0:T(8,128)}, u32[]{:S(2)}) copy-start(s32[128,128]{1,0:T(8,128)} %iota.34) | copy-start | bytes 196612
  42.0 1.6 %copy-start.28 = (s32[128,128]{1,0:T(8,128)S(1)}, s32[128,128]{1,0:T(8,128)}, u32[]{:S(2)}) copy-start(s32[128,128]{1,0:T(8,128)} %iota.35) | copy-start | bytes 196612
  42.0 2.3 %copy-start.15 = (s32[512,512]{1,0:T(8,128)S(1)}, s32[512,512]{1,0:T(8,128)}, u32[]{:S(2)}) copy-start(s32[512,512]{1,0:T(8,128)} %iota.32) | copy-start | bytes 3145732
  42.0 2.2 %copy-start.16 = (s32[512,512]{1,0:T(8,128)S(1)}, s32[512,512]{1,0:T(8,128)}, u32[]{:S(2)}) copy-start(s32[512,512]{1,0:T(8,128)} %iota.33) | copy-start | bytes 3145732
  43.6 2.9 %copy-start.2 = (f32[256,256]{1,0:T(8,128)S(1)}, f32[256,256]{1,0:T(8,128)}, u32[]{:S(2)}) copy-start(f32[256,256]{1,0:T(8,128)} %get-tuple-element.24.twi_ref) | copy-start | bytes 786436
  43.6 2.9 %copy-start.4 = (f32[256,256]{1,0:T(8,128)S(1)}, f32[256,256]{1,0:T(8,128)}, u32[]{:S(2)}) copy-start(f32[256,256]{1,0:T(8,128)} %get-tuple-element.25.twr_ref) | copy-start | bytes 786436
  43.6 2.9 %copy-start.12 = (f32[2,2]{1,0:T(2,128)S(1)}, f32[2,2]{1,0:T(2,128)}, u32[]{:S(2)}) copy-start(f32[2,2]{1,0:T(2,128)} %bias_ref.1) | copy-start | bytes 52
  46.6 1.0 %copy-start.6 = (bf16[512,512]{1,0:T(8,128)(2,1)S(1)}, bf16[512,512]{1,0:T(8,128)(2,1)}, u32[]{:S(2)}) copy-start(bf16[512,512]{1,0:T(8,128)(2,1)} %get-tuple-element.29.rf_ref) | copy-start | bytes 1572868
  47.6 1.0 %copy-start.7 = (bf16[512,512]{1,0:T(8,128)(2,1)S(1)}, bf16[512,512]{1,0:T(8,128)(2,1)}, u32[]{:S(2)}) copy-start(bf16[512,512]{1,0:T(8,128)(2,1)} %fusion.2.sh_ref) | copy-start | bytes 1572868
  48.6 0.9 %copy-start.9 = (bf16[512,128]{1,0:T(8,128)(2,1)S(1)}, bf16[512,128]{1,0:T(8,128)(2,1)}, u32[]{:S(2)}) copy-start(bf16[512,128]{1,0:T(8,128)(2,1)} %fusion.11.lf_ref) | copy-start | bytes 393220
  49.5 0.9 %copy-start.10 = (bf16[128,512]{1,0:T(8,128)(2,1)S(1)}, bf16[128,512]{1,0:T(8,128)(2,1)}, u32[]{:S(2)}) copy-start(bf16[128,512]{1,0:T(8,128)(2,1)} %pad_maximum_fusion.1.li_ref) | copy-start | bytes 393220
  50.5 0.8 copy-start.11

commit v4 on v2

--- a/solution.py
+++ b/solution.py
@@ -137,21 +137,48 @@
     )(short, spectra, bias, low(left_fwd), low(right_fwd), low(right_inv), low(left_inv), tw_re, tw_im)
 
 
+SEQ = ("g", "core")
+
+
+def spread_out(grouped):
+    chips, cores = lax.axis_size("g"), lax.axis_size("core")
+    y = grouped.reshape((chips, cores) + grouped.shape[1:])
+    first = lax.axis_index("core") == 0
+    keep = jnp.where(first, y[:, 0], y[:, 1])
+    give = jnp.where(first, y[:, 1], y[:, 0])
+    got = lax.ppermute(give, "core", [(0, 1), (1, 0)])
+    z = jnp.stack([jnp.where(first, keep, got), jnp.where(first, got, keep)], 1)
+    z = lax.all_to_all(z, "g", split_axis=0, concat_axis=0, tiled=True)
+    return z.reshape(grouped.shape)
+
+
+def bring_back(state):
+    chips, cores = lax.axis_size("g"), lax.axis_size("core")
+    per, length = state.shape
+    s = jnp.transpose(state.reshape(per, chips, cores, length // (chips * cores)), (1, 2, 0, 3))
+    r = lax.all_to_all(s, "g", split_axis=0, concat_axis=0, tiled=True)
+    first = lax.axis_index("core") == 0
+    keep = jnp.where(first, r[:, 0], r[:, 1])
+    give = jnp.where(first, r[:, 1], r[:, 0])
+    got = lax.ppermute(give, "core", [(0, 1), (1, 0)])
+    z = jnp.stack([jnp.where(first, keep, got), jnp.where(first, got, keep)], 1)
+    return z.reshape(chips * cores * per, length // (chips * cores))
+
+
 def local(layer_input, w_in, short_w, filters, filter_bias, w_out):
     width = w_out.shape[0]
-    groups = lax.axis_size("seq")
+    groups = lax.axis_size("g") * lax.axis_size("core")
     per = width // groups
     projected = lax.dot_general(
         w_in, layer_input, (((0,), (1,)), ((), ())), preferred_element_type=jnp.float32
     ).astype(jnp.bfloat16)
     positions = projected.shape[1]
-    grouped = jnp.swapaxes(projected.reshape(3, groups, per, positions), 0, 1)
     tabs = make_tables()
     spectra = filter_spectra(filters.reshape(2, per, SIDE // 2, SIDE), tabs)
-    spread = lax.all_to_all(
-        grouped.reshape(groups, 3 * per, positions), "seq", split_axis=0, concat_axis=2, tiled=True
-    ).reshape(3 * per, groups * positions)
-    me = lax.axis_index("seq")
+    grouped = jnp.swapaxes(projected.reshape(3, groups, per, positions), 0, 1)
+    spread = spread_out(grouped.reshape(groups, 3 * per, positions))
+    spread = jnp.swapaxes(spread, 0, 1).reshape(3 * per, groups * positions)
+    me = lax.axis_index("g") * lax.axis_size("core") + lax.axis_index("core")
     taps = lax.dynamic_slice_in_dim(short_w.reshape(3, 3, groups, per), me, 1, axis=2)
     taps = taps.reshape(3, 3 * per)
     extended = jnp.pad(spread.astype(jnp.float32), ((0, 0), (2, 0)))
@@ -168,7 +195,7 @@
         filter_bias,
         tabs,
     ).reshape(per, length)
-    returned = lax.all_to_all(state, "seq", split_axis=1, concat_axis=0, tiled=True)
+    returned = bring_back(state)
     output = lax.dot_general(
         returned, w_out, (((0,), (0,)), ((), ())), preferred_element_type=jnp.float32
     )
@@ -176,10 +203,13 @@
 
 
 def solution(mesh):
+    wins, seqs = mesh.devices.shape
+    view = jax.sharding.Mesh(mesh.devices.reshape(wins, seqs // 2, 2), ("win",) + SEQ)
+    rows = ("win",) + SEQ
     return jax.shard_map(
         local,
-        mesh=mesh,
-        in_specs=(P(("win", "seq"), None), P(), P(), P(None, "seq", None), P(None, "seq"), P()),
-        out_specs=P(("win", "seq"), None),
+        mesh=view,
+        in_specs=(P(rows, None), P(), P(), P(None, SEQ, None), P(None, SEQ), P()),
+        out_specs=P(rows, None),
         check_vma=False,
     )

time: 69.5 us -> 75.7 us (1.089)
  local copies, waits for them, and re-layouts: 3.91 us -> 11.6 us
  waiting for transfers between devices: 8.97 us -> 6.64 us
  starting transfers between devices: 17 us -> 18.8 us
  blocking collectives: 18.8 us -> 17.7 us
  other arithmetic: 7.75 us -> 8.67 us
  matrix products: 3 us -> 2.09 us
    ppermute x0 -> x2, starting transfers between devices: none -> 5.97 us  [the longest x1 3.29 us: spread_out(): got = lax.ppermute(give, 'core', [(0, 1), (1, 0)])]
    all_to_all x1, starting transfers between devices: 17 us -> 12.8 us  [spread_out(): z = lax.all_to_all(z, 'g', split_axis=0, concat_axis=0, tiled=True)]
    convert_element_type x0 -> x2, local copies, waits for them, and re-layouts: none -> 4.08 us  [local(): extended = jnp.pad(spread.astype(jnp.float32), ((0, 0), (2, 0)))]
    all_to_all x1, waiting for transfers between devices: 8.97 us -> 5.73 us  [spread_out(): z = lax.all_to_all(z, 'g', split_axis=0, concat_axis=0, tiled=True)]
    unnamed x37 -> x39, local copies, waits for them, and re-layouts: 1.14 us -> 3.58 us
    another operation x0 -> x4, local copies, waits for them, and re-layouts: none -> 1.58 us  [the longest x1 1.16 us: spread_out(): z = jnp.stack([jnp.where(first, keep, got), jnp.where(first, got, keep)], 1)]
    all_to_all x1, blocking collectives: 18.8 us -> 17.7 us  [bring_back(): r = lax.all_to_all(s, 'g', split_axis=0, concat_axis=0, tiled=True)]
    reshape x1, local copies, waits for them, and re-layouts: 1.02 us -> 0.06 us  [bring_back(): return z.reshape(chips * cores * per, length // (chips * cores))]
  transfers between devices with their start and end apart: 1 -> 3, of which waited for: 1 -> 2; matrix products, arithmetic and copies ran while one was open for 11% -> 11% of each run, Pallas kernels for 7% -> 7%
where the time goes in v4:
time: 75.7 us; the launch traced here: 75.3 us
  starting transfers between devices  18.8 us (25%)
  blocking collectives  17.7 us (23%)
  local copies, waits for them, and re-layouts  11.6 us (15%)
  Pallas kernels  9.41 us (12%)
  other arithmetic  8.67 us (11%)
  waiting for transfers between devices  6.64 us (9%)
  matrix products  2.09 us (3%)
    all_to_all x1, blocking collectives, bring_back(): r = lax.all_to_all(s, 'g', split_axis=0, concat_axis=0, tiled=True)  17.7 us
    all_to_all x1, starting transfers between devices, spread_out(): z = lax.all_to_all(z, 'g', split_axis=0, concat_axis=0, tiled=True)  12.8 us
    all_to_all x1, waiting for transfers between devices, spread_out(): z = lax.all_to_all(z, 'g', split_axis=0, concat_axis=0, tiled=True)  5.73 us
    pallas_call x1, Pallas kernels, filter_spectra(): pl.pallas_call(filter_kernel, grid=(orders, per), in_specs=[pl.BlockSpec(...  5.08 us
    pallas_call x1, Pallas kernels, chain(): pl.pallas_call(chain_kernel, grid=(per,), in_specs=[pl.BlockSpec((3, 1, h...  4.33 us
    convert_element_type x2, local copies, waits for them, and re-layouts, local(): extended = jnp.pad(spread.astype(jnp.float32), ((0, 0), (2, 0)))  4.08 us
    unnamed x39, local copies, waits for them, and re-layouts  3.58 us
    ppermute x1, starting transfers between devices, spread_out(): got = lax.ppermute(give, 'core', [(0, 1), (1, 0)])  3.29 us
  transfers between devices with their start and end apart: 3, of which 2 were waited for; matrix products, arithmetic and copies ran while one was open for 11% of the time, Pallas kernels for 7%

profile of v4, /device:TPU:1, one launch (start us, length us, event | category | flops | bytes accessed | tf_op | source)
XLA Modules:
  0.0 75.3 jit_solution(8808570091621362154)
XLA Ops:
  0.0 0.0 copy-start
  0.0 1.0 %copy-done = bf16[256,768]{1,0:T(8,128)(2,1)S(1)} copy-done((bf16[256,768]{1,0:T(8,128)(2,1)S(1)}, bf16[256,768]{1,0:T(8,128)(2,1)}, u32[]{:S(2)}) %copy-start) | copy-done | bytes 393240
  1.0 1.2 %convolution_convert_fusion = bf16[768,256]{1,0:T(8,128)(2,1)S(1)} fusion(bf16[256,768]{1,0:T(8,128)(2,1)S(1)} %copy-done, bf16[256,256]{1,0:T(8,128)(2,1)} %param.6), kind=kOutput, calls=%fused_computation | convolution fusion | flops 100859904 | bytes 917504 | tf_op jit(solution)/shard_map/dot_general | solution.py:172
  2.2 0.2 reshape.40
  2.4 0.2 reshape_reshape.6
  2.6 0.0 copy-start.14
  2.6 0.9 %broadcast_select_fusion.1 = (bf16[64,1,6,256]{3,1,0,2:T(2,128)(2,1)S(1)}, bf16[64,1,6,256]{3,1,0,2:T(2,128)(2,1)S(1)}) fusion(pred[]{:T(512)S(6)} %eq.6, bf16[64,2,6,256]{3,1,0,2:T(2,128)(2,1)S(1)} %reshape_reshape.6), kind=kLoop, calls=%fused_computation.5 | loop fusion | flops 196608 | bytes 786433 | tf_op jit(solution)/shard_map/jit(_where)/select_n | solution.py:147
  3.5 0.0 copy-start.17
  3.6 3.3 %collective-permute-start = (bf16[64,6,256]{2,0,1:T(8,128)(2,1)S(1)}, bf16[64,6,256]{2,0,1:T(8,128)(2,1)S(1)}, u32[]{:S(2)}, u32[]{:S(2)}) collective-permute-start(bf16[64,6,256]{2,0,1:T(8,128)(2,1)S(1)} %bitcast.55), channel_id=1, source_target_pairs={{0,1},{1,0},{2,3},{3,2},{4,5},{5,4},{6,7},{7,6},{8,9},{9,8},{10,11... | collective-permute-start | bytes 589832 | tf_op jit(solution)/shard_map/ppermute | solution.py:149
  6.9 1.6 %negate_convert_fusion = (bf16[256,256]{1,0:T(8,128)(2,1)}, f32[256,256]{1,0:T(8,128)S(1)}, s32[256,256]{1,0:T(8,128)S(1)}) fusion(s32[256,256]{1,0:T(8,128)S(1)} %iota.10, s32[256,256]{1,0:T(8,128)S(1)} %iota.11), kind=kLoop, calls=%fused_computation.38 | loop fusion | flops 1048576 | bytes 1179648 | tf_op jit(solution)/shard_map/convert.12
  8.6 0.0 copy-start.9
  8.6 0.0 copy-start.11
  8.6 0.0 copy-start.7
  8.6 0.7 copy-done.11
  9.4 0.6 slice.67
  10.0 0.0 copy-done.14
  10.0 0.5 reshape.42.filt_ref
  10.4 0.0 copy-done.17
  10.5 0.5 reshape.39
  11.0 0.1 mul.50
  11.1 0.1 mul.53
  11.2 0.1 mul.56
  11.3 0.0 collective-permute-done
  11.4 1.2 %copy.43 = bf16[64,2,6,256]{3,1,2,0:T(2,128)(2,1)} copy(bf16[64,2,6,256]{3,0,2,1:T(8,128)(2,1)S(1)} %pad_maximum_fusion) | data formatting | bytes 786432 | tf_op jit(solution)/shard_map/stack | solution.py:150
  12.5 12.8 %all-to-all-start = ((bf16[64,2,6,256]{3,1,2,0:T(2,128)(2,1)}), bf16[64,2,6,256]{3,1,2,0:T(2,128)(2,1)}, u32[]{:S(2)}, u32[]{:S(2)}) async-start(bf16[64,2,6,256]{3,1,2,0:T(2,128)(2,1)} %copy.43), calls=%async_computation | async-start | bytes 786432 | tf_op jit(solution)/shard_map/all_to_all | solution.py:151
  25.4 1.9 %fusion.3 = (f32[256,256]{1,0:T(8,128)S(1)}, f32[256,256]{1,0:T(8,128)S(1)}, bf16[256,256]{1,0:T(8,128)(2,1)S(1)}, f32[256,256]{1,0:T(8,128)S(1)}) fusion(s32[256,256]{1,0:T(8,128)S(1)} %get-tuple-element.14), kind=kLoop, calls=%fused_computation.18 | loop fusion | flops 1048576 | bytes 1179648 | tf_op jit(solution)/shard_map/sin | solution.py:49
  27.3 0.0 copy-done.9
  27.4 0.0 copy-done.5
  27.4 0.0 copy-done.7
  27.4 0.1 maximum_maximum_fusion.rf_ref
  27.5 0.0 copy-start.10
  27.5 0.0 copy-start.15
  27.5 0.0 copy-start.6
  27.5 0.0 copy-start.8
  27.5 0.0 copy-start.12
  27.5 0.0 copy-start.13
  27.6 5.1 %shard_map.64.spec_ref = f32[2,2,256,512]{3,2,1,0:T(8,128)S(1)} custom-call(f32[2,2,128,256]{3,2,1,0:T(8,128)S(1)} %reshape.42.filt_ref, f32[512,128]{1,0:T(8,128)S(1)} %pad_maximum_fusion.1.lf_ref, f32[512,512]{1,0:T(8,128)S(1)} %maximum_maximum_fusion.rf_ref, f32[256,256]{1,0:T(8,128)S(1)} %get-tuple-element.24.twr_ref, ...), custom_call_target="tpu_custom_call" | custom-call | tf_op jit(solution)/shard_map/pallas_call | solution.py:71
  32.6 0.0 copy-done.10
  32.7 0.7 fusion.11.lf_ref
  33.3 0.0 copy-done.15
  33.3 0.7 pad_maximum_fusion.2.li_ref
  34.0 0.0 copy-done.6
  34.0 0.0 copy-done.8
  34.0 0.0 copy-done.12
  34.0 0.0 copy-done.13
  34.0 0.9 %maximum_maximum_fusion.1 = (bf16[512,512]{1,0:T(8,128)(2,1)S(1)}, bf16[512,512]{1,0:T(8,128)(2,1)}) fusion(bf16[256,256]{1,0:T(8,128)(2,1)S(1)} %get-tuple-element.25, bf16[256,256]{1,0:T(8,128)(2,1)S(1)} %copy-done.12, bf16[256,256]{1,0:T(8,128)(2,1)S(1)} %copy-done.13, f32[256,256]{1,0:T(8,128)S(1)} %get-tuple-element.26, f32[256,256]{1,0:T(8,128)S(1)} %copy-done.8, ...), kind=kLoop, calls=%fused_computation.6 | loop fusion | flops 4194304 | bytes 2228224 | tf_op jit(solution)/shard_map/concatenate | solution.py:45
  34.9 5.7 %all-to-all-done = bf16[64,2,6,256]{3,1,2,0:T(2,128)(2,1)} async-done(((bf16[64,2,6,256]{3,1,2,0:T(2,128)(2,1)}), bf16[64,2,6,256]{3,1,2,0:T(2,128)(2,1)}, u32[]{:S(2)}, u32[]{:S(2)}) %all-to-all-start) | async-done | bytes 393248 | tf_op jit(solution)/shard_map/all_to_all | solution.py:151
  40.6 1.1 %copy_convert_fusion = f32[64,2,6,256]{3,0,2,1:T(8,128)S(1)} fusion(bf16[64,2,6,256]{3,1,2,0:T(2,128)(2,1)} %all-to-all-done), kind=kLoop, calls=%fused_computation.8 | loop fusion | flops 196608 | bytes 1179648 | tf_op jit(solution)/shard_map/convert_element_type | solution.py:184
  41.7 1.5 %copy.45 = f32[64,2,6,256]{3,1,0,2:T(2,128)} copy(f32[64,2,6,256]{3,0,2,1:T(8,128)S(1)} %copy_convert_fusion) | data formatting | bytes 1572864 | tf_op jit(solution)/shard_map/convert_element_type | solution.py:184
  43.2 2.6 %reshape.45 = f32[128,6,256]{2,0,1:T(8,128)} reshape(f32[64,2,6,256]{3,1,0,2:T(2,128)} %copy.45) | data formatting | bytes 1572864 | tf_op jit(solution)/shard_map/convert_element_type | solution.py:184
  45.8 1.7 %copy.55 = f32[1,6,128,256]{3,1,2,0:T(8,128)S(1)} copy(f32[1,6,128,256]{3,2,1,0:T(8,128)} %bitcast.51) | data formatting | bytes 1572864
  47.5 0.6 add_convert_fusion
  48.1 0.1 copy.56
  48.2 0.0 copy-done.1
  48.2 4.3 %shard_map.65 = bf16[2,128,256]{2,1,0:T(8,128)(2,1)S(1)} custom-call(bf16[3,2,128,256]{3,2,1,0:T(8,128)(2,1)S(1)} %bitcast.49, f32[2,2,256,512]{3,2,1,0:T(8,128)S(1)} %shard_map.64.spec_ref, f32[2,2]{1,0:T(2,128)S(1)} %copy-done.4, bf16[512,128]{1,0:T(8,128)(2,1)S(1)} %copy-done.2, bf16[512,512]{1,0:T(8,128)(2,1)S(1)} %copy-done.1, ...), custom_call_target="tpu_custom_call" | custom-call | tf_op jit(solution)/shard_map/pallas_call | solution.py:120
  52.6 0.0 copy-start.16
  52.6 0.1 copy.50
  52.7 17.7 %all_to_all.10 = bf16[64,2,2,256]{3,2,1,0:T(2,128)(2,1)S(1)} all-to-all(bf16[64,2,2,256]{3,2,1,0:T(2,128)(2,1)S(1)} %bitcast.54), channel_id=1, replica_groups=mesh['win'=2,'g'=64,'core'=2] {'g'}, dimensions={0} | all-to-all | bytes 262144 | tf_op jit(solution)/shard_map/all_to_all | solution.py:159
  70.4 0.1 fusion.17
  70.6 2.7 %collective-permute-start.1 = (bf16[64,2,256]{2,0,1:T(8,128)(2,1)S(1)}, bf16[64,2,256]{2,0,1:T(8,128)(2,1)S(1)}, u32[]{:S(2)}, u32[]{:S(2)}) collective-permute-start(bf16[64,2,256]{2,0,1:T(8,128)(2,1)S(1)} %select_bitcast_fusion), channel_id=1, source_target_pairs={{0,1},{1,0},{2,3},{3,2},{4,5},{5,4},{6,7},{7,6},{8,9},{9,8},{10,11... | collective-permute-start | bytes 196616 | tf_op jit(solution)/shard_map/ppermute | solution.py:163
  73.3 0.9 %collective-permute-done.1 = bf16[64,2,256]{2,0,1:T(8,128)(2,1)S(1)} collective-permute-done((bf16[64,2,256]{2,0,1:T(8,128)(2,1)S(1)}, bf16[64,2,256]{2,0,1:T(8,128)(2,1)S(1)}, u32[]{:S(2)}, u32[]{:S(2)}) %collective-permute-start.1) | collective-permute-done | bytes 65568 | tf_op jit(solution)/shard_map/ppermute | solution.py:163
  74.2 0.1 copy.49
  74.4 0.1 reshape.43
  74.4 0.9 %convolution_convert_fusion.1 = bf16[256,256]{1,0:T(8,128)(2,1)} fusion(bf16[256,256]{1,0:T(8,128)(2,1)S(1)} %reshape.43, bf16[256,256]{1,0:T(8,128)(2,1)S(1)} %copy-done.16), kind=kOutput, calls=%fused_computation.1 | convolution fusion | flops 33619968 | bytes 393216 | tf_op jit(solution)/shard_map/dot_general | solution.py:199
  (24 shorter events, 0.4 us)
Async XLA Ops:
  0.0 1.0 %copy-start = (bf16[256,768]{1,0:T(8,128)(2,1)S(1)}, bf16[256,768]{1,0:T(8,128)(2,1)}, u32[]{:S(2)}) copy-start(bf16[256,768]{1,0:T(8,128)(2,1)} %param.7) | copy-start | bytes 1179652
  2.6 7.4 %copy-start.14 = (f32[2,2,32768]{2,1,0:T(2,128)S(1)}, f32[2,2,32768]{2,1,0:T(2,128)}, u32[]{:S(2)}) copy-start(f32[2,2,32768]{2,1,0:T(2,128)} %param.9) | copy-start | bytes 1572868
  3.5 6.9 %copy-start.17 = (f32[3,768]{1,0:T(4,128)S(1)}, f32[3,768]{1,0:T(4,128)}, u32[]{:S(2)}) copy-start(f32[3,768]{1,0:T(4,128)} %param.8) | copy-start | bytes 27652
  3.6 7.7 %collective-permute-start = (bf16[64,6,256]{2,0,1:T(8,128)(2,1)S(1)}, bf16[64,6,256]{2,0,1:T(8,128)(2,1)S(1)}, u32[]{:S(2)}, u32[]{:S(2)}) collective-permute-start(bf16[64,6,256]{2,0,1:T(8,128)(2,1)S(1)} %bitcast.55), channel_id=1, source_target_pairs={{0,1},{1,0},{2,3},{3,2},{4,5},{5,4},{6,7},{7,6},{8,9},{9,8},{10,11... | collective-permute-start | bytes 589832 | tf_op jit(solution)/shard_map/ppermute | solution.py:149
  8.5 18.8 %copy-start.5 = (f32[256,256]{1,0:T(8,128)}, f32[256,256]{1,0:T(8,128)S(1)}, u32[]{:S(2)}) copy-start(f32[256,256]{1,0:T(8,128)S(1)} %get-tuple-element.13) | copy-start | bytes 786436
  8.6 18.8 %copy-start.9 = (f32[256,128]{1,0:T(8,128)}, f32[256,128]{1,0:T(8,128)S(1)}, u32[]{:S(2)}) copy-start(f32[256,128]{1,0:T(8,128)S(1)} %slice.65) | copy-start | bytes 393220
  8.6 0.7 copy-start.11
  8.6 18.8 %copy-start.7 = (f32[256,256]{1,0:T(8,128)}, f32[256,256]{1,0:T(8,128)S(1)}, u32[]{:S(2)}) copy-start(f32[256,256]{1,0:T(8,128)S(1)} %get-tuple-element.22) | copy-start | bytes 786436
  12.5 28.1 %all-to-all-start = ((bf16[64,2,6,256]{3,1,2,0:T(2,128)(2,1)}), bf16[64,2,6,256]{3,1,2,0:T(2,128)(2,1)}, u32[]{:S(2)}, u32[]{:S(2)}) async-start(bf16[64,2,6,256]{3,1,2,0:T(2,128)(2,1)} %copy.43), calls=%async_computation | async-start | bytes 786432 | tf_op jit(solution)/shard_map/all_to_all | solution.py:151
  27.5 5.2 %copy-start.10 = (f32[256,128]{1,0:T(8,128)S(1)}, f32[256,128]{1,0:T(8,128)}, u32[]{:S(2)}) copy-start(f32[256,128]{1,0:T(8,128)} %copy-done.9) | copy-start | bytes 393220
  27.5 5.8 %copy-start.15 = (bf16[128,256]{1,0:T(8,128)(2,1)S(1)}, bf16[128,256]{1,0:T(8,128)(2,1)}, u32[]{:S(2)}) copy-start(bf16[128,256]{1,0:T(8,128)(2,1)} %slice.67) | copy-start | bytes 196612
  27.5 6.5 %copy-start.6 = (f32[256,256]{1,0:T(8,128)S(1)}, f32[256,256]{1,0:T(8,128)}, u32[]{:S(2)}) copy-start(f32[256,256]{1,0:T(8,128)} %copy-done.5) | copy-start | bytes 786436
  27.5 6.5 %copy-start.8 = (f32[256,256]{1,0:T(8,128)S(1)}, f32[256,256]{1,0:T(8,128)}, u32[]{:S(2)}) copy-start(f32[256,256]{1,0:T(8,128)} %copy-done.7) | copy-start | bytes 786436
  27.5 6.5 %copy-start.12 = (bf16[256,256]{1,0:T(8,128)(2,1)S(1)}, bf16[256,256]{1,0:T(8,128)(2,1)}, u32[]{:S(2)}) copy-start(bf16[256,256]{1,0:T(8,128)(2,1)} %copy-done.11) | copy-start | bytes 393220
  27.5 6.5 %copy-start.13 = (bf16[256,256]{1,0:T(8,128)(2,1)S(1)}, bf16[256,256]{1,0:T(8,128)(2,1)}, u32[]{:S(2)}) copy-start(bf16[256,256]{1,0:T(8,128)(2,1)} %get-tuple-element.12) | copy-start | bytes 393220
  45.8 2.4 %copy-start.1 = (bf16[512,512]{1,0:T(8,128)(2,1)S(1)}, bf16[512,512]{1,0:T(8,128)(2,1)}, u32[]{:S(2)}) copy-start(bf16[512,512]{1,0:T(8,128)(2,1)} %get-tuple-element.32.rf_ref) | copy-start | bytes 1572868
  45.8 2.4 %copy-start.2 = (bf16[512,128]{1,0:T(8,128)(2,1)S(1)}, bf16[512,128]{1,0:T(8,128)(2,1)}, u32[]{:S(2)}) copy-start(bf16[512,128]{1,0:T(8,128)(2,1)} %fusion.11.lf_ref) | copy-start | bytes 393220
  45.8 2.4 %copy-start.3 = (bf16[128,512]{1,0:T(8,128)(2,1)S(1)}, bf16[128,512]{1,0:T(8,128)(2,1)}, u32[]{:S(2)}) copy-start(bf16[128,512]{1,0:T(8,128)(2,1)} %pad_maximum_fusion.2.li_ref) | copy-start | bytes 393220
  45.8 2.4 %copy-start.4 = (f32[2,2]{1,0:T(2,128)S(1)}, f32[2,2]{1,0:T(2,128)}, u32[]{:S(2)}) copy-start(f32[2,2]{1,0:T(2,128)} %bias_ref.1) | copy-start | bytes 52
  52.6 21.9 %copy-start.16 = (bf16[256,256]{1,0:T(8,128)(2,1)S(1)}, bf16[256,256]{1,0:T(8,128)(2,1)}, u32[]{:S(2)}) copy-start(bf16[256,256]{1,0:T(8,128)(2,1)} %param.11) | copy-start | bytes 393220
  70.6 3.6 %collective-permute-start.1 = (bf16[64,2,256]{2,0,1:T(8,128)(2,1)S(1)}, bf16[64,2,256]{2,0,1:T(8,128)(2,1)S(1)}, u32[]{:S(2)}, u32[]{:S(2)}) collective-permute-start(bf16[64,2,256]{2,0,1:T(8,128)(2,1)S(1)} %select_bitcast_fusion), channel_id=1, source_target_pairs={{0,1},{1,0},{2,3},{3,2},{4,5},{5,4},{6,7},{7,6},{8,9},{9,8},{10,11... | collective-permute-start | bytes 196616 | tf_op jit(solution)/shard_map/ppermute | solution.py:163

commit v5 on v2

--- a/solution.py
+++ b/solution.py
@@ -1,3 +1,4 @@
+import functools
 import math
 
 import jax
@@ -101,40 +102,56 @@
     return (back * scale + bias * signal).astype(jnp.bfloat16)
 
 
-def chain_kernel(short_ref, spec_ref, bias_ref, lf_ref, rf_ref, ri_ref, li_ref, twr_ref, twi_ref, out_ref):
-    channel = pl.program_id(0)
+def chain_kernel(
+    rows_ref, spec_ref, bias_ref, taps_ref,
+    lf_ref, rf_ref, ri_ref, li_ref, twr_ref, twi_ref, out_ref, *, per,
+):
+    half = SIDE // 2
     tabs = (lf_ref[...], rf_ref[...], ri_ref[...], li_ref[...], twr_ref[...], twi_ref[...])
-    state = short_ref[2, 0]
-    for order in range(2):
-        conv = convolve(state, spec_ref[order, 0], bias_ref[order, channel], tabs)
-        state = (short_ref[order, 0].astype(jnp.float32) * conv.astype(jnp.float32)).astype(jnp.bfloat16)
-    out_ref[0] = state
+    big_r = lax.broadcasted_iota(jnp.int32, (2 * SIDE, 2 * SIDE), 0)
+    big_c = lax.broadcasted_iota(jnp.int32, (2 * SIDE, 2 * SIDE), 1)
+    origin = jnp.where(big_r < SIDE, big_r, big_r - 2 * SIDE)
+    lag = jnp.where(big_c < SIDE, 1, 2)
+    target = jnp.where(big_c < SIDE, big_c, big_c - SIDE)
+    shifts = (origin + lag == target).astype(jnp.bfloat16)
+    small_r = lax.broadcasted_iota(jnp.int32, (half, half), 0)
+    small_c = lax.broadcasted_iota(jnp.int32, (half, half), 1)
+    carry = (small_c + 1 == small_r).astype(jnp.bfloat16)
+    for channel in range(per):
+        streams = []
+        for stream in range(3):
+            p = rows_ref[:, stream * per + channel, :].reshape(half, SIDE)
+            q = jnp.dot(carry, p, preferred_element_type=jnp.float32).astype(jnp.bfloat16)
+            moved = jnp.dot(jnp.concatenate([p, q], 1), shifts, preferred_element_type=jnp.float32)
+            short = (
+                taps_ref[stream, channel] * p.astype(jnp.float32)
+                + taps_ref[3 + stream, channel] * moved[:, :SIDE]
+                + taps_ref[6 + stream, channel] * moved[:, SIDE:]
+            )
+            streams.append(short.astype(jnp.bfloat16))
+        state = streams[2]
+        for order in range(2):
+            conv = convolve(state, spec_ref[order, channel], bias_ref[order, channel], tabs)
+            state = (streams[order].astype(jnp.float32) * conv.astype(jnp.float32)).astype(jnp.bfloat16)
+        out_ref[channel] = state
 
 
-def chain(short, spectra, bias, tabs):
-    per = short.shape[1]
+def chain(rows, spectra, bias, taps, tabs, per):
     half = SIDE // 2
     left_fwd, right_fwd, right_inv, left_inv, tw_re, tw_im = tabs
     low = lambda t: t.astype(jnp.bfloat16)
-    full = lambda shape: pl.BlockSpec(shape, lambda c: (0,) * len(shape))
+    vmem = pl.BlockSpec(memory_space=pltpu.VMEM)
+    smem = pl.BlockSpec(memory_space=pltpu.SMEM)
     return pl.pallas_call(
-        chain_kernel,
-        grid=(per,),
-        in_specs=[
-            pl.BlockSpec((3, 1, half, SIDE), lambda c: (0, c, 0, 0)),
-            pl.BlockSpec((2, 1, SIDE, 2 * SIDE), lambda c: (0, c, 0, 0)),
-            pl.BlockSpec(memory_space=pltpu.SMEM),
-            full((2 * SIDE, half)),
-            full((2 * SIDE, 2 * SIDE)),
-            full((2 * SIDE, 2 * SIDE)),
-            full((half, 2 * SIDE)),
-            full((SIDE, SIDE)),
-            full((SIDE, SIDE)),
-        ],
-        out_specs=pl.BlockSpec((1, half, SIDE), lambda c: (c, 0, 0)),
+        functools.partial(chain_kernel, per=per),
+        in_specs=[vmem, vmem, smem, smem] + [vmem] * 6,
+        out_specs=vmem,
         out_shape=jax.ShapeDtypeStruct((per, half, SIDE), jnp.bfloat16),
         compiler_params=pltpu.CompilerParams(vmem_limit_bytes=48 * 1024 * 1024),
-    )(short, spectra, bias, low(left_fwd), low(right_fwd), low(right_inv), low(left_inv), tw_re, tw_im)
+    )(
+        rows, spectra, bias, taps,
+        low(left_fwd), low(right_fwd), low(right_inv), low(left_inv), tw_re, tw_im,
+    )
 
 
 def local(layer_input, w_in, short_w, filters, filter_bias, w_out):
@@ -145,29 +162,16 @@
         w_in, layer_input, (((0,), (1,)), ((), ())), preferred_element_type=jnp.float32
     ).astype(jnp.bfloat16)
     positions = projected.shape[1]
-    grouped = jnp.swapaxes(projected.reshape(3, groups, per, positions), 0, 1)
     tabs = make_tables()
     spectra = filter_spectra(filters.reshape(2, per, SIDE // 2, SIDE), tabs)
+    grouped = jnp.swapaxes(projected.reshape(3, groups, per, positions), 0, 1)
     spread = lax.all_to_all(
-        grouped.reshape(groups, 3 * per, positions), "seq", split_axis=0, concat_axis=2, tiled=True
-    ).reshape(3 * per, groups * positions)
+        grouped.reshape(groups, 3 * per, positions), "seq", split_axis=0, concat_axis=0, tiled=True
+    )
     me = lax.axis_index("seq")
-    taps = lax.dynamic_slice_in_dim(short_w.reshape(3, 3, groups, per), me, 1, axis=2)
-    taps = taps.reshape(3, 3 * per)
-    extended = jnp.pad(spread.astype(jnp.float32), ((0, 0), (2, 0)))
-    length = spread.shape[1]
-    short = (
-        taps[0][:, None] * extended[:, 2:]
-        + taps[1][:, None] * extended[:, 1 : length + 1]
-        + taps[2][:, None] * extended[:, :length]
-    ).astype(jnp.bfloat16)
-    half = SIDE // 2
-    state = chain(
-        short.reshape(3, per, half, SIDE),
-        spectra,
-        filter_bias,
-        tabs,
-    ).reshape(per, length)
+    taps = lax.dynamic_slice_in_dim(short_w.reshape(9, groups, per), me, 1, axis=1)
+    state = chain(spread, spectra, filter_bias, taps.reshape(9, per), tabs, per)
+    state = state.reshape(per, groups * positions)
     returned = lax.all_to_all(state, "seq", split_axis=1, concat_axis=0, tiled=True)
     output = lax.dot_general(
         returned, w_out, (((0,), (0,)), ((), ())), preferred_element_type=jnp.float32

time: 69.5 us -> 74 us (1.065)
  local copies, waits for them, and re-layouts: 3.91 us -> 7.86 us
  Pallas kernels: 9.41 us -> 12 us
  other arithmetic: 7.75 us -> 5.89 us
  waiting for transfers between devices: 8.97 us -> 7.77 us
  blocking collectives: 18.8 us -> 19.9 us
    unnamed x37 -> x48, local copies, waits for them, and re-layouts: 1.14 us -> 3.93 us
    pallas_call x1, Pallas kernels: 4.33 us -> 6.87 us  [chain(): pl.pallas_call(functools.partial(chain_kernel, per=per), in_specs=[vmem,...]
    convert_element_type x2 -> x0, other arithmetic: 1.8 us -> none  [the longest x1 1.19 us: local(): extended = jnp.pad(spread.astype(jnp.float32), ((0, 0), (2, 0)))]
    slice x2, local copies, waits for them, and re-layouts: 0.01 us -> 1.24 us  [make_tables(): left_inv = jnp.concatenate([f_re[:half], f_im[:half]], 1)]
    all_to_all x1, waiting for transfers between devices: 8.97 us -> 7.77 us  [local(): lax.all_to_all(grouped.reshape(groups, 3 * per, positions), 'seq', split_...]
    all_to_all x1, blocking collectives: 18.8 us -> 19.9 us  [local(): lax.all_to_all(state, 'seq', split_axis=1, concat_axis=0, tiled=True)]
where the time goes in v5:
time: 74 us; the launch traced here: 73.6 us
  blocking collectives  19.9 us (27%)
  starting transfers between devices  16.8 us (23%)
  Pallas kernels  12 us (16%)
  local copies, waits for them, and re-layouts  7.86 us (11%)
  waiting for transfers between devices  7.77 us (10%)
  other arithmetic  5.89 us (8%)
  matrix products  3 us (4%)
    all_to_all x1, blocking collectives, local(): lax.all_to_all(state, 'seq', split_axis=1, concat_axis=0, tiled=True)  19.9 us
    all_to_all x1, starting transfers between devices, local(): lax.all_to_all(grouped.reshape(groups, 3 * per, positions), 'seq', split_...  16.8 us
    all_to_all x1, waiting for transfers between devices, local(): lax.all_to_all(grouped.reshape(groups, 3 * per, positions), 'seq', split_...  7.77 us
    pallas_call x1, Pallas kernels, chain(): pl.pallas_call(functools.partial(chain_kernel, per=per), in_specs=[vmem,...  6.87 us
    pallas_call x1, Pallas kernels, filter_spectra(): pl.pallas_call(filter_kernel, grid=(orders, per), in_specs=[pl.BlockSpec(...  5.08 us
    unnamed x48, local copies, waits for them, and re-layouts  3.93 us
    sin x1, other arithmetic, make_tables(): jnp.sin(big)  1.9 us
    dot_general x1, matrix products, local(): lax.dot_general(returned, w_out, (((0,), (0,)), ((), ())), preferred_elem...  1.79 us
  transfers between devices with their start and end apart: 1, of which 1 were waited for; matrix products, arithmetic and copies ran while one was open for 11% of the time, Pallas kernels for 7%

profile of v5, /device:TPU:1, one launch (start us, length us, event | category | flops | bytes accessed | tf_op | source)
XLA Modules:
  0.0 73.6 jit_solution(12068381618473819465)
XLA Ops:
  0.0 0.0 copy-start
  0.0 1.0 %copy-done = bf16[256,768]{1,0:T(8,128)(2,1)S(1)} copy-done((bf16[256,768]{1,0:T(8,128)(2,1)S(1)}, bf16[256,768]{1,0:T(8,128)(2,1)}, u32[]{:S(2)}) %copy-start) | copy-done | bytes 393240
  1.0 1.2 %convolution_convert_fusion = bf16[768,256]{1,0:T(8,128)(2,1)S(1)} fusion(bf16[256,768]{1,0:T(8,128)(2,1)S(1)} %copy-done, bf16[256,256]{1,0:T(8,128)(2,1)} %param.6), kind=kOutput, calls=%fused_computation | convolution fusion | flops 100859904 | bytes 917504 | tf_op jit(solution)/shard_map/dot_general | solution.py:161
  2.2 0.2 reshape.20
  2.4 1.0 %copy.16 = bf16[128,6,256]{2,1,0:T(8,128)(2,1)} copy(bf16[128,6,256]{2,0,1:T(8,128)(2,1)S(1)} %bitcast.9) | data formatting | bytes 786432 | tf_op jit(solution)/shard_map/reshape | solution.py:169
  3.5 16.8 %all-to-all-start = ((bf16[128,6,256]{2,1,0:T(8,128)(2,1)}), bf16[128,6,256]{2,1,0:T(8,128)(2,1)}, u32[]{:S(2)}, u32[]{:S(2)}) async-start(bf16[128,6,256]{2,1,0:T(8,128)(2,1)} %copy.16), calls=%async_computation | async-start | bytes 1048576 | tf_op jit(solution)/shard_map/all_to_all | solution.py:168
  20.3 0.0 copy-start.20
  20.4 1.6 %negate_convert_fusion = (bf16[256,256]{1,0:T(8,128)(2,1)}, f32[256,256]{1,0:T(8,128)S(1)}, s32[256,256]{1,0:T(8,128)S(1)}) fusion(s32[256,256]{1,0:T(8,128)S(1)} %iota.10, s32[256,256]{1,0:T(8,128)S(1)} %iota.11), kind=kLoop, calls=%fused_computation.18 | loop fusion | flops 1048576 | bytes 1179648 | tf_op jit(solution)/shard_map/convert.9
  22.0 1.9 %fusion.3 = (f32[256,256]{1,0:T(8,128)S(1)}, f32[256,256]{1,0:T(8,128)S(1)}, bf16[256,256]{1,0:T(8,128)(2,1)S(1)}, f32[256,256]{1,0:T(8,128)S(1)}) fusion(s32[256,256]{1,0:T(8,128)S(1)} %get-tuple-element.11), kind=kLoop, calls=%fused_computation.12 | loop fusion | flops 1048576 | bytes 1179648 | tf_op jit(solution)/shard_map/sin | solution.py:50
  23.9 0.0 copy-start.7
  23.9 0.0 copy-start.15
  24.0 0.0 copy-start.9
  24.0 0.0 copy-start.17
  24.0 0.0 copy-start.11
  24.1 0.0 copy-done.20
  24.1 0.0 copy-start.13
  24.1 0.5 reshape.22.filt_ref
  24.5 0.6 slice.21
  25.2 0.6 slice.20
  25.8 0.0 copy-done.23
  25.8 0.5 reshape.23
  26.4 0.1 copy.17
  26.5 0.1 copy.18.taps_ref
  26.6 0.0 copy-done.5
  26.6 0.1 maximum_maximum_fusion.rf_ref
  26.7 0.0 copy-done.7
  26.7 0.0 copy-done.15
  26.7 0.0 copy-done.9
  26.7 0.0 copy-done.17
  26.7 0.0 copy-done.11
  26.7 0.0 copy-done.13
  26.8 0.0 copy-start.12
  26.8 0.0 copy-start.14
  26.8 0.0 copy-start.21
  26.8 0.0 copy-start.22
  26.8 0.0 copy-start.6
  26.8 0.0 copy-start.8
  26.8 0.0 copy-start.10
  26.8 0.0 copy-start.16
  26.8 0.0 copy-start.18
  26.8 0.0 copy-start.19
  26.9 5.1 %shard_map.64.spec_ref = f32[2,2,256,512]{3,2,1,0:T(8,128)S(1)} custom-call(f32[2,2,128,256]{3,2,1,0:T(8,128)S(1)} %reshape.22.filt_ref, f32[512,128]{1,0:T(8,128)S(1)} %pad_maximum_fusion.lf_ref, f32[512,512]{1,0:T(8,128)S(1)} %maximum_maximum_fusion.rf_ref, f32[256,256]{1,0:T(8,128)S(1)} %get-tuple-element.17.twr_ref, f32[256,256]{1,0:T(8,128)S(1)} %get-tuple-element.16.twi_ref), custom_call_target="tpu_custom_call" | custom-call | tf_op jit(solution)/shard_map/pallas_call | solution.py:72
  31.9 0.0 copy-done.12
  32.0 0.0 copy-done.14
  32.0 0.0 copy-start.4
  32.0 0.7 fusion.7.lf_ref
  32.6 0.0 copy-done.21
  32.6 0.0 copy-done.22
  32.6 0.7 pad_maximum_fusion.1.li_ref
  33.3 0.0 copy-done.6
  33.3 0.0 copy-done.8
  33.3 0.0 copy-done.10
  33.3 0.0 copy-done.18
  33.3 0.0 copy-done.19
  33.3 0.9 %maximum_maximum_fusion.1 = (bf16[512,512]{1,0:T(8,128)(2,1)S(1)}, bf16[512,512]{1,0:T(8,128)(2,1)}) fusion(bf16[256,256]{1,0:T(8,128)(2,1)S(1)} %copy-done.16, bf16[256,256]{1,0:T(8,128)(2,1)S(1)} %copy-done.18, bf16[256,256]{1,0:T(8,128)(2,1)S(1)} %copy-done.19, f32[256,256]{1,0:T(8,128)S(1)} %copy-done.8, f32[256,256]{1,0:T(8,128)S(1)} %copy-done.10, ...), kind=kLoop, calls=%fused_computation.3 | loop fusion | flops 4194304 | bytes 2228224 | tf_op jit(solution)/shard_map/concatenate | solution.py:46
  34.2 7.8 %all-to-all-done.rows_ref = bf16[128,6,256]{2,1,0:T(8,128)(2,1)} async-done(((bf16[128,6,256]{2,1,0:T(8,128)(2,1)}), bf16[128,6,256]{2,1,0:T(8,128)(2,1)}, u32[]{:S(2)}, u32[]{:S(2)}) %all-to-all-start) | async-done | bytes 393248 | tf_op jit(solution)/shard_map/all_to_all | solution.py:168
  42.0 1.0 %copy-done.1 = bf16[512,512]{1,0:T(8,128)(2,1)S(1)} copy-done((bf16[512,512]{1,0:T(8,128)(2,1)S(1)}, bf16[512,512]{1,0:T(8,128)(2,1)}, u32[]{:S(2)}) %copy-start.1) | copy-done | bytes 524312
  43.0 0.9 %copy-done.2 = bf16[512,128]{1,0:T(8,128)(2,1)S(1)} copy-done((bf16[512,128]{1,0:T(8,128)(2,1)S(1)}, bf16[512,128]{1,0:T(8,128)(2,1)}, u32[]{:S(2)}) %copy-start.2) | copy-done | bytes 131096
  43.9 0.9 %copy-done.3 = bf16[128,512]{1,0:T(8,128)(2,1)S(1)} copy-done((bf16[128,512]{1,0:T(8,128)(2,1)S(1)}, bf16[128,512]{1,0:T(8,128)(2,1)}, u32[]{:S(2)}) %copy-start.3) | copy-done | bytes 131096
  44.8 6.9 %shard_map.65 = bf16[2,128,256]{2,1,0:T(8,128)(2,1)S(1)} custom-call(bf16[128,6,256]{2,1,0:T(8,128)(2,1)} %all-to-all-done.rows_ref, f32[2,2,256,512]{3,2,1,0:T(8,128)S(1)} %shard_map.64.spec_ref, f32[2,2]{1,0:T(2,128)S(1)} %copy-done.4, f32[9,2]{1,0:T(8,128)S(1)} %copy.18.taps_ref, bf16[512,128]{1,0:T(8,128)(2,1)S(1)} %copy-done.2, ...), custom_call_target="tpu_custom_call" | custom-call | tf_op jit(solution)/shard_map/pallas_call | solution.py:145
  51.7 0.1 copy.19
  51.9 19.9 %all_to_all.21 = bf16[2,128,256]{2,0,1:T(2,128)(2,1)S(1)} all-to-all(bf16[2,128,256]{2,0,1:T(2,128)(2,1)S(1)} %copy.19), channel_id=1, replica_groups=mesh['win'=2,'seq'=128] {'seq'}, dimensions={1} | all-to-all | bytes 262144 | tf_op jit(solution)/shard_map/all_to_all | solution.py:175
  71.7 0.1 all_to_all.18
  71.8 1.8 %convolution_convert_fusion.1 = bf16[256,256]{1,0:T(8,128)(2,1)} fusion(bf16[256,256]{1,0:T(8,128)(2,1)S(1)} %all_to_all.18, bf16[256,256]{1,0:T(8,128)(2,1)} %param.11), kind=kOutput, calls=%fused_computation.1 | convolution fusion | flops 33619968 | bytes 393216 | tf_op jit(solution)/shard_map/dot_general | solution.py:176
  (15 shorter events, 0.2 us)
Async XLA Ops:
  0.0 1.0 %copy-start = (bf16[256,768]{1,0:T(8,128)(2,1)S(1)}, bf16[256,768]{1,0:T(8,128)(2,1)}, u32[]{:S(2)}) copy-start(bf16[256,768]{1,0:T(8,128)(2,1)} %param.7) | copy-start | bytes 1179652
  3.5 38.5 %all-to-all-start = ((bf16[128,6,256]{2,1,0:T(8,128)(2,1)}), bf16[128,6,256]{2,1,0:T(8,128)(2,1)}, u32[]{:S(2)}, u32[]{:S(2)}) async-start(bf16[128,6,256]{2,1,0:T(8,128)(2,1)} %copy.16), calls=%async_computation | async-start | bytes 1048576 | tf_op jit(solution)/shard_map/all_to_all | solution.py:168
  20.3 3.8 %copy-start.20 = (f32[2,2,32768]{2,1,0:T(2,128)S(1)}, f32[2,2,32768]{2,1,0:T(2,128)}, u32[]{:S(2)}) copy-start(f32[2,2,32768]{2,1,0:T(2,128)} %param.9) | copy-start | bytes 1572868
  22.0 4.6 %copy-start.5 = (f32[256,256]{1,0:T(8,128)}, f32[256,256]{1,0:T(8,128)S(1)}, u32[]{:S(2)}) copy-start(f32[256,256]{1,0:T(8,128)S(1)} %get-tuple-element.10) | copy-start | bytes 786436
  22.0 3.8 %copy-start.23 = (f32[3,768]{1,0:T(4,128)S(1)}, f32[3,768]{1,0:T(4,128)}, u32[]{:S(2)}) copy-start(f32[3,768]{1,0:T(4,128)} %param.8) | copy-start | bytes 27652
  23.9 2.8 %copy-start.7 = (f32[256,256]{1,0:T(8,128)}, f32[256,256]{1,0:T(8,128)S(1)}, u32[]{:S(2)}) copy-start(f32[256,256]{1,0:T(8,128)S(1)} %get-tuple-element.19) | copy-start | bytes 786436
  23.9 2.8 %copy-start.15 = (bf16[256,256]{1,0:T(8,128)(2,1)}, bf16[256,256]{1,0:T(8,128)(2,1)S(1)}, u32[]{:S(2)}) copy-start(bf16[256,256]{1,0:T(8,128)(2,1)S(1)} %get-tuple-element.18) | copy-start | bytes 393220
  24.0 2.7 %copy-start.9 = (f32[256,256]{1,0:T(8,128)}, f32[256,256]{1,0:T(8,128)S(1)}, u32[]{:S(2)}) copy-start(f32[256,256]{1,0:T(8,128)S(1)} %get-tuple-element.15) | copy-start | bytes 786436
  24.0 2.7 %copy-start.17 = (bf16[256,256]{1,0:T(8,128)(2,1)}, bf16[256,256]{1,0:T(8,128)(2,1)S(1)}, u32[]{:S(2)}) copy-start(bf16[256,256]{1,0:T(8,128)(2,1)S(1)} %get-tuple-element.14) | copy-start | bytes 393220
  24.0 2.7 %copy-start.11 = (f32[256,128]{1,0:T(8,128)}, f32[256,128]{1,0:T(8,128)S(1)}, u32[]{:S(2)}) copy-start(f32[256,128]{1,0:T(8,128)S(1)} %slice.19) | copy-start | bytes 393220
  24.1 2.7 %copy-start.13 = (f32[256,128]{1,0:T(8,128)}, f32[256,128]{1,0:T(8,128)S(1)}, u32[]{:S(2)}) copy-start(f32[256,128]{1,0:T(8,128)S(1)} %slice.18) | copy-start | bytes 393220
  26.8 5.2 %copy-start.12 = (f32[256,128]{1,0:T(8,128)S(1)}, f32[256,128]{1,0:T(8,128)}, u32[]{:S(2)}) copy-start(f32[256,128]{1,0:T(8,128)} %copy-done.11) | copy-start | bytes 393220
  26.8 5.2 %copy-start.14 = (f32[256,128]{1,0:T(8,128)S(1)}, f32[256,128]{1,0:T(8,128)}, u32[]{:S(2)}) copy-start(f32[256,128]{1,0:T(8,128)} %copy-done.13) | copy-start | bytes 393220
  26.8 5.9 %copy-start.21 = (bf16[128,256]{1,0:T(8,128)(2,1)S(1)}, bf16[128,256]{1,0:T(8,128)(2,1)}, u32[]{:S(2)}) copy-start(bf16[128,256]{1,0:T(8,128)(2,1)} %slice.21) | copy-start | bytes 196612
  26.8 5.9 %copy-start.22 = (bf16[128,256]{1,0:T(8,128)(2,1)S(1)}, bf16[128,256]{1,0:T(8,128)(2,1)}, u32[]{:S(2)}) copy-start(bf16[128,256]{1,0:T(8,128)(2,1)} %slice.20) | copy-start | bytes 196612
  26.8 6.5 %copy-start.6 = (f32[256,256]{1,0:T(8,128)S(1)}, f32[256,256]{1,0:T(8,128)}, u32[]{:S(2)}) copy-start(f32[256,256]{1,0:T(8,128)} %copy-done.5) | copy-start | bytes 786436
  26.8 6.5 %copy-start.8 = (f32[256,256]{1,0:T(8,128)S(1)}, f32[256,256]{1,0:T(8,128)}, u32[]{:S(2)}) copy-start(f32[256,256]{1,0:T(8,128)} %copy-done.7) | copy-start | bytes 786436
  26.8 6.5 %copy-start.10 = (f32[256,256]{1,0:T(8,128)S(1)}, f32[256,256]{1,0:T(8,128)}, u32[]{:S(2)}) copy-start(f32[256,256]{1,0:T(8,128)} %copy-done.9) | copy-start | bytes 786436
  26.8 6.5 %copy-start.16 = (bf16[256,256]{1,0:T(8,128)(2,1)S(1)}, bf16[256,256]{1,0:T(8,128)(2,1)}, u32[]{:S(2)}) copy-start(bf16[256,256]{1,0:T(8,128)(2,1)} %copy-done.15) | copy-start | bytes 393220
  26.8 6.5 %copy-start.18 = (bf16[256,256]{1,0:T(8,128)(2,1)S(1)}, bf16[256,256]{1,0:T(8,128)(2,1)}, u32[]{:S(2)}) copy-start(bf16[256,256]{1,0:T(8,128)(2,1)} %copy-done.17) | copy-start | bytes 393220
  26.8 6.5 %copy-start.19 = (bf16[256,256]{1,0:T(8,128)(2,1)S(1)}, bf16[256,256]{1,0:T(8,128)(2,1)}, u32[]{:S(2)}) copy-start(bf16[256,256]{1,0:T(8,128)(2,1)} %get-tuple-element.9) | copy-start | bytes 393220
  32.0 10.0 %copy-start.4 = (f32[2,2]{1,0:T(2,128)S(1)}, f32[2,2]{1,0:T(2,128)}, u32[]{:S(2)}) copy-start(f32[2,2]{1,0:T(2,128)} %bias_ref.1) | copy-start | bytes 52
  42.0 1.0 %copy-start.1 = (bf16[512,512]{1,0:T(8,128)(2,1)S(1)}, bf16[512,512]{1,0:T(8,128)(2,1)}, u32[]{:S(2)}) copy-start(bf16[512,512]{1,0:T(8,128)(2,1)} %get-tuple-element.21.rf_ref) | copy-start | bytes 1572868
  43.0 0.9 %copy-start.2 = (bf16[512,128]{1,0:T(8,128)(2,1)S(1)}, bf16[512,128]{1,0:T(8,128)(2,1)}, u32[]{:S(2)}) copy-start(bf16[512,128]{1,0:T(8,128)(2,1)} %fusion.7.lf_ref) | copy-start | bytes 393220
  43.9 0.9 %copy-start.3 = (bf16[128,512]{1,0:T(8,128)(2,1)S(1)}, bf16[128,512]{1,0:T(8,128)(2,1)}, u32[]{:S(2)}) copy-start(bf16[128,512]{1,0:T(8,128)(2,1)} %pad_maximum_fusion.1.li_ref) | copy-start | bytes 393220

commit v6 on v2

--- a/solution.py
+++ b/solution.py
@@ -148,19 +148,18 @@
     grouped = jnp.swapaxes(projected.reshape(3, groups, per, positions), 0, 1)
     tabs = make_tables()
     spectra = filter_spectra(filters.reshape(2, per, SIDE // 2, SIDE), tabs)
-    spread = lax.all_to_all(
-        grouped.reshape(groups, 3 * per, positions), "seq", split_axis=0, concat_axis=2, tiled=True
-    ).reshape(3 * per, groups * positions)
+    spread = lax.all_to_all(grouped, "seq", split_axis=0, concat_axis=0, tiled=True)
     me = lax.axis_index("seq")
     taps = lax.dynamic_slice_in_dim(short_w.reshape(3, 3, groups, per), me, 1, axis=2)
-    taps = taps.reshape(3, 3 * per)
-    extended = jnp.pad(spread.astype(jnp.float32), ((0, 0), (2, 0)))
-    length = spread.shape[1]
-    short = (
-        taps[0][:, None] * extended[:, 2:]
-        + taps[1][:, None] * extended[:, 1 : length + 1]
-        + taps[2][:, None] * extended[:, :length]
-    ).astype(jnp.bfloat16)
+    taps = taps.reshape(3, 1, 3, per, 1)
+    signal = spread.astype(jnp.float32)
+    edge = jnp.zeros((1, 3, per, 2), jnp.float32)
+    before = jnp.concatenate([edge, signal[:-1, :, :, -2:]], 0)
+    back_one = jnp.concatenate([before[:, :, :, 1:], signal[:, :, :, :-1]], 3)
+    back_two = jnp.concatenate([before, signal[:, :, :, :-2]], 3)
+    short = (taps[0] * signal + taps[1] * back_one + taps[2] * back_two).astype(jnp.bfloat16)
+    length = groups * positions
+    short = jnp.transpose(short, (1, 2, 0, 3))
     half = SIDE // 2
     state = chain(
         short.reshape(3, per, half, SIDE),

time: 69.5 us -> 71.2 us (1.024)
  waiting for transfers between devices: 8.97 us -> 5.31 us
  blocking collectives: 18.8 us -> 22.3 us
  local copies, waits for them, and re-layouts: 3.91 us -> 5.22 us
  other arithmetic: 7.75 us -> 8.51 us
    all_to_all x1, waiting for transfers between devices: 8.97 us -> 5.31 us  [local(): lax.all_to_all(grouped, 'seq', split_axis=0, concat_axis=0, tiled=True)]
    all_to_all x1, blocking collectives: 18.8 us -> 22.3 us  [local(): lax.all_to_all(state, 'seq', split_axis=1, concat_axis=0, tiled=True)]
    transpose x0 -> x1, other arithmetic: none -> 1.55 us  [local(): short = jnp.transpose(short, (1, 2, 0, 3))]
    transpose x0 -> x1, local copies, waits for them, and re-layouts: none -> 1.03 us  [local(): grouped = jnp.swapaxes(projected.reshape(3, groups, per, positions), 0, 1)]
    reshape x1 -> x0, local copies, waits for them, and re-layouts: 1.02 us -> none  [local(): grouped.reshape(groups, 3 * per, positions)]
    slice x2, local copies, waits for them, and re-layouts: 0.01 us -> 0.76 us  [make_tables(): left_inv = jnp.concatenate([f_re[:half], f_im[:half]], 1)]
    convert_element_type x2 -> x1, other arithmetic: 1.8 us -> 1.06 us  [local(): signal = spread.astype(jnp.float32)]
  transfers between devices with their start and end apart: 1 -> 1, of which waited for: 1 -> 1; matrix products, arithmetic and copies ran while one was open for 11% -> 12% of each run, Pallas kernels for 7% -> 7%
where the time goes in v6:
time: 71.2 us; the launch traced here: 70.9 us
  blocking collectives  22.3 us (31%)
  starting transfers between devices  16.8 us (24%)
  Pallas kernels  9.41 us (13%)
  other arithmetic  8.51 us (12%)
  waiting for transfers between devices  5.31 us (7%)
  local copies, waits for them, and re-layouts  5.22 us (7%)
  matrix products  3 us (4%)
    all_to_all x1, blocking collectives, local(): lax.all_to_all(state, 'seq', split_axis=1, concat_axis=0, tiled=True)  22.3 us
    all_to_all x1, starting transfers between devices, local(): lax.all_to_all(grouped, 'seq', split_axis=0, concat_axis=0, tiled=True)  16.8 us
    all_to_all x1, waiting for transfers between devices, local(): lax.all_to_all(grouped, 'seq', split_axis=0, concat_axis=0, tiled=True)  5.31 us
    pallas_call x1, Pallas kernels, filter_spectra(): pl.pallas_call(filter_kernel, grid=(orders, per), in_specs=[pl.BlockSpec(...  5.08 us
    pallas_call x1, Pallas kernels, chain(): pl.pallas_call(chain_kernel, grid=(per,), in_specs=[pl.BlockSpec((3, 1, h...  4.33 us
    sin x1, other arithmetic, make_tables(): jnp.sin(big)  1.9 us
    dot_general x1, matrix products, local(): lax.dot_general(returned, w_out, (((0,), (0,)), ((), ())), preferred_elem...  1.79 us
    another operation x2, other arithmetic  1.67 us
  transfers between devices with their start and end apart: 1, of which 1 were waited for; matrix products, arithmetic and copies ran while one was open for 12% of the time, Pallas kernels for 7%

profile of v6, /device:TPU:1, one launch (start us, length us, event | category | flops | bytes accessed | tf_op | source)
XLA Modules:
  0.0 70.9 jit_solution(4458568753271722993)
XLA Ops:
  0.0 0.0 copy-start
  0.0 1.0 %copy-done = bf16[256,768]{1,0:T(8,128)(2,1)S(1)} copy-done((bf16[256,768]{1,0:T(8,128)(2,1)S(1)}, bf16[256,768]{1,0:T(8,128)(2,1)}, u32[]{:S(2)}) %copy-start) | copy-done | bytes 393240
  1.0 1.2 %convolution_convert_fusion = bf16[768,256]{1,0:T(8,128)(2,1)S(1)} fusion(bf16[256,768]{1,0:T(8,128)(2,1)S(1)} %copy-done, bf16[256,256]{1,0:T(8,128)(2,1)} %param.6), kind=kOutput, calls=%fused_computation | convolution fusion | flops 100859904 | bytes 917504 | tf_op jit(solution)/shard_map/dot_general | solution.py:144
  2.2 0.2 reshape.25
  2.4 0.0 copy-start.14
  2.4 1.0 %copy.21 = bf16[128,3,2,256]{3,2,1,0:T(2,128)(2,1)} copy(bf16[128,3,2,256]{3,2,0,1:T(2,128)(2,1)S(1)} %bitcast.15) | data formatting | bytes 786432 | tf_op jit(solution)/shard_map/transpose | solution.py:148
  3.4 16.8 %all-to-all-start = ((bf16[128,3,2,256]{3,2,1,0:T(2,128)(2,1)}), bf16[128,3,2,256]{3,2,1,0:T(2,128)(2,1)}, u32[]{:S(2)}, u32[]{:S(2)}) async-start(bf16[128,3,2,256]{3,2,1,0:T(2,128)(2,1)} %copy.21), calls=%async_computation | async-start | bytes 786432 | tf_op jit(solution)/shard_map/all_to_all | solution.py:151
  20.2 0.0 copy-start.16
  20.3 1.6 %negate_convert_fusion = (bf16[256,256]{1,0:T(8,128)(2,1)}, f32[256,256]{1,0:T(8,128)S(1)}, s32[256,256]{1,0:T(8,128)S(1)}) fusion(s32[256,256]{1,0:T(8,128)S(1)} %iota.10, s32[256,256]{1,0:T(8,128)S(1)} %iota.11), kind=kLoop, calls=%fused_computation.27 | loop fusion | flops 1048576 | bytes 1179648 | tf_op jit(solution)/shard_map/convert.9
  21.9 0.0 copy-start.5
  21.9 0.0 copy-start.9
  22.0 0.0 copy-start.7
  22.0 0.0 copy-start.11
  22.0 0.8 %slice.55 = bf16[128,256]{1,0:T(8,128)(2,1)} slice(bf16[256,256]{1,0:T(8,128)(2,1)S(1)} %get-tuple-element.17), slice={[0:128], [0:256]} | slice | bytes 131072 | tf_op jit(solution)/shard_map/slice | solution.py:48
  22.8 0.0 copy-done.14
  22.8 0.5 reshape.26.filt_ref
  23.2 0.0 copy-done.16
  23.2 0.5 reshape.24
  23.8 0.1 copy.19
  23.9 0.1 copy.20
  24.0 0.1 copy.23
  24.1 0.1 copy.24
  24.2 0.1 copy.25
  24.3 0.1 copy.26
  24.4 1.9 %fusion.7 = (f32[256,256]{1,0:T(8,128)S(1)}, f32[256,256]{1,0:T(8,128)S(1)}, bf16[256,256]{1,0:T(8,128)(2,1)S(1)}, f32[256,256]{1,0:T(8,128)S(1)}) fusion(s32[256,256]{1,0:T(8,128)S(1)} %get-tuple-element.11), kind=kLoop, calls=%fused_computation.19 | loop fusion | flops 1048576 | bytes 1179648 | tf_op jit(solution)/shard_map/sin | solution.py:49
  26.3 0.0 copy-done.9
  26.4 0.0 copy-done.5
  26.4 0.1 maximum_maximum_fusion.rf_ref
  26.5 0.0 copy-done.7
  26.5 0.0 copy-done.11
  26.5 0.0 copy-start.10
  26.5 0.0 copy-start.15
  26.5 0.0 copy-start.6
  26.5 0.0 copy-start.8
  26.5 0.0 copy-start.12
  26.5 0.0 copy-start.13
  26.6 5.1 %shard_map.64.spec_ref = f32[2,2,256,512]{3,2,1,0:T(8,128)S(1)} custom-call(f32[2,2,128,256]{3,2,1,0:T(8,128)S(1)} %reshape.26.filt_ref, f32[512,128]{1,0:T(8,128)S(1)} %pad_maximum_fusion.lf_ref, f32[512,512]{1,0:T(8,128)S(1)} %maximum_maximum_fusion.rf_ref, f32[256,256]{1,0:T(8,128)S(1)} %get-tuple-element.20.twr_ref, f32[256,256]{1,0:T(8,128)S(1)} %get-tuple-element.19.twi_ref), custom_call_target="tpu_custom_call" | custom-call | tf_op jit(solution)/shard_map/pallas_call | solution.py:71
  31.6 0.0 copy-done.10
  31.7 0.7 fusion.11.lf_ref
  32.3 0.0 copy-done.15
  32.3 0.6 pad_maximum_fusion.1.li_ref
  33.0 0.0 copy-done.6
  33.0 0.0 copy-done.8
  33.0 0.0 copy-done.12
  33.0 0.0 copy-done.13
  33.0 0.9 %maximum_maximum_fusion.1 = (bf16[512,512]{1,0:T(8,128)(2,1)S(1)}, bf16[512,512]{1,0:T(8,128)(2,1)}) fusion(bf16[256,256]{1,0:T(8,128)(2,1)S(1)} %get-tuple-element.21, bf16[256,256]{1,0:T(8,128)(2,1)S(1)} %copy-done.12, bf16[256,256]{1,0:T(8,128)(2,1)S(1)} %copy-done.13, f32[256,256]{1,0:T(8,128)S(1)} %get-tuple-element.22, f32[256,256]{1,0:T(8,128)S(1)} %copy-done.8, ...), kind=kLoop, calls=%fused_computation.8 | loop fusion | flops 4194304 | bytes 2228224 | tf_op jit(solution)/shard_map/concatenate | solution.py:45
  33.9 5.3 %all-to-all-done = bf16[128,3,2,256]{3,2,1,0:T(2,128)(2,1)} async-done(((bf16[128,3,2,256]{3,2,1,0:T(2,128)(2,1)}), bf16[128,3,2,256]{3,2,1,0:T(2,128)(2,1)}, u32[]{:S(2)}, u32[]{:S(2)}) %all-to-all-start) | async-done | bytes 393248 | tf_op jit(solution)/shard_map/all_to_all | solution.py:151
  39.2 1.1 %copy_convert_fusion = f32[128,3,2,256]{3,0,2,1:T(8,128)S(1)} fusion(bf16[128,3,2,256]{3,2,1,0:T(2,128)(2,1)} %all-to-all-done), kind=kLoop, calls=%fused_computation.9 | loop fusion | flops 196608 | bytes 1179648 | tf_op jit(solution)/shard_map/convert_element_type | solution.py:155
  40.3 0.2 slice.49
  40.4 0.2 pad_slice_fusion
  40.6 0.0 copy-start.1
  40.6 0.0 copy-start.2
  40.6 0.0 copy-start.3
  40.6 0.0 copy-start.4
  40.7 1.6 %fusion.3.short_ref = bf16[3,2,128,256]{3,2,1,0:T(8,128)(2,1)S(1)} fusion(f32[128,3,2,254]{3,0,2,1:T(8,128)S(1)} %bitcast.13, f32[128,3,2,2]{3,0,2,1:T(8,128)S(1)} %concatenate.37, f32[3,2]{1,0:T(4,128)S(1)} %copy.26, f32[128,3,2,255]{3,0,2,1:T(8,128)S(1)} %bitcast.14, f32[128,3,2,1]{3,0,2,1:T(8,128)S(1)} %pad_slice_fusion, f32[3,2]{1,0:T(4,128)S(1)} %copy.24, ...), kind=kLoop, calls=%fused_computation.13 | loop fusion | flops 1769472 | bytes 2359368 | tf_op jit(solution)/shard_map/transpose | solution.py:162
  42.2 0.0 copy-done.1
  42.3 0.0 copy-done.2
  42.3 0.0 copy-done.3
  42.3 0.0 copy-done.4
  42.3 4.3 %shard_map.65 = bf16[2,128,256]{2,1,0:T(8,128)(2,1)S(1)} custom-call(bf16[3,2,128,256]{3,2,1,0:T(8,128)(2,1)S(1)} %fusion.3.short_ref, f32[2,2,256,512]{3,2,1,0:T(8,128)S(1)} %shard_map.64.spec_ref, f32[2,2]{1,0:T(2,128)S(1)} %copy-done.4, bf16[512,128]{1,0:T(8,128)(2,1)S(1)} %copy-done.2, bf16[512,512]{1,0:T(8,128)(2,1)S(1)} %copy-done.1, ...), custom_call_target="tpu_custom_call" | custom-call | tf_op jit(solution)/shard_map/pallas_call | solution.py:120
  46.6 0.1 copy.27
  46.8 22.3 %all_to_all.21 = bf16[2,128,256]{2,0,1:T(2,128)(2,1)S(1)} all-to-all(bf16[2,128,256]{2,0,1:T(2,128)(2,1)S(1)} %copy.27), channel_id=1, replica_groups=mesh['win'=2,'seq'=128] {'seq'}, dimensions={1} | all-to-all | bytes 262144 | tf_op jit(solution)/shard_map/all_to_all | solution.py:170
  69.1 0.1 all_to_all.18
  69.1 1.8 %convolution_convert_fusion.1 = bf16[256,256]{1,0:T(8,128)(2,1)} fusion(bf16[256,256]{1,0:T(8,128)(2,1)S(1)} %all_to_all.18, bf16[256,256]{1,0:T(8,128)(2,1)} %param.11), kind=kOutput, calls=%fused_computation.1 | convolution fusion | flops 33619968 | bytes 393216 | tf_op jit(solution)/shard_map/dot_general | solution.py:171
  (9 shorter events, 0.2 us)
Async XLA Ops:
  0.0 1.0 %copy-start = (bf16[256,768]{1,0:T(8,128)(2,1)S(1)}, bf16[256,768]{1,0:T(8,128)(2,1)}, u32[]{:S(2)}) copy-start(bf16[256,768]{1,0:T(8,128)(2,1)} %param.7) | copy-start | bytes 1179652
  2.4 20.4 %copy-start.14 = (f32[2,2,32768]{2,1,0:T(2,128)S(1)}, f32[2,2,32768]{2,1,0:T(2,128)}, u32[]{:S(2)}) copy-start(f32[2,2,32768]{2,1,0:T(2,128)} %param.9) | copy-start | bytes 1572868
  3.4 35.8 %all-to-all-start = ((bf16[128,3,2,256]{3,2,1,0:T(2,128)(2,1)}), bf16[128,3,2,256]{3,2,1,0:T(2,128)(2,1)}, u32[]{:S(2)}, u32[]{:S(2)}) async-start(bf16[128,3,2,256]{3,2,1,0:T(2,128)(2,1)} %copy.21), calls=%async_computation | async-start | bytes 786432 | tf_op jit(solution)/shard_map/all_to_all | solution.py:151
  20.2 3.0 %copy-start.16 = (f32[3,768]{1,0:T(4,128)S(1)}, f32[3,768]{1,0:T(4,128)}, u32[]{:S(2)}) copy-start(f32[3,768]{1,0:T(4,128)} %param.8) | copy-start | bytes 27652
  21.9 4.4 %copy-start.5 = (f32[256,256]{1,0:T(8,128)}, f32[256,256]{1,0:T(8,128)S(1)}, u32[]{:S(2)}) copy-start(f32[256,256]{1,0:T(8,128)S(1)} %get-tuple-element.10) | copy-start | bytes 786436
  21.9 4.4 %copy-start.9 = (f32[256,128]{1,0:T(8,128)}, f32[256,128]{1,0:T(8,128)S(1)}, u32[]{:S(2)}) copy-start(f32[256,128]{1,0:T(8,128)S(1)} %slice.53) | copy-start | bytes 393220
  22.0 4.5 %copy-start.7 = (f32[256,256]{1,0:T(8,128)}, f32[256,256]{1,0:T(8,128)S(1)}, u32[]{:S(2)}) copy-start(f32[256,256]{1,0:T(8,128)S(1)} %get-tuple-element.18) | copy-start | bytes 786436
  22.0 4.5 %copy-start.11 = (bf16[256,256]{1,0:T(8,128)(2,1)}, bf16[256,256]{1,0:T(8,128)(2,1)S(1)}, u32[]{:S(2)}) copy-start(bf16[256,256]{1,0:T(8,128)(2,1)S(1)} %get-tuple-element.17) | copy-start | bytes 393220
  26.5 5.2 %copy-start.10 = (f32[256,128]{1,0:T(8,128)S(1)}, f32[256,128]{1,0:T(8,128)}, u32[]{:S(2)}) copy-start(f32[256,128]{1,0:T(8,128)} %copy-done.9) | copy-start | bytes 393220
  26.5 5.8 %copy-start.15 = (bf16[128,256]{1,0:T(8,128)(2,1)S(1)}, bf16[128,256]{1,0:T(8,128)(2,1)}, u32[]{:S(2)}) copy-start(bf16[128,256]{1,0:T(8,128)(2,1)} %slice.55) | copy-start | bytes 196612
  26.5 6.5 %copy-start.6 = (f32[256,256]{1,0:T(8,128)S(1)}, f32[256,256]{1,0:T(8,128)}, u32[]{:S(2)}) copy-start(f32[256,256]{1,0:T(8,128)} %copy-done.5) | copy-start | bytes 786436
  26.5 6.5 %copy-start.8 = (f32[256,256]{1,0:T(8,128)S(1)}, f32[256,256]{1,0:T(8,128)}, u32[]{:S(2)}) copy-start(f32[256,256]{1,0:T(8,128)} %copy-done.7) | copy-start | bytes 786436
  26.5 6.4 %copy-start.12 = (bf16[256,256]{1,0:T(8,128)(2,1)S(1)}, bf16[256,256]{1,0:T(8,128)(2,1)}, u32[]{:S(2)}) copy-start(bf16[256,256]{1,0:T(8,128)(2,1)} %copy-done.11) | copy-start | bytes 393220
  26.5 6.4 %copy-start.13 = (bf16[256,256]{1,0:T(8,128)(2,1)S(1)}, bf16[256,256]{1,0:T(8,128)(2,1)}, u32[]{:S(2)}) copy-start(bf16[256,256]{1,0:T(8,128)(2,1)} %get-tuple-element.9) | copy-start | bytes 393220
  40.6 1.7 %copy-start.1 = (bf16[512,512]{1,0:T(8,128)(2,1)S(1)}, bf16[512,512]{1,0:T(8,128)(2,1)}, u32[]{:S(2)}) copy-start(bf16[512,512]{1,0:T(8,128)(2,1)} %get-tuple-element.24.rf_ref) | copy-start | bytes 1572868
  40.6 1.7 %copy-start.2 = (bf16[512,128]{1,0:T(8,128)(2,1)S(1)}, bf16[512,128]{1,0:T(8,128)(2,1)}, u32[]{:S(2)}) copy-start(bf16[512,128]{1,0:T(8,128)(2,1)} %fusion.11.lf_ref) | copy-start | bytes 393220
  40.6 1.7 %copy-start.3 = (bf16[128,512]{1,0:T(8,128)(2,1)S(1)}, bf16[128,512]{1,0:T(8,128)(2,1)}, u32[]{:S(2)}) copy-start(bf16[128,512]{1,0:T(8,128)(2,1)} %pad_maximum_fusion.1.li_ref) | copy-start | bytes 393220
  40.6 1.7 %copy-start.4 = (f32[2,2]{1,0:T(2,128)S(1)}, f32[2,2]{1,0:T(2,128)}, u32[]{:S(2)}) copy-start(f32[2,2]{1,0:T(2,128)} %bias_ref.1) | copy-start | bytes 52

commit v7 on v2

--- a/solution.py
+++ b/solution.py
@@ -46,7 +46,7 @@
         [jnp.concatenate([f_re, -f_im], 1), jnp.concatenate([f_im, f_re], 1)], 0
     )
     left_inv = jnp.concatenate([f_re[:half], f_im[:half]], 1)
-    return left_fwd, right_fwd, right_inv, left_inv, jnp.cos(big), jnp.sin(big)
+    return left_fwd, right_fwd, right_inv, left_inv, jnp.cos(big), jnp.sin(big), f_re, f_im
 
 
 def spectrum(rows_in, left_fwd, right_fwd, tw_re, tw_im, mul):
@@ -64,7 +64,7 @@
 
 
 def filter_spectra(filters, tabs):
-    left_fwd, right_fwd, _, _, tw_re, tw_im = tabs
+    left_fwd, right_fwd, _, _, tw_re, tw_im = tabs[:6]
     orders, per = filters.shape[:2]
     half = SIDE // 2
     full = lambda shape: pl.BlockSpec(shape, lambda o, c: (0,) * len(shape))
@@ -101,9 +101,19 @@
     return (back * scale + bias * signal).astype(jnp.bfloat16)
 
 
-def chain_kernel(short_ref, spec_ref, bias_ref, lf_ref, rf_ref, ri_ref, li_ref, twr_ref, twi_ref, out_ref):
+def chain_kernel(short_ref, spec_ref, bias_ref, fr_ref, fi_ref, twr_ref, twi_ref, out_ref):
     channel = pl.program_id(0)
-    tabs = (lf_ref[...], rf_ref[...], ri_ref[...], li_ref[...], twr_ref[...], twi_ref[...])
+    half = SIDE // 2
+    f_re, f_im = fr_ref[...], fi_ref[...]
+    left_fwd = jnp.concatenate([f_re[:, :half], f_im[:, :half]], 0)
+    right_fwd = jnp.concatenate(
+        [jnp.concatenate([f_re, f_im], 1), jnp.concatenate([-f_im, f_re], 1)], 0
+    )
+    right_inv = jnp.concatenate(
+        [jnp.concatenate([f_re, -f_im], 1), jnp.concatenate([f_im, f_re], 1)], 0
+    )
+    left_inv = jnp.concatenate([f_re[:half], f_im[:half]], 1)
+    tabs = (left_fwd, right_fwd, right_inv, left_inv, twr_ref[...], twi_ref[...])
     state = short_ref[2, 0]
     for order in range(2):
         conv = convolve(state, spec_ref[order, 0], bias_ref[order, channel], tabs)
@@ -114,8 +124,7 @@
 def chain(short, spectra, bias, tabs):
     per = short.shape[1]
     half = SIDE // 2
-    left_fwd, right_fwd, right_inv, left_inv, tw_re, tw_im = tabs
-    low = lambda t: t.astype(jnp.bfloat16)
+    tw_re, tw_im, f_re, f_im = tabs[4:]
     full = lambda shape: pl.BlockSpec(shape, lambda c: (0,) * len(shape))
     return pl.pallas_call(
         chain_kernel,
@@ -124,17 +133,15 @@
             pl.BlockSpec((3, 1, half, SIDE), lambda c: (0, c, 0, 0)),
             pl.BlockSpec((2, 1, SIDE, 2 * SIDE), lambda c: (0, c, 0, 0)),
             pl.BlockSpec(memory_space=pltpu.SMEM),
-            full((2 * SIDE, half)),
-            full((2 * SIDE, 2 * SIDE)),
-            full((2 * SIDE, 2 * SIDE)),
-            full((half, 2 * SIDE)),
+            full((SIDE, SIDE)),
+            full((SIDE, SIDE)),
             full((SIDE, SIDE)),
             full((SIDE, SIDE)),
         ],
         out_specs=pl.BlockSpec((1, half, SIDE), lambda c: (c, 0, 0)),
         out_shape=jax.ShapeDtypeStruct((per, half, SIDE), jnp.bfloat16),
         compiler_params=pltpu.CompilerParams(vmem_limit_bytes=48 * 1024 * 1024),
-    )(short, spectra, bias, low(left_fwd), low(right_fwd), low(right_inv), low(left_inv), tw_re, tw_im)
+    )(short, spectra, bias, f_re.astype(jnp.bfloat16), f_im.astype(jnp.bfloat16), tw_re, tw_im)
 
 
 def local(layer_input, w_in, short_w, filters, filter_bias, w_out):

time: 69.5 us -> 68.3 us (0.983)
  waiting for transfers between devices: 8.97 us -> 10.8 us
  other arithmetic: 7.75 us -> 6.04 us
  matrix products: 3 us -> 2.1 us
    all_to_all x1, waiting for transfers between devices: 8.97 us -> 10.8 us  [local(): lax.all_to_all(grouped.reshape(groups, 3 * per, positions), 'seq', split_...]
    another operation x2 -> x0, other arithmetic: 1.67 us -> none
    concatenate x2 -> x0, other arithmetic: 1.59 us -> none  [the longest x1 0.91 us: make_tables(): jnp.concatenate([jnp.concatenate([f_re, -f_im], 1), jnp.concatenate([f_im...]
    convert_element_type x1, other arithmetic: 0.66 us -> 1.63 us  [chain(): f_im.astype(jnp.bfloat16)]
    dot_general x1, matrix products: 1.79 us -> 0.89 us  [local(): lax.dot_general(returned, w_out, (((0,), (0,)), ((), ())), preferred_elem...]
  transfers between devices with their start and end apart: 1 -> 1, of which waited for: 1 -> 1; matrix products, arithmetic and copies ran while one was open for 11% -> 8% of each run, Pallas kernels for 7% -> 7%
where the time goes in v7:
time: 68.3 us; the launch traced here: 68.1 us
  blocking collectives  18.8 us (28%)
  starting transfers between devices  16.8 us (25%)
  waiting for transfers between devices  10.8 us (16%)
  Pallas kernels  9.34 us (14%)
  other arithmetic  6.04 us (9%)
  local copies, waits for them, and re-layouts  3.84 us (6%)
  matrix products  2.1 us (3%)
    all_to_all x1, blocking collectives, local(): lax.all_to_all(state, 'seq', split_axis=1, concat_axis=0, tiled=True)  18.8 us
    all_to_all x1, starting transfers between devices, local(): lax.all_to_all(grouped.reshape(groups, 3 * per, positions), 'seq', split_...  16.8 us
    all_to_all x1, waiting for transfers between devices, local(): lax.all_to_all(grouped.reshape(groups, 3 * per, positions), 'seq', split_...  10.8 us
    pallas_call x1, Pallas kernels, filter_spectra(): pl.pallas_call(filter_kernel, grid=(orders, per), in_specs=[pl.BlockSpec(...  5.08 us
    pallas_call x1, Pallas kernels, chain(): pl.pallas_call(chain_kernel, grid=(per,), in_specs=[pl.BlockSpec((3, 1, h...  4.26 us
    sin x1, other arithmetic, make_tables(): jnp.sin(big)  2.54 us
    convert_element_type x1, other arithmetic, chain(): f_im.astype(jnp.bfloat16)  1.63 us
  transfers between devices with their start and end apart: 1, of which 1 were waited for; matrix products, arithmetic and copies ran while one was open for 8% of the time, Pallas kernels for 7%

profile of v7, /device:TPU:1, one launch (start us, length us, event | category | flops | bytes accessed | tf_op | source)
XLA Modules:
  0.0 68.1 jit_solution(1557933795148075626)
XLA Ops:
  0.0 0.0 copy-start
  0.0 1.0 %copy-done = bf16[256,768]{1,0:T(8,128)(2,1)S(1)} copy-done((bf16[256,768]{1,0:T(8,128)(2,1)S(1)}, bf16[256,768]{1,0:T(8,128)(2,1)}, u32[]{:S(2)}) %copy-start) | copy-done | bytes 393240
  1.0 1.2 %convolution_convert_fusion = bf16[768,256]{1,0:T(8,128)(2,1)S(1)} fusion(bf16[256,768]{1,0:T(8,128)(2,1)S(1)} %copy-done, bf16[256,256]{1,0:T(8,128)(2,1)} %param.6), kind=kOutput, calls=%fused_computation | convolution fusion | flops 100859904 | bytes 917504 | tf_op jit(solution)/shard_map/dot_general | solution.py:151
  2.2 0.2 reshape.37
  2.4 1.0 %copy.11 = bf16[128,6,256]{2,1,0:T(8,128)(2,1)} copy(bf16[128,6,256]{2,0,1:T(8,128)(2,1)S(1)} %bitcast.20) | data formatting | bytes 786432 | tf_op jit(solution)/shard_map/reshape | solution.py:159
  3.4 16.8 %all-to-all-start = ((bf16[128,6,256]{2,1,0:T(8,128)(2,1)}), bf16[128,6,256]{2,1,0:T(8,128)(2,1)}, u32[]{:S(2)}, u32[]{:S(2)}) async-start(bf16[128,6,256]{2,1,0:T(8,128)(2,1)} %copy.11), calls=%async_computation | async-start | bytes 1048576 | tf_op jit(solution)/shard_map/all_to_all | solution.py:158
  20.3 0.0 copy-start.4
  20.4 0.0 copy-start.6
  20.4 1.6 %fusion.7 = (bf16[256,256]{1,0:T(8,128)(2,1)}, f32[256,256]{1,0:T(8,128)S(1)}, s32[256,256]{1,0:T(8,128)S(1)}) fusion(s32[256,256]{1,0:T(8,128)S(1)} %iota.10, s32[256,256]{1,0:T(8,128)S(1)} %iota.11), kind=kLoop, calls=%fused_computation.20 | loop fusion | flops 983040 | bytes 1179648 | tf_op jit(solution)/shard_map/convert_element_type | solution.py:144
  22.0 2.5 %fusion.3 = (f32[256,256]{1,0:T(8,128)S(1)}, f32[256,256]{1,0:T(8,128)S(1)}, bf16[256,256]{1,0:T(8,128)(2,1)}, f32[256,256]{1,0:T(8,128)S(1)}) fusion(s32[256,256]{1,0:T(8,128)S(1)} %get-tuple-element.14), kind=kLoop, calls=%fused_computation.13 | loop fusion | flops 1048576 | bytes 1179648 | tf_op jit(solution)/shard_map/sin | solution.py:49
  24.6 0.0 copy-done.4
  24.6 0.5 reshape.40.filt_ref
  25.1 0.0 copy-done.6
  25.1 0.5 reshape.36
  25.7 0.1 mul.46
  25.7 0.1 mul.49
  25.8 0.1 mul.52
  25.9 0.1 maximum_maximum_fusion.rf_ref
  26.0 5.1 %shard_map.64.spec_ref = f32[2,2,256,512]{3,2,1,0:T(8,128)S(1)} custom-call(f32[2,2,128,256]{3,2,1,0:T(8,128)S(1)} %reshape.40.filt_ref, f32[512,128]{1,0:T(8,128)S(1)} %pad_maximum_fusion.lf_ref, f32[512,512]{1,0:T(8,128)S(1)} %maximum_maximum_fusion.rf_ref, f32[256,256]{1,0:T(8,128)S(1)} %get-tuple-element.18.twr_ref, f32[256,256]{1,0:T(8,128)S(1)} %get-tuple-element.17.twi_ref), custom_call_target="tpu_custom_call" | custom-call | tf_op jit(solution)/shard_map/pallas_call | solution.py:71
  31.1 0.0 copy-start.1
  31.1 0.0 copy-start.2
  31.2 0.0 copy-start.3
  31.2 10.8 %all-to-all-done = bf16[128,6,256]{2,1,0:T(8,128)(2,1)} async-done(((bf16[128,6,256]{2,1,0:T(8,128)(2,1)}), bf16[128,6,256]{2,1,0:T(8,128)(2,1)}, u32[]{:S(2)}, u32[]{:S(2)}) %all-to-all-start) | async-done | bytes 393248 | tf_op jit(solution)/shard_map/all_to_all | solution.py:158
  42.0 1.1 %bitcast_convert_fusion = f32[128,1,6,256]{3,2,0,1:T(8,128)S(1)} fusion(bf16[128,6,256]{2,1,0:T(8,128)(2,1)} %all-to-all-done), kind=kLoop, calls=%fused_computation.4 | loop fusion | flops 196608 | bytes 1179648 | tf_op jit(solution)/shard_map/convert_element_type | solution.py:164
  43.1 0.6 add_convert_fusion
  43.7 0.1 copy.13
  43.8 0.0 copy-done.1
  43.8 0.0 copy-done.2
  43.8 0.0 copy-done.3
  43.8 0.0 copy-start.5
  43.8 4.3 %shard_map.65 = bf16[2,128,256]{2,1,0:T(8,128)(2,1)S(1)} custom-call(bf16[3,2,128,256]{3,2,1,0:T(8,128)(2,1)S(1)} %bitcast.17, f32[2,2,256,512]{3,2,1,0:T(8,128)S(1)} %shard_map.64.spec_ref, f32[2,2]{1,0:T(2,128)S(1)} %copy-done.3, bf16[256,256]{1,0:T(8,128)(2,1)S(1)} %copy-done.2, bf16[256,256]{1,0:T(8,128)(2,1)S(1)} %copy-done.1, ...), custom_call_target="tpu_custom_call" | custom-call | tf_op jit(solution)/shard_map/pallas_call | solution.py:129
  48.1 0.1 copy.12
  48.2 18.8 %all_to_all.25 = bf16[2,128,256]{2,0,1:T(2,128)(2,1)S(1)} all-to-all(bf16[2,128,256]{2,0,1:T(2,128)(2,1)S(1)} %copy.12), channel_id=1, replica_groups=mesh['win'=2,'seq'=128] {'seq'}, dimensions={1} | all-to-all | bytes 262144 | tf_op jit(solution)/shard_map/all_to_all | solution.py:178
  67.1 0.1 all_to_all.22
  67.2 0.0 copy-done.5
  67.2 0.9 %convolution_convert_fusion.1 = bf16[256,256]{1,0:T(8,128)(2,1)} fusion(bf16[256,256]{1,0:T(8,128)(2,1)S(1)} %all_to_all.22, bf16[256,256]{1,0:T(8,128)(2,1)S(1)} %copy-done.5), kind=kOutput, calls=%fused_computation.1 | convolution fusion | flops 33619968 | bytes 393216 | tf_op jit(solution)/shard_map/dot_general | solution.py:179
  (8 shorter events, 0.2 us)
Async XLA Ops:
  0.0 1.0 %copy-start = (bf16[256,768]{1,0:T(8,128)(2,1)S(1)}, bf16[256,768]{1,0:T(8,128)(2,1)}, u32[]{:S(2)}) copy-start(bf16[256,768]{1,0:T(8,128)(2,1)} %param.7) | copy-start | bytes 1179652
  3.4 38.5 %all-to-all-start = ((bf16[128,6,256]{2,1,0:T(8,128)(2,1)}), bf16[128,6,256]{2,1,0:T(8,128)(2,1)}, u32[]{:S(2)}, u32[]{:S(2)}) async-start(bf16[128,6,256]{2,1,0:T(8,128)(2,1)} %copy.11), calls=%async_computation | async-start | bytes 1048576 | tf_op jit(solution)/shard_map/all_to_all | solution.py:158
  20.3 4.3 %copy-start.4 = (f32[2,2,32768]{2,1,0:T(2,128)S(1)}, f32[2,2,32768]{2,1,0:T(2,128)}, u32[]{:S(2)}) copy-start(f32[2,2,32768]{2,1,0:T(2,128)} %param.9) | copy-start | bytes 1572868
  20.4 4.7 %copy-start.6 = (f32[3,768]{1,0:T(4,128)S(1)}, f32[3,768]{1,0:T(4,128)}, u32[]{:S(2)}) copy-start(f32[3,768]{1,0:T(4,128)} %param.8) | copy-start | bytes 27652
  31.1 12.7 %copy-start.1 = (bf16[256,256]{1,0:T(8,128)(2,1)S(1)}, bf16[256,256]{1,0:T(8,128)(2,1)}, u32[]{:S(2)}) copy-start(bf16[256,256]{1,0:T(8,128)(2,1)} %get-tuple-element.12.fi_ref) | copy-start | bytes 393220
  31.1 12.7 %copy-start.2 = (bf16[256,256]{1,0:T(8,128)(2,1)S(1)}, bf16[256,256]{1,0:T(8,128)(2,1)}, u32[]{:S(2)}) copy-start(bf16[256,256]{1,0:T(8,128)(2,1)} %get-tuple-element.19.fr_ref) | copy-start | bytes 393220
  31.2 12.7 %copy-start.3 = (f32[2,2]{1,0:T(2,128)S(1)}, f32[2,2]{1,0:T(2,128)}, u32[]{:S(2)}) copy-start(f32[2,2]{1,0:T(2,128)} %bias_ref.1) | copy-start | bytes 52
  43.8 23.3 %copy-start.5 = (bf16[256,256]{1,0:T(8,128)(2,1)S(1)}, bf16[256,256]{1,0:T(8,128)(2,1)}, u32[]{:S(2)}) copy-start(bf16[256,256]{1,0:T(8,128)(2,1)} %param.11) | copy-start | bytes 393220

commit v8 on v7

--- a/solution.py
+++ b/solution.py
@@ -57,14 +57,20 @@
     return mul(jnp.concatenate([t_re, t_im], 1), right_fwd)
 
 
-def filter_kernel(filt_ref, lf_ref, rf_ref, twr_ref, twi_ref, out_ref):
+def filter_kernel(filt_ref, fr_ref, fi_ref, twr_ref, twi_ref, out_ref):
+    half = SIDE // 2
+    f_re, f_im = fr_ref[...], fi_ref[...]
+    left_fwd = jnp.concatenate([f_re[:, :half], f_im[:, :half]], 0)
+    right_fwd = jnp.concatenate(
+        [jnp.concatenate([f_re, f_im], 1), jnp.concatenate([-f_im, f_re], 1)], 0
+    )
     out_ref[0, 0] = spectrum(
-        filt_ref[0, 0], lf_ref[...], rf_ref[...], twr_ref[...], twi_ref[...], product
+        filt_ref[0, 0], left_fwd, right_fwd, twr_ref[...], twi_ref[...], product
     )
 
 
 def filter_spectra(filters, tabs):
-    left_fwd, right_fwd, _, _, tw_re, tw_im = tabs[:6]
+    tw_re, tw_im, f_re, f_im = tabs[4:]
     orders, per = filters.shape[:2]
     half = SIDE // 2
     full = lambda shape: pl.BlockSpec(shape, lambda o, c: (0,) * len(shape))
@@ -73,15 +79,15 @@
         grid=(orders, per),
         in_specs=[
             pl.BlockSpec((1, 1, half, SIDE), lambda o, c: (o, c, 0, 0)),
-            full((2 * SIDE, half)),
-            full((2 * SIDE, 2 * SIDE)),
+            full((SIDE, SIDE)),
+            full((SIDE, SIDE)),
             full((SIDE, SIDE)),
             full((SIDE, SIDE)),
         ],
         out_specs=pl.BlockSpec((1, 1, SIDE, 2 * SIDE), lambda o, c: (o, c, 0, 0)),
         out_shape=jax.ShapeDtypeStruct((orders, per, SIDE, 2 * SIDE), jnp.float32),
         compiler_params=pltpu.CompilerParams(vmem_limit_bytes=48 * 1024 * 1024),
-    )(filters, left_fwd, right_fwd, tw_re, tw_im)
+    )(filters, f_re, f_im, tw_re, tw_im)
 
 
 def convolve(sig, f_spec, bias, tabs):

time: 68.3 us -> 68.4 us (level)
  transfers between devices with their start and end apart: 1 -> 1, of which waited for: 1 -> 1; matrix products, arithmetic and copies ran while one was open for 8% -> 8% of each run, Pallas kernels for 7% -> 8%
where the time goes in v8:
time: 68.4 us; the launch traced here: 68.1 us
  blocking collectives  18.9 us (28%)
  starting transfers between devices  16.8 us (25%)
  waiting for transfers between devices  11 us (16%)
  Pallas kernels  9.37 us (14%)
  other arithmetic  5.89 us (9%)
  local copies, waits for them, and re-layouts  3.82 us (6%)
  matrix products  2.1 us (3%)
    all_to_all x1, blocking collectives, local(): lax.all_to_all(state, 'seq', split_axis=1, concat_axis=0, tiled=True)  18.9 us
    all_to_all x1, starting transfers between devices, local(): lax.all_to_all(grouped.reshape(groups, 3 * per, positions), 'seq', split_...  16.8 us
    all_to_all x1, waiting for transfers between devices, local(): lax.all_to_all(grouped.reshape(groups, 3 * per, positions), 'seq', split_...  11 us
    pallas_call x1, Pallas kernels, filter_spectra(): pl.pallas_call(filter_kernel, grid=(orders, per), in_specs=[pl.BlockSpec(...  5.11 us
    pallas_call x1, Pallas kernels, chain(): pl.pallas_call(chain_kernel, grid=(per,), in_specs=[pl.BlockSpec((3, 1, h...  4.25 us
    sin x1, other arithmetic, make_tables(): jnp.sin(big)  2.52 us
    convert_element_type x1, other arithmetic, chain(): f_im.astype(jnp.bfloat16)  1.63 us
  transfers between devices with their start and end apart: 1, of which 1 were waited for; matrix products, arithmetic and copies ran while one was open for 8% of the time, Pallas kernels for 8%

profile of v8, /device:TPU:1, one launch (start us, length us, event | category | flops | bytes accessed | tf_op | source)
XLA Modules:
  0.0 68.1 jit_solution(16455693508589612290)
XLA Ops:
  0.0 0.0 copy-start
  0.0 1.0 %copy-done = bf16[256,768]{1,0:T(8,128)(2,1)S(1)} copy-done((bf16[256,768]{1,0:T(8,128)(2,1)S(1)}, bf16[256,768]{1,0:T(8,128)(2,1)}, u32[]{:S(2)}) %copy-start) | copy-done | bytes 393240
  1.0 1.2 %convolution_convert_fusion = bf16[768,256]{1,0:T(8,128)(2,1)S(1)} fusion(bf16[256,768]{1,0:T(8,128)(2,1)S(1)} %copy-done, bf16[256,256]{1,0:T(8,128)(2,1)} %param.6), kind=kOutput, calls=%fused_computation | convolution fusion | flops 100859904 | bytes 917504 | tf_op jit(solution)/shard_map/dot_general | solution.py:157
  2.2 0.0 copy-start.4
  2.2 0.2 reshape.37
  2.4 0.0 copy-start.6
  2.4 1.0 %copy.11 = bf16[128,6,256]{2,1,0:T(8,128)(2,1)} copy(bf16[128,6,256]{2,0,1:T(8,128)(2,1)S(1)} %bitcast.20) | data formatting | bytes 786432 | tf_op jit(solution)/shard_map/reshape | solution.py:165
  3.5 16.8 %all-to-all-start = ((bf16[128,6,256]{2,1,0:T(8,128)(2,1)}), bf16[128,6,256]{2,1,0:T(8,128)(2,1)}, u32[]{:S(2)}, u32[]{:S(2)}) async-start(bf16[128,6,256]{2,1,0:T(8,128)(2,1)} %copy.11), calls=%async_computation | async-start | bytes 1048576 | tf_op jit(solution)/shard_map/all_to_all | solution.py:164
  20.4 0.0 copy-done.4
  20.4 0.5 reshape.40.filt_ref
  20.8 0.0 copy-done.6
  20.8 0.5 reshape.36
  21.4 0.1 mul.46
  21.5 0.1 mul.49
  21.6 0.1 mul.52
  21.7 1.6 %fusion.7 = (bf16[256,256]{1,0:T(8,128)(2,1)}, f32[256,256]{1,0:T(8,128)S(1)}, s32[256,256]{1,0:T(8,128)S(1)}) fusion(s32[256,256]{1,0:T(8,128)S(1)} %iota.10, s32[256,256]{1,0:T(8,128)S(1)} %iota.11), kind=kLoop, calls=%fused_computation.18 | loop fusion | flops 983040 | bytes 1179648 | tf_op jit(solution)/shard_map/convert_element_type | solution.py:150
  23.3 2.5 %fusion.3 = (f32[256,256]{1,0:T(8,128)S(1)}, f32[256,256]{1,0:T(8,128)S(1)}, bf16[256,256]{1,0:T(8,128)(2,1)}, f32[256,256]{1,0:T(8,128)S(1)}) fusion(s32[256,256]{1,0:T(8,128)S(1)} %get-tuple-element.14), kind=kLoop, calls=%fused_computation.11 | loop fusion | flops 1048576 | bytes 1179648 | tf_op jit(solution)/shard_map/sin | solution.py:49
  25.8 5.1 %shard_map.64.spec_ref = f32[2,2,256,512]{3,2,1,0:T(8,128)S(1)} custom-call(f32[2,2,128,256]{3,2,1,0:T(8,128)S(1)} %reshape.40.filt_ref, f32[256,256]{1,0:T(8,128)S(1)} %get-tuple-element.20.fr_ref, f32[256,256]{1,0:T(8,128)S(1)} %get-tuple-element.13.fi_ref, f32[256,256]{1,0:T(8,128)S(1)} %get-tuple-element.18.twr_ref, f32[256,256]{1,0:T(8,128)S(1)} %get-tuple-element.17.twi_ref), custom_call_target="tpu_custom_call" | custom-call | tf_op jit(solution)/shard_map/pallas_call | solution.py:77
  31.0 0.0 copy-start.1
  31.0 0.0 copy-start.2
  31.0 0.0 copy-start.3
  31.0 11.0 %all-to-all-done = bf16[128,6,256]{2,1,0:T(8,128)(2,1)} async-done(((bf16[128,6,256]{2,1,0:T(8,128)(2,1)}), bf16[128,6,256]{2,1,0:T(8,128)(2,1)}, u32[]{:S(2)}, u32[]{:S(2)}) %all-to-all-start) | async-done | bytes 393248 | tf_op jit(solution)/shard_map/all_to_all | solution.py:164
  42.0 1.1 %bitcast_convert_fusion = f32[128,1,6,256]{3,2,0,1:T(8,128)S(1)} fusion(bf16[128,6,256]{2,1,0:T(8,128)(2,1)} %all-to-all-done), kind=kLoop, calls=%fused_computation.3 | loop fusion | flops 196608 | bytes 1179648 | tf_op jit(solution)/shard_map/convert_element_type | solution.py:170
  43.1 0.6 add_convert_fusion
  43.7 0.1 copy.13
  43.8 0.0 copy-done.1
  43.8 0.0 copy-done.2
  43.8 0.0 copy-done.3
  43.8 0.0 copy-start.5
  43.9 4.3 %shard_map.65 = bf16[2,128,256]{2,1,0:T(8,128)(2,1)S(1)} custom-call(bf16[3,2,128,256]{3,2,1,0:T(8,128)(2,1)S(1)} %bitcast.17, f32[2,2,256,512]{3,2,1,0:T(8,128)S(1)} %shard_map.64.spec_ref, f32[2,2]{1,0:T(2,128)S(1)} %copy-done.3, bf16[256,256]{1,0:T(8,128)(2,1)S(1)} %copy-done.2, bf16[256,256]{1,0:T(8,128)(2,1)S(1)} %copy-done.1, ...), custom_call_target="tpu_custom_call" | custom-call | tf_op jit(solution)/shard_map/pallas_call | solution.py:135
  48.1 0.1 copy.12
  48.3 18.9 %all_to_all.25 = bf16[2,128,256]{2,0,1:T(2,128)(2,1)S(1)} all-to-all(bf16[2,128,256]{2,0,1:T(2,128)(2,1)S(1)} %copy.12), channel_id=1, replica_groups=mesh['win'=2,'seq'=128] {'seq'}, dimensions={1} | all-to-all | bytes 262144 | tf_op jit(solution)/shard_map/all_to_all | solution.py:184
  67.1 0.1 all_to_all.22
  67.2 0.0 copy-done.5
  67.2 0.9 %convolution_convert_fusion.1 = bf16[256,256]{1,0:T(8,128)(2,1)} fusion(bf16[256,256]{1,0:T(8,128)(2,1)S(1)} %all_to_all.22, bf16[256,256]{1,0:T(8,128)(2,1)S(1)} %copy-done.5), kind=kOutput, calls=%fused_computation.1 | convolution fusion | flops 33619968 | bytes 393216 | tf_op jit(solution)/shard_map/dot_general | solution.py:185
  (4 shorter events, 0.1 us)
Async XLA Ops:
  0.0 1.0 %copy-start = (bf16[256,768]{1,0:T(8,128)(2,1)S(1)}, bf16[256,768]{1,0:T(8,128)(2,1)}, u32[]{:S(2)}) copy-start(bf16[256,768]{1,0:T(8,128)(2,1)} %param.7) | copy-start | bytes 1179652
  2.2 18.2 %copy-start.4 = (f32[2,2,32768]{2,1,0:T(2,128)S(1)}, f32[2,2,32768]{2,1,0:T(2,128)}, u32[]{:S(2)}) copy-start(f32[2,2,32768]{2,1,0:T(2,128)} %param.9) | copy-start | bytes 1572868
  2.4 18.5 %copy-start.6 = (f32[3,768]{1,0:T(4,128)S(1)}, f32[3,768]{1,0:T(4,128)}, u32[]{:S(2)}) copy-start(f32[3,768]{1,0:T(4,128)} %param.8) | copy-start | bytes 27652
  3.5 38.5 %all-to-all-start = ((bf16[128,6,256]{2,1,0:T(8,128)(2,1)}), bf16[128,6,256]{2,1,0:T(8,128)(2,1)}, u32[]{:S(2)}, u32[]{:S(2)}) async-start(bf16[128,6,256]{2,1,0:T(8,128)(2,1)} %copy.11), calls=%async_computation | async-start | bytes 1048576 | tf_op jit(solution)/shard_map/all_to_all | solution.py:164
  31.0 12.9 %copy-start.1 = (bf16[256,256]{1,0:T(8,128)(2,1)S(1)}, bf16[256,256]{1,0:T(8,128)(2,1)}, u32[]{:S(2)}) copy-start(bf16[256,256]{1,0:T(8,128)(2,1)} %get-tuple-element.12.fi_ref) | copy-start | bytes 393220
  31.0 12.9 %copy-start.2 = (bf16[256,256]{1,0:T(8,128)(2,1)S(1)}, bf16[256,256]{1,0:T(8,128)(2,1)}, u32[]{:S(2)}) copy-start(bf16[256,256]{1,0:T(8,128)(2,1)} %get-tuple-element.19.fr_ref) | copy-start | bytes 393220
  31.0 12.9 %copy-start.3 = (f32[2,2]{1,0:T(2,128)S(1)}, f32[2,2]{1,0:T(2,128)}, u32[]{:S(2)}) copy-start(f32[2,2]{1,0:T(2,128)} %bias_ref.1) | copy-start | bytes 52
  43.8 23.3 %copy-start.5 = (bf16[256,256]{1,0:T(8,128)(2,1)S(1)}, bf16[256,256]{1,0:T(8,128)(2,1)}, u32[]{:S(2)}) copy-start(bf16[256,256]{1,0:T(8,128)(2,1)} %param.11) | copy-start | bytes 393220

commit v9 on v7

--- a/solution.py
+++ b/solution.py
@@ -144,6 +144,11 @@
     )(short, spectra, bias, f_re.astype(jnp.bfloat16), f_im.astype(jnp.bfloat16), tw_re, tw_im)
 
 
+def out_kernel(rows_ref, w_ref, out_ref):
+    rows = jnp.transpose(rows_ref[...].astype(jnp.float32)).astype(jnp.bfloat16)
+    out_ref[...] = jnp.dot(rows, w_ref[...], preferred_element_type=jnp.float32).astype(jnp.bfloat16)
+
+
 def local(layer_input, w_in, short_w, filters, filter_bias, w_out):
     width = w_out.shape[0]
     groups = lax.axis_size("seq")
@@ -176,10 +181,10 @@
         tabs,
     ).reshape(per, length)
     returned = lax.all_to_all(state, "seq", split_axis=1, concat_axis=0, tiled=True)
-    output = lax.dot_general(
-        returned, w_out, (((0,), (0,)), ((), ())), preferred_element_type=jnp.float32
-    )
-    return output.astype(jnp.bfloat16)
+    return pl.pallas_call(
+        out_kernel,
+        out_shape=jax.ShapeDtypeStruct((returned.shape[1], w_out.shape[1]), jnp.bfloat16),
+    )(returned, w_out)
 
 
 def solution(mesh):

time: 68.3 us -> 70 us (1.025)
  Pallas kernels: 9.34 us -> 11.2 us
  matrix products: 2.1 us -> 1.21 us
    pallas_call x0 -> x1, Pallas kernels: none -> 1.85 us  [local(): pl.pallas_call(out_kernel, out_shape=jax.ShapeDtypeStruct((returned.shape...]
    dot_general x1 -> x0, matrix products: 0.89 us -> none  [local(): lax.dot_general(returned, w_out, (((0,), (0,)), ((), ())), preferred_elem...]
where the time goes in v9:
time: 70 us; the launch traced here: 69.6 us
  blocking collectives  18.9 us (27%)
  starting transfers between devices  16.8 us (24%)
  Pallas kernels  11.2 us (16%)
  waiting for transfers between devices  10.8 us (15%)
  other arithmetic  6.05 us (9%)
  local copies, waits for them, and re-layouts  4.49 us (6%)
  matrix products  1.21 us (2%)
    all_to_all x1, blocking collectives, local(): lax.all_to_all(state, 'seq', split_axis=1, concat_axis=0, tiled=True)  18.9 us
    all_to_all x1, starting transfers between devices, local(): lax.all_to_all(grouped.reshape(groups, 3 * per, positions), 'seq', split_...  16.8 us
    all_to_all x1, waiting for transfers between devices, local(): lax.all_to_all(grouped.reshape(groups, 3 * per, positions), 'seq', split_...  10.8 us
    pallas_call x1, Pallas kernels, filter_spectra(): pl.pallas_call(filter_kernel, grid=(orders, per), in_specs=[pl.BlockSpec(...  5.08 us
    pallas_call x1, Pallas kernels, chain(): pl.pallas_call(chain_kernel, grid=(per,), in_specs=[pl.BlockSpec((3, 1, h...  4.25 us
    sin x1, other arithmetic, make_tables(): jnp.sin(big)  2.55 us
    pallas_call x1, Pallas kernels, local(): pl.pallas_call(out_kernel, out_shape=jax.ShapeDtypeStruct((returned.shape...  1.85 us
    convert_element_type x1, other arithmetic, chain(): f_im.astype(jnp.bfloat16)  1.63 us
  transfers between devices with their start and end apart: 1, of which 1 were waited for; matrix products, arithmetic and copies ran while one was open for 8% of the time, Pallas kernels for 7%

profile of v9, /device:TPU:1, one launch (start us, length us, event | category | flops | bytes accessed | tf_op | source)
XLA Modules:
  0.0 69.6 jit_solution(18118969892224553927)
XLA Ops:
  0.0 0.0 copy-start
  0.0 1.0 %copy-done = bf16[256,768]{1,0:T(8,128)(2,1)S(1)} copy-done((bf16[256,768]{1,0:T(8,128)(2,1)S(1)}, bf16[256,768]{1,0:T(8,128)(2,1)}, u32[]{:S(2)}) %copy-start) | copy-done | bytes 393240
  1.0 1.2 %convolution_convert_fusion = bf16[768,256]{1,0:T(8,128)(2,1)S(1)} fusion(bf16[256,768]{1,0:T(8,128)(2,1)S(1)} %copy-done, bf16[256,256]{1,0:T(8,128)(2,1)} %param.6), kind=kOutput, calls=%fused_computation | convolution fusion | flops 100859904 | bytes 917504 | tf_op jit(solution)/shard_map/dot_general | solution.py:156
  2.2 0.2 reshape.37
  2.4 1.0 %copy.12 = bf16[128,6,256]{2,1,0:T(8,128)(2,1)} copy(bf16[128,6,256]{2,0,1:T(8,128)(2,1)S(1)} %bitcast.18) | data formatting | bytes 786432 | tf_op jit(solution)/shard_map/reshape | solution.py:164
  3.4 16.8 %all-to-all-start = ((bf16[128,6,256]{2,1,0:T(8,128)(2,1)}), bf16[128,6,256]{2,1,0:T(8,128)(2,1)}, u32[]{:S(2)}, u32[]{:S(2)}) async-start(bf16[128,6,256]{2,1,0:T(8,128)(2,1)} %copy.12), calls=%async_computation | async-start | bytes 1048576 | tf_op jit(solution)/shard_map/all_to_all | solution.py:163
  20.3 0.0 copy-start.4
  20.4 0.0 copy-start.5
  20.4 1.6 %fusion.7 = (bf16[256,256]{1,0:T(8,128)(2,1)}, f32[256,256]{1,0:T(8,128)S(1)}, s32[256,256]{1,0:T(8,128)S(1)}) fusion(s32[256,256]{1,0:T(8,128)S(1)} %iota.10, s32[256,256]{1,0:T(8,128)S(1)} %iota.11), kind=kLoop, calls=%fused_computation.19 | loop fusion | flops 983040 | bytes 1179648 | tf_op jit(solution)/shard_map/convert_element_type | solution.py:144
  22.0 2.5 %fusion.3 = (f32[256,256]{1,0:T(8,128)S(1)}, f32[256,256]{1,0:T(8,128)S(1)}, bf16[256,256]{1,0:T(8,128)(2,1)}, f32[256,256]{1,0:T(8,128)S(1)}) fusion(s32[256,256]{1,0:T(8,128)S(1)} %get-tuple-element.14), kind=kLoop, calls=%fused_computation.12 | loop fusion | flops 1048576 | bytes 1179648 | tf_op jit(solution)/shard_map/sin | solution.py:49
  24.6 0.0 copy-done.4
  24.6 0.5 reshape.40.filt_ref
  25.1 0.0 copy-done.5
  25.1 0.5 reshape.36
  25.7 0.1 mul.46
  25.8 0.1 mul.49
  25.8 0.1 mul.52
  25.9 0.1 maximum_maximum_fusion.rf_ref
  26.1 5.1 %shard_map.64.spec_ref = f32[2,2,256,512]{3,2,1,0:T(8,128)S(1)} custom-call(f32[2,2,128,256]{3,2,1,0:T(8,128)S(1)} %reshape.40.filt_ref, f32[512,128]{1,0:T(8,128)S(1)} %pad_maximum_fusion.lf_ref, f32[512,512]{1,0:T(8,128)S(1)} %maximum_maximum_fusion.rf_ref, f32[256,256]{1,0:T(8,128)S(1)} %get-tuple-element.18.twr_ref, f32[256,256]{1,0:T(8,128)S(1)} %get-tuple-element.17.twi_ref), custom_call_target="tpu_custom_call" | custom-call | tf_op jit(solution)/shard_map/pallas_call | solution.py:71
  31.1 0.0 copy-start.1
  31.2 0.0 copy-start.2
  31.2 0.0 copy-start.3
  31.2 10.8 %all-to-all-done = bf16[128,6,256]{2,1,0:T(8,128)(2,1)} async-done(((bf16[128,6,256]{2,1,0:T(8,128)(2,1)}), bf16[128,6,256]{2,1,0:T(8,128)(2,1)}, u32[]{:S(2)}, u32[]{:S(2)}) %all-to-all-start) | async-done | bytes 393248 | tf_op jit(solution)/shard_map/all_to_all | solution.py:163
  42.0 1.1 %bitcast_convert_fusion = f32[128,1,6,256]{3,2,0,1:T(8,128)S(1)} fusion(bf16[128,6,256]{2,1,0:T(8,128)(2,1)} %all-to-all-done), kind=kLoop, calls=%fused_computation.3 | loop fusion | flops 196608 | bytes 1179648 | tf_op jit(solution)/shard_map/convert_element_type | solution.py:169
  43.1 0.6 add_convert_fusion
  43.7 0.1 copy.14
  43.8 0.0 copy-done.1
  43.8 0.0 copy-done.2
  43.8 0.0 copy-done.3
  43.8 4.2 %shard_map.65 = bf16[2,128,256]{2,1,0:T(8,128)(2,1)S(1)} custom-call(bf16[3,2,128,256]{3,2,1,0:T(8,128)(2,1)S(1)} %bitcast.15, f32[2,2,256,512]{3,2,1,0:T(8,128)S(1)} %shard_map.64.spec_ref, f32[2,2]{1,0:T(2,128)S(1)} %copy-done.3, bf16[256,256]{1,0:T(8,128)(2,1)S(1)} %copy-done.2, bf16[256,256]{1,0:T(8,128)(2,1)S(1)} %copy-done.1, ...), custom_call_target="tpu_custom_call" | custom-call | tf_op jit(solution)/shard_map/pallas_call | solution.py:129
  48.1 0.1 copy.13
  48.2 18.9 %all_to_all.25 = bf16[2,128,256]{2,0,1:T(2,128)(2,1)S(1)} all-to-all(bf16[2,128,256]{2,0,1:T(2,128)(2,1)S(1)} %copy.13), channel_id=1, replica_groups=mesh['win'=2,'seq'=128] {'seq'}, dimensions={1} | all-to-all | bytes 262144 | tf_op jit(solution)/shard_map/all_to_all | solution.py:183
  67.1 0.7 %all_to_all.22.rows_ref = bf16[256,256]{1,0:T(8,128)(2,1)} reshape(bf16[128,2,256]{2,1,0:T(2,128)(2,1)S(1)} %bitcast.19) | data formatting | bytes 262144 | tf_op jit(solution)/shard_map/all_to_all | solution.py:183
  67.8 1.9 %shard_map.66 = bf16[256,256]{1,0:T(8,128)(2,1)} custom-call(bf16[256,256]{1,0:T(8,128)(2,1)} %all_to_all.22.rows_ref, bf16[256,256]{1,0:T(8,128)(2,1)} %w_ref.1), custom_call_target="tpu_custom_call" | custom-call | tf_op jit(solution)/shard_map/pallas_call | solution.py:184
  (8 shorter events, 0.2 us)
Async XLA Ops:
  0.0 1.0 %copy-start = (bf16[256,768]{1,0:T(8,128)(2,1)S(1)}, bf16[256,768]{1,0:T(8,128)(2,1)}, u32[]{:S(2)}) copy-start(bf16[256,768]{1,0:T(8,128)(2,1)} %param.7) | copy-start | bytes 1179652
  3.4 38.5 %all-to-all-start = ((bf16[128,6,256]{2,1,0:T(8,128)(2,1)}), bf16[128,6,256]{2,1,0:T(8,128)(2,1)}, u32[]{:S(2)}, u32[]{:S(2)}) async-start(bf16[128,6,256]{2,1,0:T(8,128)(2,1)} %copy.12), calls=%async_computation | async-start | bytes 1048576 | tf_op jit(solution)/shard_map/all_to_all | solution.py:163
  20.3 4.3 %copy-start.4 = (f32[2,2,32768]{2,1,0:T(2,128)S(1)}, f32[2,2,32768]{2,1,0:T(2,128)}, u32[]{:S(2)}) copy-start(f32[2,2,32768]{2,1,0:T(2,128)} %param.9) | copy-start | bytes 1572868
  20.4 4.7 %copy-start.5 = (f32[3,768]{1,0:T(4,128)S(1)}, f32[3,768]{1,0:T(4,128)}, u32[]{:S(2)}) copy-start(f32[3,768]{1,0:T(4,128)} %param.8) | copy-start | bytes 27652
  31.1 12.7 %copy-start.1 = (bf16[256,256]{1,0:T(8,128)(2,1)S(1)}, bf16[256,256]{1,0:T(8,128)(2,1)}, u32[]{:S(2)}) copy-start(bf16[256,256]{1,0:T(8,128)(2,1)} %get-tuple-element.12.fi_ref) | copy-start | bytes 393220
  31.2 12.7 %copy-start.2 = (bf16[256,256]{1,0:T(8,128)(2,1)S(1)}, bf16[256,256]{1,0:T(8,128)(2,1)}, u32[]{:S(2)}) copy-start(bf16[256,256]{1,0:T(8,128)(2,1)} %get-tuple-element.19.fr_ref) | copy-start | bytes 393220
  31.2 12.7 %copy-start.3 = (f32[2,2]{1,0:T(2,128)S(1)}, f32[2,2]{1,0:T(2,128)}, u32[]{:S(2)}) copy-start(f32[2,2]{1,0:T(2,128)} %bias_ref.1) | copy-start | bytes 52

commit v10 on v7

--- a/solution.py
+++ b/solution.py
@@ -80,7 +80,7 @@
         ],
         out_specs=pl.BlockSpec((1, 1, SIDE, 2 * SIDE), lambda o, c: (o, c, 0, 0)),
         out_shape=jax.ShapeDtypeStruct((orders, per, SIDE, 2 * SIDE), jnp.float32),
-        compiler_params=pltpu.CompilerParams(vmem_limit_bytes=48 * 1024 * 1024),
+        compiler_params=pltpu.CompilerParams(vmem_limit_bytes=16 * 1024 * 1024),
     )(filters, left_fwd, right_fwd, tw_re, tw_im)
 
 
@@ -140,7 +140,7 @@
         ],
         out_specs=pl.BlockSpec((1, half, SIDE), lambda c: (c, 0, 0)),
         out_shape=jax.ShapeDtypeStruct((per, half, SIDE), jnp.bfloat16),
-        compiler_params=pltpu.CompilerParams(vmem_limit_bytes=48 * 1024 * 1024),
+        compiler_params=pltpu.CompilerParams(vmem_limit_bytes=16 * 1024 * 1024),
     )(short, spectra, bias, f_re.astype(jnp.bfloat16), f_im.astype(jnp.bfloat16), tw_re, tw_im)
 
 

time: 68.3 us -> 68.3 us (level)
  no operation moved by 1% of the time
where the time goes in v10:
time: 68.3 us; the launch traced here: 68.1 us
  blocking collectives  18.8 us (28%)
  starting transfers between devices  16.8 us (25%)
  waiting for transfers between devices  10.8 us (16%)
  Pallas kernels  9.34 us (14%)
  other arithmetic  6.04 us (9%)
  local copies, waits for them, and re-layouts  3.84 us (6%)
  matrix products  2.1 us (3%)
    all_to_all x1, blocking collectives, local(): lax.all_to_all(state, 'seq', split_axis=1, concat_axis=0, tiled=True)  18.8 us
    all_to_all x1, starting transfers between devices, local(): lax.all_to_all(grouped.reshape(groups, 3 * per, positions), 'seq', split_...  16.8 us
    all_to_all x1, waiting for transfers between devices, local(): lax.all_to_all(grouped.reshape(groups, 3 * per, positions), 'seq', split_...  10.8 us
    pallas_call x1, Pallas kernels, filter_spectra(): pl.pallas_call(filter_kernel, grid=(orders, per), in_specs=[pl.BlockSpec(...  5.08 us
    pallas_call x1, Pallas kernels, chain(): pl.pallas_call(chain_kernel, grid=(per,), in_specs=[pl.BlockSpec((3, 1, h...  4.26 us
    sin x1, other arithmetic, make_tables(): jnp.sin(big)  2.54 us
    convert_element_type x1, other arithmetic, chain(): f_im.astype(jnp.bfloat16)  1.63 us
  transfers between devices with their start and end apart: 1, of which 1 were waited for; matrix products, arithmetic and copies ran while one was open for 8% of the time, Pallas kernels for 7%

profile of v10, /device:TPU:1, one launch (start us, length us, event | category | flops | bytes accessed | tf_op | source)
XLA Modules:
  0.0 68.1 jit_solution(17899927047272084822)
XLA Ops:
  0.0 0.0 copy-start
  0.0 1.0 %copy-done = bf16[256,768]{1,0:T(8,128)(2,1)S(1)} copy-done((bf16[256,768]{1,0:T(8,128)(2,1)S(1)}, bf16[256,768]{1,0:T(8,128)(2,1)}, u32[]{:S(2)}) %copy-start) | copy-done | bytes 393240
  1.0 1.2 %convolution_convert_fusion = bf16[768,256]{1,0:T(8,128)(2,1)S(1)} fusion(bf16[256,768]{1,0:T(8,128)(2,1)S(1)} %copy-done, bf16[256,256]{1,0:T(8,128)(2,1)} %param.6), kind=kOutput, calls=%fused_computation | convolution fusion | flops 100859904 | bytes 917504 | tf_op jit(solution)/shard_map/dot_general | solution.py:151
  2.2 0.2 reshape.37
  2.4 1.0 %copy.11 = bf16[128,6,256]{2,1,0:T(8,128)(2,1)} copy(bf16[128,6,256]{2,0,1:T(8,128)(2,1)S(1)} %bitcast.20) | data formatting | bytes 786432 | tf_op jit(solution)/shard_map/reshape | solution.py:159
  3.4 16.8 %all-to-all-start = ((bf16[128,6,256]{2,1,0:T(8,128)(2,1)}), bf16[128,6,256]{2,1,0:T(8,128)(2,1)}, u32[]{:S(2)}, u32[]{:S(2)}) async-start(bf16[128,6,256]{2,1,0:T(8,128)(2,1)} %copy.11), calls=%async_computation | async-start | bytes 1048576 | tf_op jit(solution)/shard_map/all_to_all | solution.py:158
  20.3 0.0 copy-start.4
  20.4 0.0 copy-start.6
  20.4 1.6 %fusion.7 = (bf16[256,256]{1,0:T(8,128)(2,1)}, f32[256,256]{1,0:T(8,128)S(1)}, s32[256,256]{1,0:T(8,128)S(1)}) fusion(s32[256,256]{1,0:T(8,128)S(1)} %iota.10, s32[256,256]{1,0:T(8,128)S(1)} %iota.11), kind=kLoop, calls=%fused_computation.20 | loop fusion | flops 983040 | bytes 1179648 | tf_op jit(solution)/shard_map/convert_element_type | solution.py:144
  22.0 2.5 %fusion.3 = (f32[256,256]{1,0:T(8,128)S(1)}, f32[256,256]{1,0:T(8,128)S(1)}, bf16[256,256]{1,0:T(8,128)(2,1)}, f32[256,256]{1,0:T(8,128)S(1)}) fusion(s32[256,256]{1,0:T(8,128)S(1)} %get-tuple-element.14), kind=kLoop, calls=%fused_computation.13 | loop fusion | flops 1048576 | bytes 1179648 | tf_op jit(solution)/shard_map/sin | solution.py:49
  24.6 0.0 copy-done.4
  24.6 0.5 reshape.40.filt_ref
  25.1 0.0 copy-done.6
  25.1 0.5 reshape.36
  25.7 0.1 mul.46
  25.7 0.1 mul.49
  25.8 0.1 mul.52
  25.9 0.1 maximum_maximum_fusion.rf_ref
  26.0 5.1 %shard_map.64.spec_ref = f32[2,2,256,512]{3,2,1,0:T(8,128)S(1)} custom-call(f32[2,2,128,256]{3,2,1,0:T(8,128)S(1)} %reshape.40.filt_ref, f32[512,128]{1,0:T(8,128)S(1)} %pad_maximum_fusion.lf_ref, f32[512,512]{1,0:T(8,128)S(1)} %maximum_maximum_fusion.rf_ref, f32[256,256]{1,0:T(8,128)S(1)} %get-tuple-element.18.twr_ref, f32[256,256]{1,0:T(8,128)S(1)} %get-tuple-element.17.twi_ref), custom_call_target="tpu_custom_call" | custom-call | tf_op jit(solution)/shard_map/pallas_call | solution.py:71
  31.1 0.0 copy-start.1
  31.1 0.0 copy-start.2
  31.2 0.0 copy-start.3
  31.2 10.8 %all-to-all-done = bf16[128,6,256]{2,1,0:T(8,128)(2,1)} async-done(((bf16[128,6,256]{2,1,0:T(8,128)(2,1)}), bf16[128,6,256]{2,1,0:T(8,128)(2,1)}, u32[]{:S(2)}, u32[]{:S(2)}) %all-to-all-start) | async-done | bytes 393248 | tf_op jit(solution)/shard_map/all_to_all | solution.py:158
  42.0 1.1 %bitcast_convert_fusion = f32[128,1,6,256]{3,2,0,1:T(8,128)S(1)} fusion(bf16[128,6,256]{2,1,0:T(8,128)(2,1)} %all-to-all-done), kind=kLoop, calls=%fused_computation.4 | loop fusion | flops 196608 | bytes 1179648 | tf_op jit(solution)/shard_map/convert_element_type | solution.py:164
  43.1 0.6 add_convert_fusion
  43.7 0.1 copy.13
  43.8 0.0 copy-done.1
  43.8 0.0 copy-done.2
  43.8 0.0 copy-done.3
  43.8 0.0 copy-start.5
  43.8 4.3 %shard_map.65 = bf16[2,128,256]{2,1,0:T(8,128)(2,1)S(1)} custom-call(bf16[3,2,128,256]{3,2,1,0:T(8,128)(2,1)S(1)} %bitcast.17, f32[2,2,256,512]{3,2,1,0:T(8,128)S(1)} %shard_map.64.spec_ref, f32[2,2]{1,0:T(2,128)S(1)} %copy-done.3, bf16[256,256]{1,0:T(8,128)(2,1)S(1)} %copy-done.2, bf16[256,256]{1,0:T(8,128)(2,1)S(1)} %copy-done.1, ...), custom_call_target="tpu_custom_call" | custom-call | tf_op jit(solution)/shard_map/pallas_call | solution.py:129
  48.1 0.1 copy.12
  48.2 18.8 %all_to_all.25 = bf16[2,128,256]{2,0,1:T(2,128)(2,1)S(1)} all-to-all(bf16[2,128,256]{2,0,1:T(2,128)(2,1)S(1)} %copy.12), channel_id=1, replica_groups=mesh['win'=2,'seq'=128] {'seq'}, dimensions={1} | all-to-all | bytes 262144 | tf_op jit(solution)/shard_map/all_to_all | solution.py:178
  67.1 0.1 all_to_all.22
  67.2 0.0 copy-done.5
  67.2 0.9 %convolution_convert_fusion.1 = bf16[256,256]{1,0:T(8,128)(2,1)} fusion(bf16[256,256]{1,0:T(8,128)(2,1)S(1)} %all_to_all.22, bf16[256,256]{1,0:T(8,128)(2,1)S(1)} %copy-done.5), kind=kOutput, calls=%fused_computation.1 | convolution fusion | flops 33619968 | bytes 393216 | tf_op jit(solution)/shard_map/dot_general | solution.py:179
  (8 shorter events, 0.2 us)
Async XLA Ops:
  0.0 1.0 %copy-start = (bf16[256,768]{1,0:T(8,128)(2,1)S(1)}, bf16[256,768]{1,0:T(8,128)(2,1)}, u32[]{:S(2)}) copy-start(bf16[256,768]{1,0:T(8,128)(2,1)} %param.7) | copy-start | bytes 1179652
  3.4 38.5 %all-to-all-start = ((bf16[128,6,256]{2,1,0:T(8,128)(2,1)}), bf16[128,6,256]{2,1,0:T(8,128)(2,1)}, u32[]{:S(2)}, u32[]{:S(2)}) async-start(bf16[128,6,256]{2,1,0:T(8,128)(2,1)} %copy.11), calls=%async_computation | async-start | bytes 1048576 | tf_op jit(solution)/shard_map/all_to_all | solution.py:158
  20.3 4.3 %copy-start.4 = (f32[2,2,32768]{2,1,0:T(2,128)S(1)}, f32[2,2,32768]{2,1,0:T(2,128)}, u32[]{:S(2)}) copy-start(f32[2,2,32768]{2,1,0:T(2,128)} %param.9) | copy-start | bytes 1572868
  20.4 4.7 %copy-start.6 = (f32[3,768]{1,0:T(4,128)S(1)}, f32[3,768]{1,0:T(4,128)}, u32[]{:S(2)}) copy-start(f32[3,768]{1,0:T(4,128)} %param.8) | copy-start | bytes 27652
  31.1 12.7 %copy-start.1 = (bf16[256,256]{1,0:T(8,128)(2,1)S(1)}, bf16[256,256]{1,0:T(8,128)(2,1)}, u32[]{:S(2)}) copy-start(bf16[256,256]{1,0:T(8,128)(2,1)} %get-tuple-element.12.fi_ref) | copy-start | bytes 393220
  31.1 12.7 %copy-start.2 = (bf16[256,256]{1,0:T(8,128)(2,1)S(1)}, bf16[256,256]{1,0:T(8,128)(2,1)}, u32[]{:S(2)}) copy-start(bf16[256,256]{1,0:T(8,128)(2,1)} %get-tuple-element.19.fr_ref) | copy-start | bytes 393220
  31.2 12.7 %copy-start.3 = (f32[2,2]{1,0:T(2,128)S(1)}, f32[2,2]{1,0:T(2,128)}, u32[]{:S(2)}) copy-start(f32[2,2]{1,0:T(2,128)} %bias_ref.1) | copy-start | bytes 52
  43.8 23.3 %copy-start.5 = (bf16[256,256]{1,0:T(8,128)(2,1)S(1)}, bf16[256,256]{1,0:T(8,128)(2,1)}, u32[]{:S(2)}) copy-start(bf16[256,256]{1,0:T(8,128)(2,1)} %param.11) | copy-start | bytes 393220

commit v11 on v7

--- a/solution.py
+++ b/solution.py
@@ -19,8 +19,7 @@
     left_hi, left_lo = halves(left)
     right_hi, right_lo = halves(right)
     total = jnp.dot(left_hi, right_hi, preferred_element_type=jnp.float32)
-    total = total + jnp.dot(left_lo, right_hi, preferred_element_type=jnp.float32)
-    return total + jnp.dot(left_hi, right_lo, preferred_element_type=jnp.float32)
+    return total + jnp.dot(left_lo, right_hi, preferred_element_type=jnp.float32)
 
 
 def single(left, right):

time: 68.3 us -> 68.3 us (level)
  Pallas kernels: 9.34 us -> 8 us
  waiting for transfers between devices: 10.8 us -> 12.1 us
    all_to_all x1, waiting for transfers between devices: 10.8 us -> 12.1 us  [local(): lax.all_to_all(grouped.reshape(groups, 3 * per, positions), 'seq', split_...]
    pallas_call x1, Pallas kernels: 5.08 us -> 3.74 us  [filter_spectra(): pl.pallas_call(filter_kernel, grid=(orders, per), in_specs=[pl.BlockSpec(...]
  transfers between devices with their start and end apart: 1 -> 1, of which waited for: 1 -> 1; matrix products, arithmetic and copies ran while one was open for 8% -> 8% of each run, Pallas kernels for 7% -> 5%
where the time goes in v11:
time: 68.3 us; the launch traced here: 68.1 us
  blocking collectives  18.8 us (28%)
  starting transfers between devices  16.8 us (25%)
  waiting for transfers between devices  12.1 us (18%)
  Pallas kernels  8 us (12%)
  other arithmetic  6.04 us (9%)
  local copies, waits for them, and re-layouts  3.84 us (6%)
  matrix products  2.1 us (3%)
    all_to_all x1, blocking collectives, local(): lax.all_to_all(state, 'seq', split_axis=1, concat_axis=0, tiled=True)  18.8 us
    all_to_all x1, starting transfers between devices, local(): lax.all_to_all(grouped.reshape(groups, 3 * per, positions), 'seq', split_...  16.8 us
    all_to_all x1, waiting for transfers between devices, local(): lax.all_to_all(grouped.reshape(groups, 3 * per, positions), 'seq', split_...  12.1 us
    pallas_call x1, Pallas kernels, chain(): pl.pallas_call(chain_kernel, grid=(per,), in_specs=[pl.BlockSpec((3, 1, h...  4.26 us
    pallas_call x1, Pallas kernels, filter_spectra(): pl.pallas_call(filter_kernel, grid=(orders, per), in_specs=[pl.BlockSpec(...  3.74 us
    sin x1, other arithmetic, make_tables(): jnp.sin(big)  2.54 us
    convert_element_type x1, other arithmetic, chain(): f_im.astype(jnp.bfloat16)  1.63 us
  transfers between devices with their start and end apart: 1, of which 1 were waited for; matrix products, arithmetic and copies ran while one was open for 8% of the time, Pallas kernels for 5%

profile of v11, /device:TPU:1, one launch (start us, length us, event | category | flops | bytes accessed | tf_op | source)
XLA Modules:
  0.0 68.1 jit_solution(10030471146405501714)
XLA Ops:
  0.0 0.0 copy-start
  0.0 1.0 %copy-done = bf16[256,768]{1,0:T(8,128)(2,1)S(1)} copy-done((bf16[256,768]{1,0:T(8,128)(2,1)S(1)}, bf16[256,768]{1,0:T(8,128)(2,1)}, u32[]{:S(2)}) %copy-start) | copy-done | bytes 393240
  1.0 1.2 %convolution_convert_fusion = bf16[768,256]{1,0:T(8,128)(2,1)S(1)} fusion(bf16[256,768]{1,0:T(8,128)(2,1)S(1)} %copy-done, bf16[256,256]{1,0:T(8,128)(2,1)} %param.6), kind=kOutput, calls=%fused_computation | convolution fusion | flops 100859904 | bytes 917504 | tf_op jit(solution)/shard_map/dot_general | solution.py:150
  2.2 0.2 reshape.37
  2.4 1.0 %copy.11 = bf16[128,6,256]{2,1,0:T(8,128)(2,1)} copy(bf16[128,6,256]{2,0,1:T(8,128)(2,1)S(1)} %bitcast.20) | data formatting | bytes 786432 | tf_op jit(solution)/shard_map/reshape | solution.py:158
  3.4 16.8 %all-to-all-start = ((bf16[128,6,256]{2,1,0:T(8,128)(2,1)}), bf16[128,6,256]{2,1,0:T(8,128)(2,1)}, u32[]{:S(2)}, u32[]{:S(2)}) async-start(bf16[128,6,256]{2,1,0:T(8,128)(2,1)} %copy.11), calls=%async_computation | async-start | bytes 1048576 | tf_op jit(solution)/shard_map/all_to_all | solution.py:157
  20.3 0.0 copy-start.4
  20.4 0.0 copy-start.6
  20.4 1.6 %fusion.7 = (bf16[256,256]{1,0:T(8,128)(2,1)}, f32[256,256]{1,0:T(8,128)S(1)}, s32[256,256]{1,0:T(8,128)S(1)}) fusion(s32[256,256]{1,0:T(8,128)S(1)} %iota.10, s32[256,256]{1,0:T(8,128)S(1)} %iota.11), kind=kLoop, calls=%fused_computation.20 | loop fusion | flops 983040 | bytes 1179648 | tf_op jit(solution)/shard_map/convert_element_type | solution.py:143
  22.0 2.5 %fusion.3 = (f32[256,256]{1,0:T(8,128)S(1)}, f32[256,256]{1,0:T(8,128)S(1)}, bf16[256,256]{1,0:T(8,128)(2,1)}, f32[256,256]{1,0:T(8,128)S(1)}) fusion(s32[256,256]{1,0:T(8,128)S(1)} %get-tuple-element.14), kind=kLoop, calls=%fused_computation.13 | loop fusion | flops 1048576 | bytes 1179648 | tf_op jit(solution)/shard_map/sin | solution.py:48
  24.6 0.0 copy-done.4
  24.6 0.5 reshape.40.filt_ref
  25.1 0.0 copy-done.6
  25.1 0.5 reshape.36
  25.7 0.1 mul.46
  25.7 0.1 mul.49
  25.8 0.1 mul.52
  25.9 0.1 maximum_maximum_fusion.rf_ref
  26.0 3.7 %shard_map.64.spec_ref = f32[2,2,256,512]{3,2,1,0:T(8,128)S(1)} custom-call(f32[2,2,128,256]{3,2,1,0:T(8,128)S(1)} %reshape.40.filt_ref, f32[512,128]{1,0:T(8,128)S(1)} %pad_maximum_fusion.lf_ref, f32[512,512]{1,0:T(8,128)S(1)} %maximum_maximum_fusion.rf_ref, f32[256,256]{1,0:T(8,128)S(1)} %get-tuple-element.18.twr_ref, f32[256,256]{1,0:T(8,128)S(1)} %get-tuple-element.17.twi_ref), custom_call_target="tpu_custom_call" | custom-call | tf_op jit(solution)/shard_map/pallas_call | solution.py:70
  29.8 0.0 copy-start.1
  29.8 0.0 copy-start.2
  29.8 0.0 copy-start.3
  29.8 12.1 %all-to-all-done = bf16[128,6,256]{2,1,0:T(8,128)(2,1)} async-done(((bf16[128,6,256]{2,1,0:T(8,128)(2,1)}), bf16[128,6,256]{2,1,0:T(8,128)(2,1)}, u32[]{:S(2)}, u32[]{:S(2)}) %all-to-all-start) | async-done | bytes 393248 | tf_op jit(solution)/shard_map/all_to_all | solution.py:157
  42.0 1.1 %bitcast_convert_fusion = f32[128,1,6,256]{3,2,0,1:T(8,128)S(1)} fusion(bf16[128,6,256]{2,1,0:T(8,128)(2,1)} %all-to-all-done), kind=kLoop, calls=%fused_computation.4 | loop fusion | flops 196608 | bytes 1179648 | tf_op jit(solution)/shard_map/convert_element_type | solution.py:163
  43.1 0.6 add_convert_fusion
  43.7 0.1 copy.13
  43.8 0.0 copy-done.1
  43.8 0.0 copy-done.2
  43.8 0.0 copy-done.3
  43.8 0.0 copy-start.5
  43.8 4.3 %shard_map.65 = bf16[2,128,256]{2,1,0:T(8,128)(2,1)S(1)} custom-call(bf16[3,2,128,256]{3,2,1,0:T(8,128)(2,1)S(1)} %bitcast.17, f32[2,2,256,512]{3,2,1,0:T(8,128)S(1)} %shard_map.64.spec_ref, f32[2,2]{1,0:T(2,128)S(1)} %copy-done.3, bf16[256,256]{1,0:T(8,128)(2,1)S(1)} %copy-done.2, bf16[256,256]{1,0:T(8,128)(2,1)S(1)} %copy-done.1, ...), custom_call_target="tpu_custom_call" | custom-call | tf_op jit(solution)/shard_map/pallas_call | solution.py:128
  48.1 0.1 copy.12
  48.2 18.8 %all_to_all.25 = bf16[2,128,256]{2,0,1:T(2,128)(2,1)S(1)} all-to-all(bf16[2,128,256]{2,0,1:T(2,128)(2,1)S(1)} %copy.12), channel_id=1, replica_groups=mesh['win'=2,'seq'=128] {'seq'}, dimensions={1} | all-to-all | bytes 262144 | tf_op jit(solution)/shard_map/all_to_all | solution.py:177
  67.1 0.1 all_to_all.22
  67.2 0.0 copy-done.5
  67.2 0.9 %convolution_convert_fusion.1 = bf16[256,256]{1,0:T(8,128)(2,1)} fusion(bf16[256,256]{1,0:T(8,128)(2,1)S(1)} %all_to_all.22, bf16[256,256]{1,0:T(8,128)(2,1)S(1)} %copy-done.5), kind=kOutput, calls=%fused_computation.1 | convolution fusion | flops 33619968 | bytes 393216 | tf_op jit(solution)/shard_map/dot_general | solution.py:178
  (8 shorter events, 0.2 us)
Async XLA Ops:
  0.0 1.0 %copy-start = (bf16[256,768]{1,0:T(8,128)(2,1)S(1)}, bf16[256,768]{1,0:T(8,128)(2,1)}, u32[]{:S(2)}) copy-start(bf16[256,768]{1,0:T(8,128)(2,1)} %param.7) | copy-start | bytes 1179652
  3.4 38.5 %all-to-all-start = ((bf16[128,6,256]{2,1,0:T(8,128)(2,1)}), bf16[128,6,256]{2,1,0:T(8,128)(2,1)}, u32[]{:S(2)}, u32[]{:S(2)}) async-start(bf16[128,6,256]{2,1,0:T(8,128)(2,1)} %copy.11), calls=%async_computation | async-start | bytes 1048576 | tf_op jit(solution)/shard_map/all_to_all | solution.py:157
  20.3 4.3 %copy-start.4 = (f32[2,2,32768]{2,1,0:T(2,128)S(1)}, f32[2,2,32768]{2,1,0:T(2,128)}, u32[]{:S(2)}) copy-start(f32[2,2,32768]{2,1,0:T(2,128)} %param.9) | copy-start | bytes 1572868
  20.4 4.7 %copy-start.6 = (f32[3,768]{1,0:T(4,128)S(1)}, f32[3,768]{1,0:T(4,128)}, u32[]{:S(2)}) copy-start(f32[3,768]{1,0:T(4,128)} %param.8) | copy-start | bytes 27652
  29.8 14.0 %copy-start.1 = (bf16[256,256]{1,0:T(8,128)(2,1)S(1)}, bf16[256,256]{1,0:T(8,128)(2,1)}, u32[]{:S(2)}) copy-start(bf16[256,256]{1,0:T(8,128)(2,1)} %get-tuple-element.12.fi_ref) | copy-start | bytes 393220
  29.8 14.0 %copy-start.2 = (bf16[256,256]{1,0:T(8,128)(2,1)S(1)}, bf16[256,256]{1,0:T(8,128)(2,1)}, u32[]{:S(2)}) copy-start(bf16[256,256]{1,0:T(8,128)(2,1)} %get-tuple-element.19.fr_ref) | copy-start | bytes 393220
  29.8 14.0 %copy-start.3 = (f32[2,2]{1,0:T(2,128)S(1)}, f32[2,2]{1,0:T(2,128)}, u32[]{:S(2)}) copy-start(f32[2,2]{1,0:T(2,128)} %bias_ref.1) | copy-start | bytes 52
  43.8 23.3 %copy-start.5 = (bf16[256,256]{1,0:T(8,128)(2,1)S(1)}, bf16[256,256]{1,0:T(8,128)(2,1)}, u32[]{:S(2)}) copy-start(bf16[256,256]{1,0:T(8,128)(2,1)} %param.11) | copy-start | bytes 393220
